TPU v7x, 512 devices: a whole 4x8x8 slice. The times are simulated.
512 devices in a mesh: dp: 32 (over y, z_lo), ctx: 16 (over z_hi, x, core).
Axes of the slice: x: 4, y: 8, z: 8 (z_hi: 2, z_lo: 4; z = z_hi * 4 + z_lo), core: 2. Of those that a mesh axis runs over, the one named last changes fastest.
Arguments:
- projected: bfloat16 [2, 32, 2048, 4096], P(None, 'dp', 'ctx'), may hold values from -6 to 6
- token_ids: int32 [32, 2048], P('dp', 'ctx'), may hold values from 0 to 511
- short_filters: float32 [2, 7, 4096], P(None, None, 'ctx'), may hold values from -2 to 2
- medium_filter: bfloat16 [128, 4096], P(None, 'ctx'), may hold values from -0.75 to 0.75
- skip_gain: float32 [4096], P('ctx'), may hold values from -3 to 3
Outputs:
- grad_projected: bfloat16 [2, 32, 2048, 4096], P(None, 'dp', 'ctx')
- grad_short: float32 [2, 7, 4096], P(None, None, 'ctx')
- grad_medium: float32 [128, 4096], P(None, 'ctx')
- grad_skip: float32 [4096], P('ctx')
All inputs are finite; a program needn't handle non-finite values.
Results may differ from a plain program's by a relative error of at most 0.024.
Values may be sent and summed in bfloat16 or wider, within the bound.
No kernel may reach another device: no remote copies, remote signals or barrier semaphores. Data moves between devices by JAX's collectives and lax.ppermute only.
A program may use at most 128 MiB of HBM per device.

v0:
```python
import jax
import jax.numpy as jnp
from jax import lax
from jax.sharding import PartitionSpec as P


def short_forward(extended, filters):
    short_len = filters.shape[1]
    length = extended.shape[1] - short_len + 1
    result = jnp.zeros((extended.shape[0], length, extended.shape[2]), jnp.float32)
    for offset in range(short_len):
        start = short_len - 1 - offset
        result = result + filters[:, offset][:, None, :] * extended[
            :, start : start + length
        ].astype(jnp.float32)
    return result


def short_backward(extended, filters):
    short_len = filters.shape[1]
    length = extended.shape[1] - short_len + 1
    result = jnp.zeros((extended.shape[0], length, extended.shape[2]), jnp.float32)
    for offset in range(short_len):
        result = result + filters[:, offset][:, None, :] * extended[
            :, offset : offset + length
        ].astype(jnp.float32)
    return result


def short_weights(grads, extended):
    short_len = extended.shape[1] - grads.shape[1] + 1
    length = grads.shape[1]
    rows = []
    for offset in range(short_len):
        start = short_len - 1 - offset
        rows.append(
            jnp.sum(
                grads.astype(jnp.float32) * extended[:, start : start + length].astype(jnp.float32),
                axis=1,
            )
        )
    return jnp.stack(rows, axis=1)


def depthwise(extended, kernel):
    result = lax.conv_general_dilated(
        extended[None],
        kernel[:, None, :],
        (1,),
        "VALID",
        dimension_numbers=("NWC", "WIO", "NWC"),
        feature_group_count=extended.shape[1],
        preferred_element_type=jnp.float32,
    )
    return result[0]


def local(projected, token_ids, short_filters, medium_filter, skip_gain):
    inputs = projected[:, 0]
    short_len = short_filters.shape[1]
    filter_len = medium_filter.shape[0]
    length = inputs.shape[1]
    groups = lax.axis_size("dp")
    shards = lax.axis_size("ctx")
    loss_weight = jnp.where((token_ids[0] >= 97) & (token_ids[0] <= 122), 0.1, 1.0).astype(
        jnp.bfloat16
    )
    weight_rows = jnp.broadcast_to(loss_weight[None, :, None], (1, length, shards))
    all_inputs, all_weight = (
        lax.all_to_all(inputs, "ctx", split_axis=2, concat_axis=1, tiled=True),
        lax.all_to_all(weight_rows, "ctx", split_axis=2, concat_axis=1, tiled=True),
    )
    weight_seq = all_weight[0, :, 0].astype(jnp.float32)
    padded_inputs = jnp.pad(all_inputs, ((0, 0), (short_len - 1, 0), (0, 0)))
    filtered = short_forward(padded_inputs, short_filters)
    product = (filtered[0] * filtered[1]).astype(jnp.bfloat16)
    padded_product = jnp.pad(product, ((filter_len - 1, 0), (0, 0)))
    mix = depthwise(padded_product, medium_filter[::-1]) + skip_gain * product.astype(jnp.float32)
    grad_mix = (weight_seq[:, None] * mix).astype(jnp.bfloat16)
    padded_later = jnp.pad(grad_mix, ((0, filter_len - 1), (0, 0)))
    back_product = depthwise(padded_later, medium_filter) + skip_gain * grad_mix.astype(jnp.float32)
    grad_key = (back_product * filtered[1]).astype(jnp.bfloat16)
    grad_value = (back_product * filtered[0]).astype(jnp.bfloat16)
    grad_filtered = jnp.stack([grad_key, grad_value])
    padded_grads = jnp.pad(grad_filtered, ((0, 0), (0, short_len - 1), (0, 0)))
    grad_channels = short_backward(padded_grads, short_filters).astype(jnp.bfloat16)
    grad_inputs = lax.all_to_all(grad_channels, "ctx", split_axis=1, concat_axis=2, tiled=True)
    grad_taps = depthwise(padded_product, grad_mix)[::-1]
    grad_gain = jnp.sum(grad_mix.astype(jnp.float32) * product.astype(jnp.float32), axis=0)
    grad_short = short_weights(grad_filtered, padded_inputs)
    grad_taps, grad_gain, grad_short = (
        lax.psum(grad_taps.astype(jnp.bfloat16), "dp").astype(jnp.float32),
        lax.psum(grad_gain.astype(jnp.bfloat16), "dp").astype(jnp.float32),
        lax.psum(grad_short.astype(jnp.bfloat16), "dp").astype(jnp.float32),
    )
    return (grad_inputs[:, None], grad_short / groups, grad_taps / groups, grad_gain / groups)


def solution(mesh):
    placed = (
        P(None, "dp", "ctx", None),
        P("dp", "ctx"),
        P(None, None, "ctx"),
        P(None, "ctx"),
        P("ctx"),
    )
    return jax.shard_map(
        local,
        mesh=mesh,
        in_specs=placed,
        out_specs=(P(None, "dp", "ctx", None), P(None, None, "ctx"), P(None, "ctx"), P("ctx")),
        check_vma=False,
    )
```

profile of v0, /device:TPU:6, one launch (start us, length us, event | category | flops | bytes accessed | tf_op | source)
XLA Modules:
  0.0 554.1 jit_solution(2337777558290786517)
XLA Ops:
  7.2 0.7 fusion.60
  7.8 0.6 broadcast_in_dim.36
  8.4 13.2 %all-to-all-start = ((bf16[1,128,16]{1,0,2:T(2,128)(2,1)}), bf16[1,128,16]{1,0,2:T(2,128)(2,1)S(1)}, u32[]{:S(2)}, u32[]{:S(2)}) async-start(bf16[1,128,16]{1,0,2:T(2,128)(2,1)} %broadcast_in_dim.36), calls=%async_computation | async-start | bytes 16384 | tf_op jit(solution)/shard_map/all_to_all | solution.py:71
  21.7 6.2 %copy.27 = bf16[2,1,128,4096]{2,0,3,1:T(2,128)(2,1)} copy(bf16[2,1,128,4096]{3,2,1,0:T(8,128)(2,1)} %param.5) | data formatting | bytes 4194304 | tf_op args[0]
  27.8 1.8 all-to-all-done
  29.6 8.0 %all-to-all-start.1 = ((bf16[2,128,4096]{1,0,2:T(2,128)(2,1)}), bf16[2,128,4096]{1,0,2:T(2,128)(2,1)S(1)}, u32[]{:S(2)}, u32[]{:S(2)}) async-start(bf16[2,128,4096]{1,0,2:T(2,128)(2,1)} %bitcast.5), calls=%async_computation.1 | async-start | bytes 4194304 | tf_op jit(solution)/shard_map/all_to_all | solution.py:70
  37.8 31.3 %all-to-all-done.1 = bf16[2,128,4096]{1,0,2:T(2,128)(2,1)S(1)} async-done(((bf16[2,128,4096]{1,0,2:T(2,128)(2,1)}), bf16[2,128,4096]{1,0,2:T(2,128)(2,1)S(1)}, u32[]{:S(2)}, u32[]{:S(2)}) %all-to-all-start.1) | async-done | bytes 2097184 | tf_op jit(solution)/shard_map/all_to_all | solution.py:70
  69.1 1.3 copy-done.2
  70.4 4.7 copy.28
  75.2 3.7 fusion.5
  79.8 0.5 copy-done.3
  81.1 47.9 %fusion.52 = f32[8,272,256]{2,0,1:T(8,128)S(1)} fusion(pred[8,272]{0,1:T(8,128)(4,1)S(1)} %copy-done.7, bf16[128,1,256]{2,0,1:T(8,128)(2,1)S(1)} %bitcast.113, bf16[8,399,256]{2,0,1:T(8,128)(2,1)S(1)} %fusion.75), kind=kOutput, calls=%fused_computation.76 | convolution fusion | flops 143163392 | bytes 3930240 | tf_op jit(solution)/shard_map/conv_general_dilated | solution.py:46
  129.1 0.7 copy.32
  129.8 1.3 fusion.33
  132.5 48.0 %fusion.49 = f32[8,272,256]{2,0,1:T(8,128)S(1)} fusion(pred[8,272]{0,1:T(8,128)(4,1)S(1)} %copy-done.7, bf16[128,1,256]{2,0,1:T(8,128)(2,1)S(1)} %bitcast.112, bf16[8,399,256]{2,0,1:T(8,128)(2,1)S(1)} %fusion.73), kind=kOutput, calls=%fused_computation.75 | convolution fusion | flops 143163392 | bytes 3930240 | tf_op jit(solution)/shard_map/conv_general_dilated | solution.py:46
  180.4 0.7 copy.36
  181.2 0.8 multiply_convert_fusion.1
  182.6 0.8 copy-done
  183.3 3.7 fusion.12
  187.0 14.2 %copy.37 = bf16[2,2048,256]{2,0,1:T(2,128)(2,1)} copy(bf16[2,2048,256]{2,1,0:T(8,128)(2,1)S(1)} %fusion.12) | data formatting | bytes 4194304 | tf_op jit(solution)/shard_map/convert_element_type | solution.py:86
  201.2 23.9 %all-to-all-start.2 = ((bf16[2,2048,256]{2,0,1:T(2,128)(2,1)}), bf16[2,2048,256]{2,0,1:T(2,128)(2,1)}, u32[]{:S(2)}, u32[]{:S(2)}) async-start(bf16[2,2048,256]{2,0,1:T(2,128)(2,1)} %copy.37), calls=%async_computation.2 | async-start | bytes 4194304 | tf_op jit(solution)/shard_map/all_to_all | solution.py:87
  225.2 28.2 %fusion.21 = bf16[1,128,256]{2,0,1:T(2,128)(2,1)S(1)} fusion(bf16[1,2175,256]{2,1,0:T(8,128)(2,1)} %copy-done.3, bf16[2048,1,256]{2,0,1:T(8,128)(2,1)} %fusion.33), kind=kOutput, calls=%fused_computation.40 | convolution fusion | flops 134217728 | bytes 2227712 | tf_op jit(solution)/shard_map/conv_general_dilated | solution.py:46
  253.5 0.7 rev.7
  254.2 1.9 multiply_reduce_fusion
  256.1 3.6 fusion.18
  259.8 88.7 %all-reduce.4 = (bf16[2,7,256]{2,0,1:T(2,128)(2,1)S(1)}, bf16[256]{0:T(256)(128)(2,1)S(1)}) all-reduce(bf16[2,7,256]{2,0,1:T(2,128)(2,1)S(1)} %constant_dynamic-update-slice_fusion, bf16[256]{0:T(256)(128)(2,1)S(1)} %get-tuple-element.12), channel_id=1, replica_groups=mesh['dp'=32,'ctx'=16] {'dp'}, use_global_device_ids=true, to_apply=%region_7.8 | all-reduce | flops 3840 | bytes 15360 | tf_op jit(solution)/shard_map/psum | solution.py:94
  348.5 0.6 convert_multiply_fusion.17
  349.1 0.6 convert_multiply_fusion.18
  349.7 191.0 %all-reduce.7.cloned.1.call-done = bf16[128,256]{1,0:T(8,128)(2,1)} async-done(((bf16[128,256]{1,0:T(8,128)(2,1)}), bf16[128,256]{1,0:T(8,128)(2,1)}) %all-reduce.7.cloned.1.call-update) | async-done | bytes 65552 | tf_op jit(solution)/shard_map/psum | solution.py:92
  540.6 1.5 convert_multiply_fusion.16
  542.1 2.8 copy.38
  544.9 2.3 broadcast_in_dim.41
  (41 shorter events, 3.9 us)
Async XLA Ops:
  8.4 21.2 %all-to-all-start = ((bf16[1,128,16]{1,0,2:T(2,128)(2,1)}), bf16[1,128,16]{1,0,2:T(2,128)(2,1)S(1)}, u32[]{:S(2)}, u32[]{:S(2)}) async-start(bf16[1,128,16]{1,0,2:T(2,128)(2,1)} %broadcast_in_dim.36), calls=%async_computation | async-start | bytes 16384 | tf_op jit(solution)/shard_map/all_to_all | solution.py:71
  29.6 8.0 %copy-start.4 = (bf16[128,256]{1,0:T(8,128)(2,1)S(1)}, bf16[128,256]{1,0:T(8,128)(2,1)}, u32[]{:S(2)}) copy-start(bf16[128,256]{1,0:T(8,128)(2,1)} %param.8) | copy-start | bytes 196612
  29.6 8.1 %copy-start.6 = (f32[2,7,256]{2,0,1:T(2,128)S(1)}, f32[2,7,256]{2,0,1:T(2,128)}, u32[]{:S(2)}) copy-start(f32[2,7,256]{2,0,1:T(2,128)} %param.7) | copy-start | bytes 43012
  29.6 39.5 %all-to-all-start.1 = ((bf16[2,128,4096]{1,0,2:T(2,128)(2,1)}), bf16[2,128,4096]{1,0,2:T(2,128)(2,1)S(1)}, u32[]{:S(2)}, u32[]{:S(2)}) async-start(bf16[2,128,4096]{1,0,2:T(2,128)(2,1)} %bitcast.5), calls=%async_computation.1 | async-start | bytes 4194304 | tf_op jit(solution)/shard_map/all_to_all | solution.py:70
  69.1 1.3 copy-start.2
  79.4 1.0 copy-start.3
  80.4 0.8 copy-start.7
  129.0 0.7 copy-start.5
  182.3 1.0 copy-start
  201.2 340.9 %all-to-all-start.2 = ((bf16[2,2048,256]{2,0,1:T(2,128)(2,1)}), bf16[2,2048,256]{2,0,1:T(2,128)(2,1)}, u32[]{:S(2)}, u32[]{:S(2)}) async-start(bf16[2,2048,256]{2,0,1:T(2,128)(2,1)} %copy.37), calls=%async_computation.2 | async-start | bytes 4194304 | tf_op jit(solution)/shard_map/all_to_all | solution.py:87
  225.1 315.5 %all-reduce.7.cloned.1.call-start = ((), (), s32[]{:S(2)}) async-start(), calls=%async_computation.3 | async-start | bytes 131072 | tf_op jit(solution)/shard_map/psum | solution.py:92
  254.2 1.9 copy-start.1
Sparse Core Ops, SparseCore 0:
  254.3 286.2 all-reduce.6
where the time goes:
time: 555 us; the launch traced here: 554 us
  waiting for transfers between devices  224 us (40%)
  matrix products  124 us (22%)
  blocking collectives  88.7 us (16%)
  starting transfers between devices  45.2 us (8%)
  local copies, waits for them, and re-layouts  37.7 us (7%)
  other arithmetic  20 us (4%)
  between operations  14.3 us (3%)
    psum x1, waiting for transfers between devices, local(): lax.psum(grad_taps.astype(jnp.bfloat16), 'dp').astype(jnp.float32)  191 us
    conv_general_dilated x3, matrix products, depthwise(): lax.conv_general_dilated(extended[None], kernel[:, None, :], (1,), 'VALID...  124 us
    psum x1, blocking collectives, local(): lax.psum(grad_short.astype(jnp.bfloat16), 'dp').astype(jnp.float32)  88.7 us
    all_to_all x1, waiting for transfers between devices, local(): lax.all_to_all(inputs, 'ctx', split_axis=2, concat_axis=1, tiled=True)  31.3 us
    all_to_all x1, starting transfers between devices, local(): lax.all_to_all(grad_channels, 'ctx', split_axis=1, concat_axis=2, tiled=T...  23.9 us
    convert_element_type x1, local copies, waits for them, and re-layouts, local(): short_backward(padded_grads, short_filters).astype(jnp.bfloat16)  14.2 us
    all_to_all x1, starting transfers between devices, local(): lax.all_to_all(weight_rows, 'ctx', split_axis=2, concat_axis=1, tiled=True)  13.2 us
  transfers between devices with their start and end apart: 4, of which 3 were waited for; matrix products, arithmetic and copies ran while one was open for 8% of the time, Pallas kernels for 0%

commit v1 on v0

--- a/solution.py
+++ b/solution.py
@@ -55,6 +55,15 @@
     return result[0]
 
 
+def butterfly_sum(value, axis, size):
+    bit = 1
+    while bit < size:
+        perm = [(i, i ^ bit) for i in range(size)]
+        value = value + lax.ppermute(value, axis, perm)
+        bit *= 2
+    return value
+
+
 def local(projected, token_ids, short_filters, medium_filter, skip_gain):
     inputs = projected[:, 0]
     short_len = short_filters.shape[1]
@@ -88,11 +97,14 @@
     grad_taps = depthwise(padded_product, grad_mix)[::-1]
     grad_gain = jnp.sum(grad_mix.astype(jnp.float32) * product.astype(jnp.float32), axis=0)
     grad_short = short_weights(grad_filtered, padded_inputs)
-    grad_taps, grad_gain, grad_short = (
-        lax.psum(grad_taps.astype(jnp.bfloat16), "dp").astype(jnp.float32),
-        lax.psum(grad_gain.astype(jnp.bfloat16), "dp").astype(jnp.float32),
-        lax.psum(grad_short.astype(jnp.bfloat16), "dp").astype(jnp.float32),
-    )
+    taps = grad_taps.shape[0]
+    stacked = jnp.concatenate(
+        [grad_taps, grad_short.reshape(-1, grad_short.shape[-1]), grad_gain[None]], axis=0
+    ).astype(jnp.float32)
+    stacked = butterfly_sum(stacked, "dp", groups)
+    grad_taps = stacked[:taps]
+    grad_short = stacked[taps : taps + grad_short.shape[0] * short_len].reshape(grad_short.shape)
+    grad_gain = stacked[-1]
     return (grad_inputs[:, None], grad_short / groups, grad_taps / groups, grad_gain / groups)
 
 

time: 555 us -> 328 us (0.59)
  waiting for transfers between devices: 224 us -> 70.2 us
  blocking collectives: 88.7 us -> 0 us
  starting transfers between devices: 45.2 us -> 74.5 us
  between operations: 14.3 us -> 1.02 us
    psum x1 -> x0, waiting for transfers between devices: 191 us -> none  [local(): lax.psum(grad_taps.astype(jnp.bfloat16), 'dp').astype(jnp.float32)]
    psum x1 -> x0, blocking collectives: 88.7 us -> none  [local(): lax.psum(grad_short.astype(jnp.bfloat16), 'dp').astype(jnp.float32)]
    ppermute x0 -> x5, waiting for transfers between devices: none -> 37.1 us  [butterfly_sum(): value = value + lax.ppermute(value, axis, perm)]
    ppermute x0 -> x5, starting transfers between devices: none -> 29.3 us  [butterfly_sum(): value = value + lax.ppermute(value, axis, perm)]
  transfers between devices with their start and end apart: 4 -> 8, of which waited for: 3 -> 7; matrix products, arithmetic and copies ran while one was open for 8% -> 13% of each run, Pallas kernels for 0% -> 0%
where the time goes in v1:
time: 328 us; the launch traced here: 326 us
  matrix products  124 us (38%)
  starting transfers between devices  74.5 us (23%)
  waiting for transfers between devices  70.2 us (21%)
  local copies, waits for them, and re-layouts  38 us (12%)
  other arithmetic  18.6 us (6%)
    conv_general_dilated x3, matrix products, depthwise(): lax.conv_general_dilated(extended[None], kernel[:, None, :], (1,), 'VALID...  124 us
    ppermute x5, waiting for transfers between devices, butterfly_sum(): value = value + lax.ppermute(value, axis, perm)  37.1 us
    all_to_all x1, waiting for transfers between devices, local(): lax.all_to_all(inputs, 'ctx', split_axis=2, concat_axis=1, tiled=True)  31.3 us
    ppermute x5, starting transfers between devices, butterfly_sum(): value = value + lax.ppermute(value, axis, perm)  29.3 us
    all_to_all x1, starting transfers between devices, local(): lax.all_to_all(grad_channels, 'ctx', split_axis=1, concat_axis=2, tiled=T...  23.9 us
    convert_element_type x1, local copies, waits for them, and re-layouts, local(): short_backward(padded_grads, short_filters).astype(jnp.bfloat16)  14.2 us
    all_to_all x1, starting transfers between devices, local(): lax.all_to_all(weight_rows, 'ctx', split_axis=2, concat_axis=1, tiled=True)  13.2 us
    unnamed x19, local copies, waits for them, and re-layouts  9.91 us
  transfers between devices with their start and end apart: 8, of which 7 were waited for; matrix products, arithmetic and copies ran while one was open for 13% of the time, Pallas kernels for 0%

profile of v1, /device:TPU:6, one launch (start us, length us, event | category | flops | bytes accessed | tf_op | source)
XLA Modules:
  0.0 326.4 jit_solution(17930976652553337548)
XLA Ops:
  1.9 13.2 %all-to-all-start = ((bf16[1,128,16]{1,0,2:T(2,128)(2,1)}), bf16[1,128,16]{1,0,2:T(2,128)(2,1)S(1)}, u32[]{:S(2)}, u32[]{:S(2)}) async-start(bf16[1,128,16]{1,0,2:T(2,128)(2,1)} %broadcast_in_dim.39), calls=%async_computation | async-start | bytes 16384 | tf_op jit(solution)/shard_map/all_to_all | solution.py:80
  15.1 6.2 %copy.29 = bf16[2,1,128,4096]{2,0,3,1:T(2,128)(2,1)} copy(bf16[2,1,128,4096]{3,2,1,0:T(8,128)(2,1)} %param.5) | data formatting | bytes 4194304 | tf_op args[0]
  21.3 1.8 all-to-all-done
  23.1 8.0 %all-to-all-start.1 = ((bf16[2,128,4096]{1,0,2:T(2,128)(2,1)}), bf16[2,128,4096]{1,0,2:T(2,128)(2,1)S(1)}, u32[]{:S(2)}, u32[]{:S(2)}) async-start(bf16[2,128,4096]{1,0,2:T(2,128)(2,1)} %bitcast.5), calls=%async_computation.1 | async-start | bytes 4194304 | tf_op jit(solution)/shard_map/all_to_all | solution.py:79
  31.2 31.3 %all-to-all-done.1 = bf16[2,128,4096]{1,0,2:T(2,128)(2,1)S(1)} async-done(((bf16[2,128,4096]{1,0,2:T(2,128)(2,1)}), bf16[2,128,4096]{1,0,2:T(2,128)(2,1)S(1)}, u32[]{:S(2)}, u32[]{:S(2)}) %all-to-all-start.1) | async-done | bytes 2097184 | tf_op jit(solution)/shard_map/all_to_all | solution.py:79
  62.6 1.3 copy-done.2
  63.9 4.7 %copy.30 = bf16[2,128,16,256]{3,1,2,0:T(8,128)(2,1)S(1)} copy(bf16[2,128,16,256]{1,0,3,2:T(2,128)(2,1)} %bitcast.96) | data formatting | bytes 4194304 | tf_op jit(solution)/shard_map/all_to_all | solution.py:79
  68.6 3.7 %fusion.5 = f32[2,2048,256]{2,1,0:T(8,128)S(1)} fusion(bf16[2,2048,256]{2,1,0:T(8,128)(2,1)S(1)} %bitcast.87, f32[2,256]{1,0:T(2,128)S(1)} %get-tuple-element.31, f32[2,256]{1,0:T(2,128)S(1)} %get-tuple-element.32, f32[2,256]{1,0:T(2,128)S(1)} %get-tuple-element.27, f32[2,256]{1,0:T(2,128)S(1)} %get-tuple-element.28, f32[2,256]{1,0:T(2,128)S(1)} %get-tuple-element.29, ...), kind=kLoop, calls=%fused_computation.18 | loop fusion | flops 20971520 | bytes 6305792 | tf_op jit(solution)/shard_map/add | solution.py:13
  74.6 47.9 %fusion.52 = f32[8,272,256]{2,0,1:T(8,128)S(1)} fusion(pred[8,272]{0,1:T(8,128)(4,1)S(1)} %copy-done.7, bf16[128,1,256]{2,0,1:T(8,128)(2,1)S(1)} %bitcast.101, bf16[8,399,256]{2,0,1:T(8,128)(2,1)S(1)} %fusion.76), kind=kOutput, calls=%fused_computation.76 | convolution fusion | flops 143163392 | bytes 3930240 | tf_op jit(solution)/shard_map/conv_general_dilated | solution.py:46
  122.5 0.7 copy.34
  123.3 1.3 fusion.33
  125.9 48.0 %fusion.49 = f32[8,272,256]{2,0,1:T(8,128)S(1)} fusion(pred[8,272]{0,1:T(8,128)(4,1)S(1)} %copy-done.7, bf16[128,1,256]{2,0,1:T(8,128)(2,1)S(1)} %bitcast.100, bf16[8,399,256]{2,0,1:T(8,128)(2,1)S(1)} %fusion.74), kind=kOutput, calls=%fused_computation.75 | convolution fusion | flops 143163392 | bytes 3930240 | tf_op jit(solution)/shard_map/conv_general_dilated | solution.py:46
  174.6 0.8 multiply_convert_fusion.1
  176.0 0.8 copy-done
  176.8 3.7 %fusion.12 = bf16[2,2048,256]{2,1,0:T(8,128)(2,1)S(1)} fusion(bf16[2,2048,256]{2,1,0:T(8,128)(2,1)S(1)} %pad_maximum_fusion, f32[2,256]{1,0:T(2,128)S(1)} %get-tuple-element.31, f32[2,256]{1,0:T(2,128)S(1)} %get-tuple-element.32, f32[2,256]{1,0:T(2,128)S(1)} %get-tuple-element.27, f32[2,256]{1,0:T(2,128)S(1)} %get-tuple-element.28, ...), kind=kLoop, calls=%fused_computation.25 | loop fusion | flops 22020096 | bytes 4208640 | tf_op jit(solution)/shard_map/convert_element_type | solution.py:95
  180.5 14.2 %copy.39 = bf16[2,2048,256]{2,0,1:T(2,128)(2,1)} copy(bf16[2,2048,256]{2,1,0:T(8,128)(2,1)S(1)} %fusion.12) | data formatting | bytes 4194304 | tf_op jit(solution)/shard_map/convert_element_type | solution.py:95
  194.7 23.9 %all-to-all-start.2 = ((bf16[2,2048,256]{2,0,1:T(2,128)(2,1)}), bf16[2,2048,256]{2,0,1:T(2,128)(2,1)}, u32[]{:S(2)}, u32[]{:S(2)}) async-start(bf16[2,2048,256]{2,0,1:T(2,128)(2,1)} %copy.39), calls=%async_computation.2 | async-start | bytes 4194304 | tf_op jit(solution)/shard_map/all_to_all | solution.py:96
  218.6 28.2 %fusion.21 = f32[1,128,256]{2,0,1:T(1,128)S(1)} fusion(bf16[1,2175,256]{2,1,0:T(8,128)(2,1)} %copy-done.3, bf16[2048,1,256]{2,0,1:T(8,128)(2,1)} %fusion.33), kind=kOutput, calls=%fused_computation.40 | convolution fusion | flops 134217728 | bytes 2293248 | tf_op jit(solution)/shard_map/conv_general_dilated | solution.py:46
  247.2 1.9 multiply_reduce_fusion
  249.1 3.6 %fusion.18 = (f32[2,256]{1,0:T(2,128)S(1)}, f32[2,256]{1,0:T(2,128)S(1)}, f32[2,256]{1,0:T(2,128)S(1)}, f32[2,256]{1,0:T(2,128)S(1)}, f32[2,256]{1,0:T(2,128)S(1)}, /*index=5*/f32[2,256]{1,0:T(2,128)S(1)}) fusion(bf16[2,2048,256]{2,1,0:T(8,128)(2,1)S(1)} %bitcast.88, bf16[1,2048,256]{2,1,0:T(8,128)(2,1)S(1)} %copy-done.1, ...), kind=kLoop, calls=%fused_computation.31 | loop fusion | flops 23065600 | bytes 4206592 | tf_op jit(solution)/shard_map/reduce_sum | solution.py:37
  252.9 6.3 %collective-permute-start = (f32[143,256]{1,0:T(8,128)S(1)}, f32[143,256]{1,0:T(8,128)S(1)}, u32[]{:S(2)}, u32[]{:S(2)}) collective-permute-start(f32[143,256]{1,0:T(8,128)S(1)} %pad_maximum_fusion.1), channel_id=1, source_target_pairs={{0,16},{16,0},{32,48},{48,32},{64,80},{80,64},{96,112},{112,96},{1... | collective-permute-start | bytes 439304 | tf_op jit(solution)/shard_map/ppermute | solution.py:62
  259.2 13.2 %collective-permute-done = f32[143,256]{1,0:T(8,128)S(1)} collective-permute-done((f32[143,256]{1,0:T(8,128)S(1)}, f32[143,256]{1,0:T(8,128)S(1)}, u32[]{:S(2)}, u32[]{:S(2)}) %collective-permute-start) | collective-permute-done | bytes 146464 | tf_op jit(solution)/shard_map/ppermute | solution.py:62
  272.4 7.3 %collective-permute-start.1 = (f32[143,256]{1,0:T(8,128)S(1)}, f32[143,256]{1,0:T(8,128)S(1)}, u32[]{:S(2)}, u32[]{:S(2)}) collective-permute-start(f32[143,256]{1,0:T(8,128)S(1)} %fusion.69), channel_id=1, source_target_pairs={{0,32},{16,48},{32,0},{48,16},{64,96},{80,112},{96,64},{112,80},{1... | collective-permute-start | bytes 439304 | tf_op jit(solution)/shard_map/ppermute | solution.py:62
  279.7 6.4 %collective-permute-done.1 = f32[143,256]{1,0:T(8,128)S(1)} collective-permute-done((f32[143,256]{1,0:T(8,128)S(1)}, f32[143,256]{1,0:T(8,128)S(1)}, u32[]{:S(2)}, u32[]{:S(2)}) %collective-permute-start.1) | collective-permute-done | bytes 146464 | tf_op jit(solution)/shard_map/ppermute | solution.py:62
  286.1 3.5 %collective-permute-start.2 = (f32[143,256]{1,0:T(8,128)S(1)}, f32[143,256]{1,0:T(8,128)S(1)}, u32[]{:S(2)}, u32[]{:S(2)}) collective-permute-start(f32[143,256]{1,0:T(8,128)S(1)} %add.97), channel_id=1, source_target_pairs={{0,64},{16,80},{32,96},{48,112},{64,0},{80,16},{96,32},{112,48},{1... | collective-permute-start | bytes 439304 | tf_op jit(solution)/shard_map/ppermute | solution.py:62
  289.6 4.2 %collective-permute-done.2 = f32[143,256]{1,0:T(8,128)S(1)} collective-permute-done((f32[143,256]{1,0:T(8,128)S(1)}, f32[143,256]{1,0:T(8,128)S(1)}, u32[]{:S(2)}, u32[]{:S(2)}) %collective-permute-start.2) | collective-permute-done | bytes 146464 | tf_op jit(solution)/shard_map/ppermute | solution.py:62
  293.9 4.5 %collective-permute-start.3 = (f32[143,256]{1,0:T(8,128)S(1)}, f32[143,256]{1,0:T(8,128)S(1)}, u32[]{:S(2)}, u32[]{:S(2)}) collective-permute-start(f32[143,256]{1,0:T(8,128)S(1)} %add.98), channel_id=1, source_target_pairs={{0,128},{16,144},{32,160},{48,176},{64,192},{80,208},{96,224},{112... | collective-permute-start | bytes 439304 | tf_op jit(solution)/shard_map/ppermute | solution.py:62
  298.4 6.4 %collective-permute-done.3 = f32[143,256]{1,0:T(8,128)S(1)} collective-permute-done((f32[143,256]{1,0:T(8,128)S(1)}, f32[143,256]{1,0:T(8,128)S(1)}, u32[]{:S(2)}, u32[]{:S(2)}) %collective-permute-start.3) | collective-permute-done | bytes 146464 | tf_op jit(solution)/shard_map/ppermute | solution.py:62
  304.8 7.7 %collective-permute-start.4 = (f32[143,256]{1,0:T(8,128)S(1)}, f32[143,256]{1,0:T(8,128)S(1)}, u32[]{:S(2)}, u32[]{:S(2)}) collective-permute-start(f32[143,256]{1,0:T(8,128)S(1)} %add.99), channel_id=1, source_target_pairs={{0,256},{16,272},{32,288},{48,304},{64,320},{80,336},{96,352},{112... | collective-permute-start | bytes 439304 | tf_op jit(solution)/shard_map/ppermute | solution.py:62
  312.5 6.9 %collective-permute-done.4 = f32[143,256]{1,0:T(8,128)S(1)} collective-permute-done((f32[143,256]{1,0:T(8,128)S(1)}, f32[143,256]{1,0:T(8,128)S(1)}, u32[]{:S(2)}, u32[]{:S(2)}) %collective-permute-start.4) | collective-permute-done | bytes 146464 | tf_op jit(solution)/shard_map/ppermute | solution.py:62
  321.3 2.8 copy.40
  324.0 2.3 broadcast_in_dim.44
  (57 shorter events, 8.6 us)
Async XLA Ops:
  1.9 21.2 %all-to-all-start = ((bf16[1,128,16]{1,0,2:T(2,128)(2,1)}), bf16[1,128,16]{1,0,2:T(2,128)(2,1)S(1)}, u32[]{:S(2)}, u32[]{:S(2)}) async-start(bf16[1,128,16]{1,0,2:T(2,128)(2,1)} %broadcast_in_dim.39), calls=%async_computation | async-start | bytes 16384 | tf_op jit(solution)/shard_map/all_to_all | solution.py:80
  23.1 8.0 %copy-start.4 = (bf16[128,256]{1,0:T(8,128)(2,1)S(1)}, bf16[128,256]{1,0:T(8,128)(2,1)}, u32[]{:S(2)}) copy-start(bf16[128,256]{1,0:T(8,128)(2,1)} %param.8) | copy-start | bytes 196612
  23.1 8.1 %copy-start.6 = (f32[2,7,256]{2,0,1:T(2,128)S(1)}, f32[2,7,256]{2,0,1:T(2,128)}, u32[]{:S(2)}) copy-start(f32[2,7,256]{2,0,1:T(2,128)} %param.7) | copy-start | bytes 43012
  23.1 39.5 %all-to-all-start.1 = ((bf16[2,128,4096]{1,0,2:T(2,128)(2,1)}), bf16[2,128,4096]{1,0,2:T(2,128)(2,1)S(1)}, u32[]{:S(2)}, u32[]{:S(2)}) async-start(bf16[2,128,4096]{1,0,2:T(2,128)(2,1)} %bitcast.5), calls=%async_computation.1 | async-start | bytes 4194304 | tf_op jit(solution)/shard_map/all_to_all | solution.py:79
  62.6 1.3 copy-start.2
  72.8 1.0 copy-start.3
  73.8 0.8 copy-start.7
  122.5 0.7 copy-start.5
  175.8 1.0 copy-start
  194.7 126.6 %all-to-all-start.2 = ((bf16[2,2048,256]{2,0,1:T(2,128)(2,1)}), bf16[2,2048,256]{2,0,1:T(2,128)(2,1)}, u32[]{:S(2)}, u32[]{:S(2)}) async-start(bf16[2,2048,256]{2,0,1:T(2,128)(2,1)} %copy.39), calls=%async_computation.2 | async-start | bytes 4194304 | tf_op jit(solution)/shard_map/all_to_all | solution.py:96
  247.2 1.9 copy-start.1
  252.9 19.5 %collective-permute-start = (f32[143,256]{1,0:T(8,128)S(1)}, f32[143,256]{1,0:T(8,128)S(1)}, u32[]{:S(2)}, u32[]{:S(2)}) collective-permute-start(f32[143,256]{1,0:T(8,128)S(1)} %pad_maximum_fusion.1), channel_id=1, source_target_pairs={{0,16},{16,0},{32,48},{48,32},{64,80},{80,64},{96,112},{112,96},{1... | collective-permute-start | bytes 439304 | tf_op jit(solution)/shard_map/ppermute | solution.py:62
  272.4 13.7 %collective-permute-start.1 = (f32[143,256]{1,0:T(8,128)S(1)}, f32[143,256]{1,0:T(8,128)S(1)}, u32[]{:S(2)}, u32[]{:S(2)}) collective-permute-start(f32[143,256]{1,0:T(8,128)S(1)} %fusion.69), channel_id=1, source_target_pairs={{0,32},{16,48},{32,0},{48,16},{64,96},{80,112},{96,64},{112,80},{1... | collective-permute-start | bytes 439304 | tf_op jit(solution)/shard_map/ppermute | solution.py:62
  286.1 7.7 %collective-permute-start.2 = (f32[143,256]{1,0:T(8,128)S(1)}, f32[143,256]{1,0:T(8,128)S(1)}, u32[]{:S(2)}, u32[]{:S(2)}) collective-permute-start(f32[143,256]{1,0:T(8,128)S(1)} %add.97), channel_id=1, source_target_pairs={{0,64},{16,80},{32,96},{48,112},{64,0},{80,16},{96,32},{112,48},{1... | collective-permute-start | bytes 439304 | tf_op jit(solution)/shard_map/ppermute | solution.py:62
  293.9 10.9 %collective-permute-start.3 = (f32[143,256]{1,0:T(8,128)S(1)}, f32[143,256]{1,0:T(8,128)S(1)}, u32[]{:S(2)}, u32[]{:S(2)}) collective-permute-start(f32[143,256]{1,0:T(8,128)S(1)} %add.98), channel_id=1, source_target_pairs={{0,128},{16,144},{32,160},{48,176},{64,192},{80,208},{96,224},{112... | collective-permute-start | bytes 439304 | tf_op jit(solution)/shard_map/ppermute | solution.py:62
  304.8 14.6 %collective-permute-start.4 = (f32[143,256]{1,0:T(8,128)S(1)}, f32[143,256]{1,0:T(8,128)S(1)}, u32[]{:S(2)}, u32[]{:S(2)}) collective-permute-start(f32[143,256]{1,0:T(8,128)S(1)} %add.99), channel_id=1, source_target_pairs={{0,256},{16,272},{32,288},{48,304},{64,320},{80,336},{96,352},{112... | collective-permute-start | bytes 439304 | tf_op jit(solution)/shard_map/ppermute | solution.py:62

commit v2 on v1

--- a/solution.py
+++ b/solution.py
@@ -71,21 +71,26 @@
     length = inputs.shape[1]
     groups = lax.axis_size("dp")
     shards = lax.axis_size("ctx")
-    loss_weight = jnp.where((token_ids[0] >= 97) & (token_ids[0] <= 122), 0.1, 1.0).astype(
-        jnp.bfloat16
+    all_inputs = lax.all_to_all(inputs, "ctx", split_axis=2, concat_axis=1, tiled=True)
+    all_ids = lax.all_gather(token_ids[0], "ctx", tiled=True)
+    weight_seq = (
+        jnp.where((all_ids >= 97) & (all_ids <= 122), 0.1, 1.0)
+        .astype(jnp.bfloat16)
+        .astype(jnp.float32)
     )
-    weight_rows = jnp.broadcast_to(loss_weight[None, :, None], (1, length, shards))
-    all_inputs, all_weight = (
-        lax.all_to_all(inputs, "ctx", split_axis=2, concat_axis=1, tiled=True),
-        lax.all_to_all(weight_rows, "ctx", split_axis=2, concat_axis=1, tiled=True),
-    )
-    weight_seq = all_weight[0, :, 0].astype(jnp.float32)
     padded_inputs = jnp.pad(all_inputs, ((0, 0), (short_len - 1, 0), (0, 0)))
     filtered = short_forward(padded_inputs, short_filters)
     product = (filtered[0] * filtered[1]).astype(jnp.bfloat16)
     padded_product = jnp.pad(product, ((filter_len - 1, 0), (0, 0)))
     mix = depthwise(padded_product, medium_filter[::-1]) + skip_gain * product.astype(jnp.float32)
     grad_mix = (weight_seq[:, None] * mix).astype(jnp.bfloat16)
+    grad_taps = depthwise(padded_product, grad_mix)[::-1]
+    grad_gain = jnp.sum(grad_mix.astype(jnp.float32) * product.astype(jnp.float32), axis=0)
+    taps = grad_taps.shape[0]
+    stacked = jnp.concatenate([grad_taps, grad_gain[None]], axis=0).astype(jnp.float32)
+    stacked = butterfly_sum(stacked, "dp", groups)
+    grad_taps = stacked[:taps]
+    grad_gain = stacked[taps]
     padded_later = jnp.pad(grad_mix, ((0, filter_len - 1), (0, 0)))
     back_product = depthwise(padded_later, medium_filter) + skip_gain * grad_mix.astype(jnp.float32)
     grad_key = (back_product * filtered[1]).astype(jnp.bfloat16)
@@ -94,17 +99,8 @@
     padded_grads = jnp.pad(grad_filtered, ((0, 0), (0, short_len - 1), (0, 0)))
     grad_channels = short_backward(padded_grads, short_filters).astype(jnp.bfloat16)
     grad_inputs = lax.all_to_all(grad_channels, "ctx", split_axis=1, concat_axis=2, tiled=True)
-    grad_taps = depthwise(padded_product, grad_mix)[::-1]
-    grad_gain = jnp.sum(grad_mix.astype(jnp.float32) * product.astype(jnp.float32), axis=0)
     grad_short = short_weights(grad_filtered, padded_inputs)
-    taps = grad_taps.shape[0]
-    stacked = jnp.concatenate(
-        [grad_taps, grad_short.reshape(-1, grad_short.shape[-1]), grad_gain[None]], axis=0
-    ).astype(jnp.float32)
-    stacked = butterfly_sum(stacked, "dp", groups)
-    grad_taps = stacked[:taps]
-    grad_short = stacked[taps : taps + grad_short.shape[0] * short_len].reshape(grad_short.shape)
-    grad_gain = stacked[-1]
+    grad_short = butterfly_sum(grad_short.astype(jnp.float32), "dp", groups)
     return (grad_inputs[:, None], grad_short / groups, grad_taps / groups, grad_gain / groups)
 
 

time: 328 us -> 354 us (1.079)
  blocking collectives: 0 us -> 64.3 us
  waiting for transfers between devices: 70.2 us -> 50.8 us
  starting transfers between devices: 74.5 us -> 56.6 us
    all_gather x0 -> x1, blocking collectives: none -> 64.3 us  [local(): all_ids = lax.all_gather(token_ids[0], 'ctx', tiled=True)]
    all_to_all x1, waiting for transfers between devices: 31.3 us -> 0.01 us  [local(): lax.all_to_all(inputs, 'ctx', split_axis=2, concat_axis=1, tiled=True)]
    ppermute x5 -> x10, waiting for transfers between devices: 37.1 us -> 50.8 us  [butterfly_sum(): value = value + lax.ppermute(value, axis, perm)]
    all_to_all x1, starting transfers between devices: 23.9 us -> 10.4 us  [local(): lax.all_to_all(grad_channels, 'ctx', split_axis=1, concat_axis=2, tiled=T...]
    all_to_all x1 -> x0, starting transfers between devices: 13.2 us -> none  [local(): lax.all_to_all(weight_rows, 'ctx', split_axis=2, concat_axis=1, tiled=True)]
    all_to_all x1, starting transfers between devices: 7.98 us -> 13.4 us  [local(): lax.all_to_all(inputs, 'ctx', split_axis=2, concat_axis=1, tiled=True)]
    ppermute x5 -> x10, starting transfers between devices: 29.3 us -> 32.8 us  [butterfly_sum(): value = value + lax.ppermute(value, axis, perm)]
    unnamed x19 -> x26, local copies, waits for them, and re-layouts: 9.91 us -> 9.35 us
  transfers between devices with their start and end apart: 8 -> 12, of which waited for: 7 -> 8; matrix products, arithmetic and copies ran while one was open for 13% -> 10% of each run, Pallas kernels for 0% -> 0%
where the time goes in v2:
time: 354 us; the launch traced here: 352 us
  matrix products  124 us (35%)
  blocking collectives  64.3 us (18%)
  starting transfers between devices  56.6 us (16%)
  waiting for transfers between devices  50.8 us (14%)
  local copies, waits for them, and re-layouts  36.5 us (10%)
  other arithmetic  18.6 us (5%)
    conv_general_dilated x3, matrix products, depthwise(): lax.conv_general_dilated(extended[None], kernel[:, None, :], (1,), 'VALID...  124 us
    all_gather x1, blocking collectives, local(): all_ids = lax.all_gather(token_ids[0], 'ctx', tiled=True)  64.3 us
    ppermute x10, waiting for transfers between devices, butterfly_sum(): value = value + lax.ppermute(value, axis, perm)  50.8 us
    ppermute x10, starting transfers between devices, butterfly_sum(): value = value + lax.ppermute(value, axis, perm)  32.8 us
    convert_element_type x1, local copies, waits for them, and re-layouts, local(): short_backward(padded_grads, short_filters).astype(jnp.bfloat16)  14.2 us
    all_to_all x1, starting transfers between devices, local(): lax.all_to_all(inputs, 'ctx', split_axis=2, concat_axis=1, tiled=True)  13.4 us
    all_to_all x1, starting transfers between devices, local(): lax.all_to_all(grad_channels, 'ctx', split_axis=1, concat_axis=2, tiled=T...  10.4 us
    unnamed x26, local copies, waits for them, and re-layouts  9.35 us
  transfers between devices with their start and end apart: 12, of which 8 were waited for; matrix products, arithmetic and copies ran while one was open for 10% of the time, Pallas kernels for 0%

profile of v2, /device:TPU:6, one launch (start us, length us, event | category | flops | bytes accessed | tf_op | source)
XLA Modules:
  0.0 352.0 jit_solution(2197330277565388248)
XLA Ops:
  0.6 6.2 %copy.26 = bf16[2,1,128,4096]{2,0,3,1:T(2,128)(2,1)} copy(bf16[2,1,128,4096]{3,2,1,0:T(8,128)(2,1)} %param.5) | data formatting | bytes 4194304 | tf_op args[0]
  6.8 13.4 %all-to-all-start = ((bf16[2,128,4096]{1,0,2:T(2,128)(2,1)}), bf16[2,128,4096]{1,0,2:T(2,128)(2,1)S(1)}, u32[]{:S(2)}, u32[]{:S(2)}) async-start(bf16[2,128,4096]{1,0,2:T(2,128)(2,1)} %bitcast.103), calls=%async_computation | async-start | bytes 4194304 | tf_op jit(solution)/shard_map/all_to_all | solution.py:74
  20.3 64.3 %all-gather = s32[1,2048]{1,0:T(1,128)S(1)} all-gather(s32[1,128]{1,0:T(1,128)S(1)} %copy-done.7), channel_id=2, replica_groups=mesh['dp'=32,'ctx'=16] {'ctx'}, dimensions={1}, use_global_device_ids=true | all-gather | bytes 8704 | tf_op jit(solution)/shard_map/all_gather | solution.py:75
  86.0 4.7 %copy.27 = bf16[2,128,16,256]{3,1,2,0:T(8,128)(2,1)S(1)} copy(bf16[2,128,16,256]{1,0,3,2:T(2,128)(2,1)} %bitcast.102) | data formatting | bytes 4194304 | tf_op jit(solution)/shard_map/all_to_all | solution.py:74
  90.7 3.7 %fusion.5 = f32[2,2048,256]{2,1,0:T(8,128)S(1)} fusion(bf16[2,2048,256]{2,1,0:T(8,128)(2,1)S(1)} %bitcast.93, f32[2,256]{1,0:T(2,128)S(1)} %get-tuple-element.19, f32[2,256]{1,0:T(2,128)S(1)} %get-tuple-element.20, f32[2,256]{1,0:T(2,128)S(1)} %get-tuple-element.15, f32[2,256]{1,0:T(2,128)S(1)} %get-tuple-element.16, f32[2,256]{1,0:T(2,128)S(1)} %get-tuple-element.17, ...), kind=kLoop, calls=%fused_computation.18 | loop fusion | flops 20971520 | bytes 6305792 | tf_op jit(solution)/shard_map/add | solution.py:13
  96.7 47.9 %fusion.52 = f32[8,272,256]{2,0,1:T(8,128)S(1)} fusion(pred[8,272]{0,1:T(8,128)(4,1)S(1)} %copy-done.8, bf16[128,1,256]{2,0,1:T(8,128)(2,1)S(1)} %bitcast.111, bf16[8,399,256]{2,0,1:T(8,128)(2,1)S(1)} %fusion.76), kind=kOutput, calls=%fused_computation.76 | convolution fusion | flops 143163392 | bytes 3930240 | tf_op jit(solution)/shard_map/conv_general_dilated | solution.py:46
  148.0 48.0 %fusion.49 = f32[8,272,256]{2,0,1:T(8,128)S(1)} fusion(pred[8,272]{0,1:T(8,128)(4,1)S(1)} %copy-done.8, bf16[128,1,256]{2,0,1:T(8,128)(2,1)S(1)} %bitcast.110, bf16[8,399,256]{2,0,1:T(8,128)(2,1)S(1)} %fusion.74), kind=kOutput, calls=%fused_computation.75 | convolution fusion | flops 143163392 | bytes 3930240 | tf_op jit(solution)/shard_map/conv_general_dilated | solution.py:46
  198.9 3.7 %fusion.12 = bf16[2,2048,256]{2,1,0:T(8,128)(2,1)S(1)} fusion(bf16[2,2048,256]{2,1,0:T(8,128)(2,1)S(1)} %pad_maximum_fusion, f32[2,256]{1,0:T(2,128)S(1)} %get-tuple-element.19, f32[2,256]{1,0:T(2,128)S(1)} %get-tuple-element.20, f32[2,256]{1,0:T(2,128)S(1)} %get-tuple-element.15, f32[2,256]{1,0:T(2,128)S(1)} %get-tuple-element.16, ...), kind=kLoop, calls=%fused_computation.25 | loop fusion | flops 22020096 | bytes 4208640 | tf_op jit(solution)/shard_map/convert_element_type | solution.py:100
  202.6 14.2 %copy.36 = bf16[2,2048,256]{2,0,1:T(2,128)(2,1)} copy(bf16[2,2048,256]{2,1,0:T(8,128)(2,1)S(1)} %fusion.12) | data formatting | bytes 4194304 | tf_op jit(solution)/shard_map/convert_element_type | solution.py:100
  216.8 10.4 %all-to-all-start.1 = ((bf16[2,2048,256]{2,0,1:T(2,128)(2,1)}), bf16[2,2048,256]{2,0,1:T(2,128)(2,1)}, u32[]{:S(2)}, u32[]{:S(2)}) async-start(bf16[2,2048,256]{2,0,1:T(2,128)(2,1)} %copy.36), calls=%async_computation.1 | async-start | bytes 4194304 | tf_op jit(solution)/shard_map/all_to_all | solution.py:101
  227.2 28.2 %fusion.21 = f32[1,128,256]{2,0,1:T(1,128)S(1)} fusion(bf16[1,2175,256]{2,1,0:T(8,128)(2,1)} %copy-done.3, bf16[2048,1,256]{2,0,1:T(8,128)(2,1)} %fusion.33), kind=kOutput, calls=%fused_computation.40 | convolution fusion | flops 134217728 | bytes 2293248 | tf_op jit(solution)/shard_map/conv_general_dilated | solution.py:46
  255.6 3.3 collective-permute-start.5
  260.8 3.6 %fusion.18 = (f32[2,256]{1,0:T(2,128)S(1)}, f32[2,256]{1,0:T(2,128)S(1)}, f32[2,256]{1,0:T(2,128)S(1)}, f32[2,256]{1,0:T(2,128)S(1)}, f32[2,256]{1,0:T(2,128)S(1)}, /*index=5*/f32[2,256]{1,0:T(2,128)S(1)}) fusion(bf16[2,2048,256]{2,1,0:T(8,128)(2,1)S(1)} %bitcast.94, bf16[1,2048,256]{2,1,0:T(8,128)(2,1)S(1)} %copy-done.1, ...), kind=kLoop, calls=%fused_computation.31 | loop fusion | flops 23065600 | bytes 4206592 | tf_op jit(solution)/shard_map/reduce_sum | solution.py:37
  264.4 16.2 %collective-permute-done.5 = f32[129,256]{1,0:T(8,128)S(1)} collective-permute-done((f32[129,256]{1,0:T(8,128)S(1)}, f32[129,256]{1,0:T(8,128)S(1)}, u32[]{:S(2)}, u32[]{:S(2)}) %collective-permute-start.5) | collective-permute-done | bytes 132128 | tf_op jit(solution)/shard_map/ppermute | solution.py:62
  280.7 1.9 collective-permute-start.6
  282.6 9.4 %collective-permute-done.6 = f32[129,256]{1,0:T(8,128)S(1)} collective-permute-done((f32[129,256]{1,0:T(8,128)S(1)}, f32[129,256]{1,0:T(8,128)S(1)}, u32[]{:S(2)}, u32[]{:S(2)}) %collective-permute-start.6) | collective-permute-done | bytes 132128 | tf_op jit(solution)/shard_map/ppermute | solution.py:62
  292.1 3.5 collective-permute-start.7
  295.6 3.4 collective-permute-done.7
  299.1 4.5 %collective-permute-start.8 = (f32[129,256]{1,0:T(8,128)S(1)}, f32[129,256]{1,0:T(8,128)S(1)}, u32[]{:S(2)}, u32[]{:S(2)}) collective-permute-start(f32[129,256]{1,0:T(8,128)S(1)} %add.118), channel_id=1, source_target_pairs={{0,128},{16,144},{32,160},{48,176},{64,192},{80,208},{96,224},{112... | collective-permute-start | bytes 396296 | tf_op jit(solution)/shard_map/ppermute | solution.py:62
  303.6 1.9 collective-permute-start
  305.5 3.7 %collective-permute-done = f32[2,7,256]{2,0,1:T(2,128)S(1)} collective-permute-done((f32[2,7,256]{2,0,1:T(2,128)S(1)}, f32[2,7,256]{2,0,1:T(2,128)S(1)}, u32[]{:S(2)}, u32[]{:S(2)}) %collective-permute-start) | collective-permute-done | bytes 14368 | tf_op jit(solution)/shard_map/ppermute | solution.py:62
  309.2 2.2 collective-permute-start.1
  311.4 4.3 %collective-permute-done.1 = f32[2,7,256]{2,0,1:T(2,128)S(1)} collective-permute-done((f32[2,7,256]{2,0,1:T(2,128)S(1)}, f32[2,7,256]{2,0,1:T(2,128)S(1)}, u32[]{:S(2)}, u32[]{:S(2)}) %collective-permute-start.1) | collective-permute-done | bytes 14368 | tf_op jit(solution)/shard_map/ppermute | solution.py:62
  315.7 3.5 collective-permute-start.2
  319.2 2.1 collective-permute-done.2
  321.4 2.2 collective-permute-start.3
  323.6 4.3 %collective-permute-done.3 = f32[2,7,256]{2,0,1:T(2,128)S(1)} collective-permute-done((f32[2,7,256]{2,0,1:T(2,128)S(1)}, f32[2,7,256]{2,0,1:T(2,128)S(1)}, u32[]{:S(2)}, u32[]{:S(2)}) %collective-permute-start.3) | collective-permute-done | bytes 14368 | tf_op jit(solution)/shard_map/ppermute | solution.py:62
  327.9 6.2 %collective-permute-start.4 = (f32[2,7,256]{2,0,1:T(2,128)S(1)}, f32[2,7,256]{2,0,1:T(2,128)S(1)}, u32[]{:S(2)}, u32[]{:S(2)}) collective-permute-start(f32[2,7,256]{2,0,1:T(2,128)S(1)} %add.113), channel_id=1, source_target_pairs={{0,256},{16,272},{32,288},{48,304},{64,320},{80,336},{96,352},{112... | collective-permute-start | bytes 43016 | tf_op jit(solution)/shard_map/ppermute | solution.py:62
  334.1 3.6 %collective-permute-start.9 = (f32[129,256]{1,0:T(8,128)S(1)}, f32[129,256]{1,0:T(8,128)S(1)}, u32[]{:S(2)}, u32[]{:S(2)}) collective-permute-start(f32[129,256]{1,0:T(8,128)S(1)} %add.119), channel_id=1, source_target_pairs={{0,256},{16,272},{32,288},{48,304},{64,320},{80,336},{96,352},{112... | collective-permute-start | bytes 396296 | tf_op jit(solution)/shard_map/ppermute | solution.py:62
  338.3 7.3 %collective-permute-done.9 = f32[129,256]{1,0:T(8,128)S(1)} collective-permute-done((f32[129,256]{1,0:T(8,128)S(1)}, f32[129,256]{1,0:T(8,128)S(1)}, u32[]{:S(2)}, u32[]{:S(2)}) %collective-permute-start.9) | collective-permute-done | bytes 132128 | tf_op jit(solution)/shard_map/ppermute | solution.py:62
  346.9 2.8 copy.37
  349.7 2.3 broadcast_in_dim.37
  (66 shorter events, 13.9 us)
Async XLA Ops:
  6.8 13.4 %copy-start.4 = (bf16[128,256]{1,0:T(8,128)(2,1)S(1)}, bf16[128,256]{1,0:T(8,128)(2,1)}, u32[]{:S(2)}) copy-start(bf16[128,256]{1,0:T(8,128)(2,1)} %param.8) | copy-start | bytes 196612
  6.8 13.5 %copy-start.7 = (s32[1,128]{1,0:T(1,128)S(1)}, s32[1,128]{1,0:T(1,128)}, u32[]{:S(2)}) copy-start(s32[1,128]{1,0:T(1,128)} %param.6) | copy-start | bytes 1540
  6.8 77.9 %copy-start.6 = (f32[2,7,256]{2,0,1:T(2,128)S(1)}, f32[2,7,256]{2,0,1:T(2,128)}, u32[]{:S(2)}) copy-start(f32[2,7,256]{2,0,1:T(2,128)} %param.7) | copy-start | bytes 43012
  6.8 77.9 %all-to-all-start = ((bf16[2,128,4096]{1,0,2:T(2,128)(2,1)}), bf16[2,128,4096]{1,0,2:T(2,128)(2,1)S(1)}, u32[]{:S(2)}, u32[]{:S(2)}) async-start(bf16[2,128,4096]{1,0,2:T(2,128)(2,1)} %bitcast.103), calls=%async_computation | async-start | bytes 4194304 | tf_op jit(solution)/shard_map/all_to_all | solution.py:74
  84.7 1.3 copy-start.2
  94.9 1.0 copy-start.3
  96.0 0.8 copy-start.8
  144.6 0.7 copy-start.5
  197.9 1.0 copy-start
  216.8 130.1 %all-to-all-start.1 = ((bf16[2,2048,256]{2,0,1:T(2,128)(2,1)}), bf16[2,2048,256]{2,0,1:T(2,128)(2,1)}, u32[]{:S(2)}, u32[]{:S(2)}) async-start(bf16[2,2048,256]{2,0,1:T(2,128)(2,1)} %copy.36), calls=%async_computation.1 | async-start | bytes 4194304 | tf_op jit(solution)/shard_map/all_to_all | solution.py:101
  255.6 25.1 %collective-permute-start.5 = (f32[129,256]{1,0:T(8,128)S(1)}, f32[129,256]{1,0:T(8,128)S(1)}, u32[]{:S(2)}, u32[]{:S(2)}) collective-permute-start(f32[129,256]{1,0:T(8,128)S(1)} %pad_maximum_fusion.1), channel_id=1, source_target_pairs={{0,16},{16,0},{32,48},{48,32},{64,80},{80,64},{96,112},{112,96},{1... | collective-permute-start | bytes 396296 | tf_op jit(solution)/shard_map/ppermute | solution.py:62
  258.8 1.9 copy-start.1
  280.7 11.4 %collective-permute-start.6 = (f32[129,256]{1,0:T(8,128)S(1)}, f32[129,256]{1,0:T(8,128)S(1)}, u32[]{:S(2)}, u32[]{:S(2)}) collective-permute-start(f32[129,256]{1,0:T(8,128)S(1)} %fusion.67), channel_id=1, source_target_pairs={{0,32},{16,48},{32,0},{48,16},{64,96},{80,112},{96,64},{112,80},{1... | collective-permute-start | bytes 396296 | tf_op jit(solution)/shard_map/ppermute | solution.py:62
  292.1 6.9 %collective-permute-start.7 = (f32[129,256]{1,0:T(8,128)S(1)}, f32[129,256]{1,0:T(8,128)S(1)}, u32[]{:S(2)}, u32[]{:S(2)}) collective-permute-start(f32[129,256]{1,0:T(8,128)S(1)} %add.117), channel_id=1, source_target_pairs={{0,64},{16,80},{32,96},{48,112},{64,0},{80,16},{96,32},{112,48},{1... | collective-permute-start | bytes 396296 | tf_op jit(solution)/shard_map/ppermute | solution.py:62
  299.1 35.0 %collective-permute-start.8 = (f32[129,256]{1,0:T(8,128)S(1)}, f32[129,256]{1,0:T(8,128)S(1)}, u32[]{:S(2)}, u32[]{:S(2)}) collective-permute-start(f32[129,256]{1,0:T(8,128)S(1)} %add.118), channel_id=1, source_target_pairs={{0,128},{16,144},{32,160},{48,176},{64,192},{80,208},{96,224},{112... | collective-permute-start | bytes 396296 | tf_op jit(solution)/shard_map/ppermute | solution.py:62
  303.6 5.6 %collective-permute-start = (f32[2,7,256]{2,0,1:T(2,128)S(1)}, f32[2,7,256]{2,0,1:T(2,128)S(1)}, u32[]{:S(2)}, u32[]{:S(2)}) collective-permute-start(f32[2,7,256]{2,0,1:T(2,128)S(1)} %constant_dynamic-update-slice_fusion), channel_id=1, source_target_pairs={{0,16},{16,0},{32,48},{48,32},{64,80},{80,64},{96,112},{112,96},{1... | collective-permute-start | bytes 43016 | tf_op jit(solution)/shard_map/ppermute | solution.py:62
  309.2 6.5 %collective-permute-start.1 = (f32[2,7,256]{2,0,1:T(2,128)S(1)}, f32[2,7,256]{2,0,1:T(2,128)S(1)}, u32[]{:S(2)}, u32[]{:S(2)}) collective-permute-start(f32[2,7,256]{2,0,1:T(2,128)S(1)} %add.110), channel_id=1, source_target_pairs={{0,32},{16,48},{32,0},{48,16},{64,96},{80,112},{96,64},{112,80},{1... | collective-permute-start | bytes 43016 | tf_op jit(solution)/shard_map/ppermute | solution.py:62
  315.7 5.6 %collective-permute-start.2 = (f32[2,7,256]{2,0,1:T(2,128)S(1)}, f32[2,7,256]{2,0,1:T(2,128)S(1)}, u32[]{:S(2)}, u32[]{:S(2)}) collective-permute-start(f32[2,7,256]{2,0,1:T(2,128)S(1)} %add.111), channel_id=1, source_target_pairs={{0,64},{16,80},{32,96},{48,112},{64,0},{80,16},{96,32},{112,48},{1... | collective-permute-start | bytes 43016 | tf_op jit(solution)/shard_map/ppermute | solution.py:62
  321.4 6.5 %collective-permute-start.3 = (f32[2,7,256]{2,0,1:T(2,128)S(1)}, f32[2,7,256]{2,0,1:T(2,128)S(1)}, u32[]{:S(2)}, u32[]{:S(2)}) collective-permute-start(f32[2,7,256]{2,0,1:T(2,128)S(1)} %add.112), channel_id=1, source_target_pairs={{0,128},{16,144},{32,160},{48,176},{64,192},{80,208},{96,224},{112... | collective-permute-start | bytes 43016 | tf_op jit(solution)/shard_map/ppermute | solution.py:62
  327.9 9.8 %collective-permute-start.4 = (f32[2,7,256]{2,0,1:T(2,128)S(1)}, f32[2,7,256]{2,0,1:T(2,128)S(1)}, u32[]{:S(2)}, u32[]{:S(2)}) collective-permute-start(f32[2,7,256]{2,0,1:T(2,128)S(1)} %add.113), channel_id=1, source_target_pairs={{0,256},{16,272},{32,288},{48,304},{64,320},{80,336},{96,352},{112... | collective-permute-start | bytes 43016 | tf_op jit(solution)/shard_map/ppermute | solution.py:62
  334.1 11.5 %collective-permute-start.9 = (f32[129,256]{1,0:T(8,128)S(1)}, f32[129,256]{1,0:T(8,128)S(1)}, u32[]{:S(2)}, u32[]{:S(2)}) collective-permute-start(f32[129,256]{1,0:T(8,128)S(1)} %add.119), channel_id=1, source_target_pairs={{0,256},{16,272},{32,288},{48,304},{64,320},{80,336},{96,352},{112... | collective-permute-start | bytes 396296 | tf_op jit(solution)/shard_map/ppermute | solution.py:62

commit v3 on v1

--- a/solution.py
+++ b/solution.py
@@ -64,6 +64,17 @@
     return value
 
 
+def exchange_sum(value, axis, size):
+    rows = value.shape[0]
+    piece = -(-rows // size)
+    padded = jnp.pad(value, ((0, piece * size - rows), (0, 0))).reshape(size, piece, -1)
+    received = lax.all_to_all(padded, axis, split_axis=0, concat_axis=0, tiled=True)
+    reduced = jnp.sum(received, axis=0)
+    spread = jnp.broadcast_to(reduced[None], (size,) + reduced.shape)
+    gathered = lax.all_to_all(spread, axis, split_axis=0, concat_axis=0, tiled=True)
+    return gathered.reshape(size * piece, -1)[:rows]
+
+
 def local(projected, token_ids, short_filters, medium_filter, skip_gain):
     inputs = projected[:, 0]
     short_len = short_filters.shape[1]
@@ -101,7 +112,7 @@
     stacked = jnp.concatenate(
         [grad_taps, grad_short.reshape(-1, grad_short.shape[-1]), grad_gain[None]], axis=0
     ).astype(jnp.float32)
-    stacked = butterfly_sum(stacked, "dp", groups)
+    stacked = exchange_sum(stacked, "dp", groups)
     grad_taps = stacked[:taps]
     grad_short = stacked[taps : taps + grad_short.shape[0] * short_len].reshape(grad_short.shape)
     grad_gain = stacked[-1]

time: 328 us -> 343 us (1.046)
  the two profiles are of different devices: /device:TPU:6 before, /device:TPU:143 now
where the time goes in v3:
time: 343 us; the launch traced here: 342 us
  matrix products  122 us (36%)
  waiting for transfers between devices  117 us (34%)
  starting transfers between devices  42 us (12%)
  local copies, waits for them, and re-layouts  41.9 us (12%)
  other arithmetic  17.8 us (5%)
    conv_general_dilated x3, matrix products, depthwise(): lax.conv_general_dilated(extended[None], kernel[:, None, :], (1,), 'VALID...  122 us
    all_to_all x1, waiting for transfers between devices, local(): lax.all_to_all(inputs, 'ctx', split_axis=2, concat_axis=1, tiled=True)  54.7 us
    all_to_all x1, waiting for transfers between devices, local(): lax.all_to_all(grad_channels, 'ctx', split_axis=1, concat_axis=2, tiled=T...  53 us
    convert_element_type x1, local copies, waits for them, and re-layouts, local(): short_backward(padded_grads, short_filters).astype(jnp.bfloat16)  14 us
    all_to_all x1, starting transfers between devices, local(): lax.all_to_all(weight_rows, 'ctx', split_axis=2, concat_axis=1, tiled=True)  11.7 us
    unnamed x23, local copies, waits for them, and re-layouts  11 us
    all_to_all x1, starting transfers between devices, exchange_sum(): lax.all_to_all(padded, axis, split_axis=0, concat_axis=0, tiled=True)  8.94 us
    all_to_all x1, starting transfers between devices, local(): lax.all_to_all(inputs, 'ctx', split_axis=2, concat_axis=1, tiled=True)  8.23 us
  transfers between devices with their start and end apart: 5, of which 4 were waited for; matrix products, arithmetic and copies ran while one was open for 8% of the time, Pallas kernels for 0%

profile of v3, /device:TPU:143, one launch (start us, length us, event | category | flops | bytes accessed | tf_op | source)
XLA Modules:
  0.0 342.4 jit_solution(13362662046561449137)
XLA Ops:
  0.6 0.7 fusion.60
  1.9 11.7 %all-to-all-start = ((bf16[1,128,16]{1,0,2:T(2,128)(2,1)}), bf16[1,128,16]{1,0,2:T(2,128)(2,1)S(1)}, u32[]{:S(2)}, u32[]{:S(2)}) async-start(bf16[1,128,16]{1,0,2:T(2,128)(2,1)} %broadcast_in_dim.45), calls=%async_computation | async-start | bytes 16384 | tf_op jit(solution)/shard_map/all_to_all | solution.py:91
  13.6 6.2 %copy.28 = bf16[2,1,128,4096]{2,0,3,1:T(2,128)(2,1)} copy(bf16[2,1,128,4096]{3,2,1,0:T(8,128)(2,1)} %param.5) | data formatting | bytes 4194304 | tf_op args[0]
  19.8 1.5 all-to-all-done
  21.3 8.2 %all-to-all-start.1 = ((bf16[2,128,4096]{1,0,2:T(2,128)(2,1)}), bf16[2,128,4096]{1,0,2:T(2,128)(2,1)S(1)}, u32[]{:S(2)}, u32[]{:S(2)}) async-start(bf16[2,128,4096]{1,0,2:T(2,128)(2,1)} %bitcast.5), calls=%async_computation.1 | async-start | bytes 4194304 | tf_op jit(solution)/shard_map/all_to_all | solution.py:90
  29.7 54.7 %all-to-all-done.1 = bf16[2,128,4096]{1,0,2:T(2,128)(2,1)S(1)} async-done(((bf16[2,128,4096]{1,0,2:T(2,128)(2,1)}), bf16[2,128,4096]{1,0,2:T(2,128)(2,1)S(1)}, u32[]{:S(2)}, u32[]{:S(2)}) %all-to-all-start.1) | async-done | bytes 2097184 | tf_op jit(solution)/shard_map/all_to_all | solution.py:90
  84.4 1.3 copy-done.5
  85.7 4.7 %copy.29 = bf16[2,128,16,256]{3,1,2,0:T(8,128)(2,1)S(1)} copy(bf16[2,128,16,256]{1,0,3,2:T(2,128)(2,1)} %bitcast.96) | data formatting | bytes 4194304 | tf_op jit(solution)/shard_map/all_to_all | solution.py:90
  90.5 3.7 %fusion.5 = f32[2,2048,256]{2,1,0:T(8,128)S(1)} fusion(bf16[2,2048,256]{2,1,0:T(8,128)(2,1)S(1)} %bitcast.87, f32[2,256]{1,0:T(2,128)S(1)} %get-tuple-element.27, f32[2,256]{1,0:T(2,128)S(1)} %get-tuple-element.28, f32[2,256]{1,0:T(2,128)S(1)} %get-tuple-element.23, f32[2,256]{1,0:T(2,128)S(1)} %get-tuple-element.24, f32[2,256]{1,0:T(2,128)S(1)} %get-tuple-element.25, ...), kind=kLoop, calls=%fused_computation.18 | loop fusion | flops 20971520 | bytes 6305792 | tf_op jit(solution)/shard_map/add | solution.py:13
  95.9 47.9 %fusion.52 = f32[8,272,256]{2,0,1:T(8,128)S(1)} fusion(pred[8,272]{0,1:T(8,128)(4,1)S(1)} %copy-done.9, bf16[128,1,256]{2,0,1:T(8,128)(2,1)S(1)} %bitcast.102, bf16[8,399,256]{2,0,1:T(8,128)(2,1)S(1)} %fusion.75), kind=kOutput, calls=%fused_computation.76 | convolution fusion | flops 143163392 | bytes 3930240 | tf_op jit(solution)/shard_map/conv_general_dilated | solution.py:46
  143.9 0.7 copy.33
  145.1 0.9 copy-done.2
  146.5 26.5 %fusion.21 = f32[1,128,256]{2,0,1:T(1,128)S(1)} fusion(bf16[1,2175,256]{2,1,0:T(8,128)(2,1)S(1)} %pad_bitcast_fusion.1, bf16[2048,1,256]{2,0,1:T(8,128)(2,1)S(1)} %fusion.33), kind=kOutput, calls=%fused_computation.40 | convolution fusion | flops 134217728 | bytes 2293248 | tf_op jit(solution)/shard_map/conv_general_dilated | solution.py:46
  174.2 48.0 %fusion.49 = f32[8,272,256]{2,0,1:T(8,128)S(1)} fusion(pred[8,272]{0,1:T(8,128)(4,1)S(1)} %copy-done.9, bf16[128,1,256]{2,0,1:T(8,128)(2,1)S(1)} %bitcast.101, bf16[8,399,256]{2,0,1:T(8,128)(2,1)S(1)} %fusion.73), kind=kOutput, calls=%fused_computation.75 | convolution fusion | flops 143163392 | bytes 3930240 | tf_op jit(solution)/shard_map/conv_general_dilated | solution.py:46
  222.3 0.7 copy.37
  223.0 1.4 copy-done.1
  224.4 0.8 multiply_convert_fusion.1
  225.7 3.6 %fusion.18 = (f32[2,256]{1,0:T(2,128)S(1)}, f32[2,256]{1,0:T(2,128)S(1)}, f32[2,256]{1,0:T(2,128)S(1)}, f32[2,256]{1,0:T(2,128)S(1)}, f32[2,256]{1,0:T(2,128)S(1)}, /*index=5*/f32[2,256]{1,0:T(2,128)S(1)}) fusion(bf16[2,2048,256]{2,1,0:T(8,128)(2,1)S(1)} %bitcast.88, bf16[1,2048,256]{2,1,0:T(8,128)(2,1)S(1)} %multiply_convert_fusion, ...), kind=kLoop, calls=%fused_computation.31 | loop fusion | flops 23065600 | bytes 4206592 | tf_op jit(solution)/shard_map/reduce_sum | solution.py:37
  229.3 0.7 multiply_reduce_fusion
  230.2 0.7 reshape.177
  230.9 8.9 %all-to-all-start.3 = ((f32[32,5,256]{2,1,0:T(8,128)}), f32[32,5,256]{2,1,0:T(8,128)S(1)}, u32[]{:S(2)}, u32[]{:S(2)}) async-start(f32[32,5,256]{2,1,0:T(8,128)} %reshape.177), calls=%async_computation.3 | async-start | bytes 524288 | tf_op jit(solution)/shard_map/all_to_all | solution.py:71
  239.8 1.4 pad_maximum_fusion
  241.3 8.0 %all-to-all-done.3 = f32[32,5,256]{2,1,0:T(8,128)S(1)} async-done(((f32[32,5,256]{2,1,0:T(8,128)}), f32[32,5,256]{2,1,0:T(8,128)S(1)}, u32[]{:S(2)}, u32[]{:S(2)}) %all-to-all-start.3) | async-done | bytes 163872 | tf_op jit(solution)/shard_map/all_to_all | solution.py:71
  249.3 0.7 broadcast_in_dim.52
  250.0 7.1 %all-to-all-start.4 = ((f32[32,5,256]{2,1,0:T(8,128)}), f32[32,5,256]{2,1,0:T(8,128)S(1)}, u32[]{:S(2)}, u32[]{:S(2)}) async-start(f32[32,5,256]{2,1,0:T(8,128)} %broadcast_in_dim.52), calls=%async_computation.4 | async-start | bytes 524288 | tf_op jit(solution)/shard_map/all_to_all | solution.py:74
  257.2 3.7 %fusion.12 = bf16[2,2048,256]{2,1,0:T(8,128)(2,1)S(1)} fusion(bf16[2,2048,256]{2,1,0:T(8,128)(2,1)S(1)} %pad_maximum_fusion, f32[2,256]{1,0:T(2,128)S(1)} %get-tuple-element.27, f32[2,256]{1,0:T(2,128)S(1)} %get-tuple-element.28, f32[2,256]{1,0:T(2,128)S(1)} %get-tuple-element.23, f32[2,256]{1,0:T(2,128)S(1)} %get-tuple-element.24, ...), kind=kLoop, calls=%fused_computation.25 | loop fusion | flops 22020096 | bytes 4208640 | tf_op jit(solution)/shard_map/convert_element_type | solution.py:106
  260.9 14.0 %copy.38 = bf16[2,2048,256]{2,0,1:T(2,128)(2,1)} copy(bf16[2,2048,256]{2,1,0:T(8,128)(2,1)S(1)} %fusion.12) | data formatting | bytes 4194304 | tf_op jit(solution)/shard_map/convert_element_type | solution.py:106
  274.9 6.0 %all-to-all-start.2 = ((bf16[2,2048,256]{2,0,1:T(2,128)(2,1)}), bf16[2,2048,256]{2,0,1:T(2,128)(2,1)S(1)}, u32[]{:S(2)}, u32[]{:S(2)}) async-start(bf16[2,2048,256]{2,0,1:T(2,128)(2,1)} %copy.38), calls=%async_computation.2 | async-start | bytes 4194304 | tf_op jit(solution)/shard_map/all_to_all | solution.py:107
  282.1 0.7 slice_multiply_fusion
  282.8 53.0 %all-to-all-done.2 = bf16[2,2048,256]{2,0,1:T(2,128)(2,1)S(1)} async-done(((bf16[2,2048,256]{2,0,1:T(2,128)(2,1)}), bf16[2,2048,256]{2,0,1:T(2,128)(2,1)S(1)}, u32[]{:S(2)}, u32[]{:S(2)}) %all-to-all-start.2) | async-done | bytes 2097184 | tf_op jit(solution)/shard_map/all_to_all | solution.py:107
  335.7 2.5 copy.39
  338.3 4.2 %broadcast_in_dim.50 = bf16[2,1,128,4096]{3,2,1,0:T(8,128)(2,1)} reshape(bf16[2,128,16,256]{3,2,1,0:T(8,128)(2,1)} %copy.39) | data formatting | bytes 4194304 | tf_op jit(solution)/shard_map/broadcast_in_dim | solution.py:119
  (54 shorter events, 6.3 us)
Async XLA Ops:
  1.9 19.4 %all-to-all-start = ((bf16[1,128,16]{1,0,2:T(2,128)(2,1)}), bf16[1,128,16]{1,0,2:T(2,128)(2,1)S(1)}, u32[]{:S(2)}, u32[]{:S(2)}) async-start(bf16[1,128,16]{1,0,2:T(2,128)(2,1)} %broadcast_in_dim.45), calls=%async_computation | async-start | bytes 16384 | tf_op jit(solution)/shard_map/all_to_all | solution.py:91
  21.3 8.2 %copy-start.6 = (bf16[128,256]{1,0:T(8,128)(2,1)S(1)}, bf16[128,256]{1,0:T(8,128)(2,1)}, u32[]{:S(2)}) copy-start(bf16[128,256]{1,0:T(8,128)(2,1)} %param.8) | copy-start | bytes 196612
  21.3 8.4 %copy-start.8 = (f32[2,7,256]{2,0,1:T(2,128)S(1)}, f32[2,7,256]{2,0,1:T(2,128)}, u32[]{:S(2)}) copy-start(f32[2,7,256]{2,0,1:T(2,128)} %param.7) | copy-start | bytes 43012
  21.3 63.1 %all-to-all-start.1 = ((bf16[2,128,4096]{1,0,2:T(2,128)(2,1)}), bf16[2,128,4096]{1,0,2:T(2,128)(2,1)S(1)}, u32[]{:S(2)}, u32[]{:S(2)}) async-start(bf16[2,128,4096]{1,0,2:T(2,128)(2,1)} %bitcast.5), calls=%async_computation.1 | async-start | bytes 4194304 | tf_op jit(solution)/shard_map/all_to_all | solution.py:90
  84.4 1.3 copy-start.5
  94.2 50.9 %copy-start = (f32[2,2048,256]{2,1,0:T(8,128)}, f32[2,2048,256]{2,1,0:T(8,128)S(1)}, u32[]{:S(2)}) copy-start(f32[2,2048,256]{2,1,0:T(8,128)S(1)} %fusion.5) | copy-start | bytes 12582916
  95.1 0.8 copy-start.9
  143.9 0.8 copy-start.7
  144.6 1.4 copy-start.2
  174.2 48.8 %copy-start.3 = (f32[8,272,256]{2,1,0:T(8,128)S(1)}, f32[8,272,256]{2,1,0:T(8,128)}, u32[]{:S(2)}) copy-start(f32[8,272,256]{2,1,0:T(8,128)} %copy-done.2) | copy-start | bytes 6684676
  222.2 2.2 copy-start.1
  225.7 3.7 %copy-start.4 = (bf16[1,2048,256]{2,1,0:T(8,128)(2,1)}, bf16[1,2048,256]{2,1,0:T(8,128)(2,1)S(1)}, u32[]{:S(2)}) copy-start(bf16[1,2048,256]{2,1,0:T(8,128)(2,1)S(1)} %multiply_convert_fusion) | copy-start | bytes 3145732
  230.9 18.4 %all-to-all-start.3 = ((f32[32,5,256]{2,1,0:T(8,128)}), f32[32,5,256]{2,1,0:T(8,128)S(1)}, u32[]{:S(2)}, u32[]{:S(2)}) async-start(f32[32,5,256]{2,1,0:T(8,128)} %reshape.177), calls=%async_computation.3 | async-start | bytes 524288 | tf_op jit(solution)/shard_map/all_to_all | solution.py:71
  250.0 24.9 %all-to-all-start.4 = ((f32[32,5,256]{2,1,0:T(8,128)}), f32[32,5,256]{2,1,0:T(8,128)S(1)}, u32[]{:S(2)}, u32[]{:S(2)}) async-start(f32[32,5,256]{2,1,0:T(8,128)} %broadcast_in_dim.52), calls=%async_computation.4 | async-start | bytes 524288 | tf_op jit(solution)/shard_map/all_to_all | solution.py:74
  274.9 60.9 %all-to-all-start.2 = ((bf16[2,2048,256]{2,0,1:T(2,128)(2,1)}), bf16[2,2048,256]{2,0,1:T(2,128)(2,1)S(1)}, u32[]{:S(2)}, u32[]{:S(2)}) async-start(bf16[2,2048,256]{2,0,1:T(2,128)(2,1)} %copy.38), calls=%async_computation.2 | async-start | bytes 4194304 | tf_op jit(solution)/shard_map/all_to_all | solution.py:107

commit v4 on v2

--- a/solution.py
+++ b/solution.py
@@ -71,13 +71,15 @@
     length = inputs.shape[1]
     groups = lax.axis_size("dp")
     shards = lax.axis_size("ctx")
-    all_inputs = lax.all_to_all(inputs, "ctx", split_axis=2, concat_axis=1, tiled=True)
-    all_ids = lax.all_gather(token_ids[0], "ctx", tiled=True)
-    weight_seq = (
-        jnp.where((all_ids >= 97) & (all_ids <= 122), 0.1, 1.0)
-        .astype(jnp.bfloat16)
-        .astype(jnp.float32)
+    loss_weight = jnp.where((token_ids[0] >= 97) & (token_ids[0] <= 122), 0.1, 1.0).astype(
+        jnp.bfloat16
     )
+    weight_rows = jnp.broadcast_to(loss_weight[None, :, None], (1, length, shards))
+    all_inputs, all_weight = (
+        lax.all_to_all(inputs, "ctx", split_axis=2, concat_axis=1, tiled=True),
+        lax.all_to_all(weight_rows, "ctx", split_axis=2, concat_axis=1, tiled=True),
+    )
+    weight_seq = all_weight[0, :, 0].astype(jnp.float32)
     padded_inputs = jnp.pad(all_inputs, ((0, 0), (short_len - 1, 0), (0, 0)))
     filtered = short_forward(padded_inputs, short_filters)
     product = (filtered[0] * filtered[1]).astype(jnp.bfloat16)
@@ -88,11 +90,27 @@
     grad_gain = jnp.sum(grad_mix.astype(jnp.float32) * product.astype(jnp.float32), axis=0)
     taps = grad_taps.shape[0]
     stacked = jnp.concatenate([grad_taps, grad_gain[None]], axis=0).astype(jnp.float32)
-    stacked = butterfly_sum(stacked, "dp", groups)
+    stacked, grad_mix = lax.optimization_barrier((stacked, grad_mix))
+    padded_later = jnp.pad(grad_mix, ((0, filter_len - 1), (0, 0)))
+    pieces = 4
+    span = grad_mix.shape[0] // pieces
+    parts = []
+    bit = 1
+    for k in range(pieces):
+        window = padded_later[k * span : (k + 1) * span + filter_len - 1]
+        if k > 0:
+            stacked = stacked + lax.ppermute(
+                stacked, "dp", [(i, i ^ bit) for i in range(groups)]
+            )
+            bit *= 2
+            stacked, window = lax.optimization_barrier((stacked, window))
+        parts.append(depthwise(window, medium_filter))
+    while bit < groups:
+        stacked = stacked + lax.ppermute(stacked, "dp", [(i, i ^ bit) for i in range(groups)])
+        bit *= 2
     grad_taps = stacked[:taps]
     grad_gain = stacked[taps]
-    padded_later = jnp.pad(grad_mix, ((0, filter_len - 1), (0, 0)))
-    back_product = depthwise(padded_later, medium_filter) + skip_gain * grad_mix.astype(jnp.float32)
+    back_product = jnp.concatenate(parts, axis=0) + skip_gain * grad_mix.astype(jnp.float32)
     grad_key = (back_product * filtered[1]).astype(jnp.bfloat16)
     grad_value = (back_product * filtered[0]).astype(jnp.bfloat16)
     grad_filtered = jnp.stack([grad_key, grad_value])

time: 354 us -> 362 us (1.023)
  the two profiles are of different devices: /device:TPU:6 before, /device:TPU:10 now
where the time goes in v4:
time: 362 us; the launch traced here: 356 us
  matrix products  129 us (36%)
  starting transfers between devices  92.3 us (25%)
  waiting for transfers between devices  81.9 us (23%)
  local copies, waits for them, and re-layouts  34 us (9%)
  other arithmetic  17.6 us (5%)
    conv_general_dilated x6, matrix products, depthwise(): lax.conv_general_dilated(extended[None], kernel[:, None, :], (1,), 'VALID...  129 us
    ppermute x5, waiting for transfers between devices, butterfly_sum(): value = value + lax.ppermute(value, axis, perm)  45 us
    ppermute x5, starting transfers between devices, local(): lax.ppermute(stacked, 'dp', [(i, i ^ bit) for i in range(groups)])  38.9 us
    all_to_all x1, waiting for transfers between devices, local(): lax.all_to_all(inputs, 'ctx', split_axis=2, concat_axis=1, tiled=True)  24.7 us
    ppermute x5, starting transfers between devices, butterfly_sum(): value = value + lax.ppermute(value, axis, perm)  21.6 us
    convert_element_type x1, local copies, waits for them, and re-layouts, local(): short_backward(padded_grads, short_filters).astype(jnp.bfloat16)  14.2 us
    all_to_all x1, starting transfers between devices, local(): lax.all_to_all(weight_rows, 'ctx', split_axis=2, concat_axis=1, tiled=True)  13.3 us
    all_to_all x1, starting transfers between devices, local(): lax.all_to_all(grad_channels, 'ctx', split_axis=1, concat_axis=2, tiled=T...  11.2 us
  transfers between devices with their start and end apart: 13, of which 7 were waited for; matrix products, arithmetic and copies ran while one was open for 15% of the time, Pallas kernels for 0%

profile of v4, /device:TPU:10, one launch (start us, length us, event | category | flops | bytes accessed | tf_op | source)
XLA Modules:
  0.0 356.0 jit_solution(10291783302065598726)
XLA Ops:
  1.9 13.3 %all-to-all-start.1 = ((bf16[1,128,16]{1,0,2:T(2,128)(2,1)}), bf16[1,128,16]{1,0,2:T(2,128)(2,1)S(1)}, u32[]{:S(2)}, u32[]{:S(2)}) async-start(bf16[1,128,16]{1,0,2:T(2,128)(2,1)} %broadcast_in_dim.52), calls=%async_computation.1 | async-start | bytes 16384 | tf_op jit(solution)/shard_map/all_to_all | solution.py:80
  15.2 6.2 %copy.52 = bf16[2,1,128,4096]{2,0,3,1:T(2,128)(2,1)} copy(bf16[2,1,128,4096]{3,2,1,0:T(8,128)(2,1)} %param.5) | data formatting | bytes 4194304 | tf_op args[0]
  21.4 2.4 all-to-all-done.1
  23.7 7.4 %all-to-all-start = ((bf16[2,128,4096]{1,0,2:T(2,128)(2,1)}), bf16[2,128,4096]{1,0,2:T(2,128)(2,1)}, u32[]{:S(2)}, u32[]{:S(2)}) async-start(bf16[2,128,4096]{1,0,2:T(2,128)(2,1)} %bitcast.1), calls=%async_computation | async-start | bytes 4194304 | tf_op jit(solution)/shard_map/all_to_all | solution.py:79
  31.4 24.7 %all-to-all-done = bf16[2,128,4096]{1,0,2:T(2,128)(2,1)} async-done(((bf16[2,128,4096]{1,0,2:T(2,128)(2,1)}), bf16[2,128,4096]{1,0,2:T(2,128)(2,1)}, u32[]{:S(2)}, u32[]{:S(2)}) %all-to-all-start) | async-done | bytes 2097184 | tf_op jit(solution)/shard_map/all_to_all | solution.py:79
  56.1 4.7 %copy.53 = bf16[2,128,16,256]{3,1,2,0:T(8,128)(2,1)S(1)} copy(bf16[2,128,16,256]{1,0,3,2:T(2,128)(2,1)} %bitcast.2) | data formatting | bytes 4194304 | tf_op jit(solution)/shard_map/all_to_all | solution.py:79
  60.9 3.7 %fusion.5 = f32[2,2048,256]{2,1,0:T(8,128)S(1)} fusion(bf16[2,2048,256]{2,1,0:T(8,128)(2,1)S(1)} %bitcast.111, f32[2,256]{1,0:T(2,128)S(1)} %get-tuple-element.39, f32[2,256]{1,0:T(2,128)S(1)} %get-tuple-element.40, f32[2,256]{1,0:T(2,128)S(1)} %get-tuple-element.35, f32[2,256]{1,0:T(2,128)S(1)} %get-tuple-element.36, f32[2,256]{1,0:T(2,128)S(1)} %get-tuple-element.37, ...), kind=kLoop, calls=%fused_computation.18 | loop fusion | flops 20971520 | bytes 6305792 | tf_op jit(solution)/shard_map/add | solution.py:13
  66.4 48.0 %fusion.40 = f32[8,272,256]{2,0,1:T(8,128)S(1)} fusion(pred[8,272]{0,1:T(8,128)(4,1)S(1)} %copy-done.23, bf16[128,1,256]{2,0,1:T(8,128)(2,1)S(1)} %bitcast.130, bf16[8,399,256]{2,0,1:T(8,128)(2,1)S(1)} %fusion.67), kind=kOutput, calls=%fused_computation.67 | convolution fusion | flops 143163392 | bytes 3930240 | tf_op jit(solution)/shard_map/conv_general_dilated | solution.py:46
  116.1 26.6 %fusion.20 = f32[1,128,256]{2,0,1:T(1,128)S(1)} fusion(bf16[1,2175,256]{2,1,0:T(8,128)(2,1)S(1)} %pad_bitcast_fusion, bf16[2048,1,256]{2,0,1:T(8,128)(2,1)S(1)} %fusion.28), kind=kOutput, calls=%fused_computation.37 | convolution fusion | flops 134217728 | bytes 2293248 | tf_op jit(solution)/shard_map/conv_general_dilated | solution.py:46
  142.9 22.8 %collective-permute-start = (f32[129,256]{1,0:T(8,128)S(1)}, f32[129,256]{1,0:T(8,128)S(1)}, u32[]{:S(2)}, u32[]{:S(2)}) collective-permute-start(f32[129,256]{1,0:T(8,128)S(1)} %pad_maximum_fusion.1), channel_id=1, source_target_pairs={{0,16},{16,0},{32,48},{48,32},{64,80},{80,64},{96,112},{112,96},{1... | collective-permute-start | bytes 396296 | tf_op jit(solution)/shard_map/ppermute | solution.py:102
  165.8 13.8 %fusion.51 = f32[1,512,256]{2,0,1:T(1,128)S(1)} fusion(bf16[1,639,256]{2,1,0:T(8,128)(2,1)S(1)} %get-tuple-element.30, bf16[128,1,256]{2,0,1:T(8,128)(2,1)S(1)} %bitcast.126), kind=kOutput, calls=%fused_computation.78 | convolution fusion | flops 33554432 | bytes 916992 | tf_op jit(solution)/shard_map/conv_general_dilated | solution.py:46
  179.7 7.0 %collective-permute-start.1 = (f32[129,256]{1,0:T(8,128)S(1)}, f32[129,256]{1,0:T(8,128)S(1)}, u32[]{:S(2)}, u32[]{:S(2)}) collective-permute-start(f32[129,256]{1,0:T(8,128)S(1)} %add.97), channel_id=1, source_target_pairs={{0,32},{16,48},{32,0},{48,16},{64,96},{80,112},{96,64},{112,80},{1... | collective-permute-start | bytes 396296 | tf_op jit(solution)/shard_map/ppermute | solution.py:102
  186.7 13.3 %fusion.49 = f32[1,512,256]{2,0,1:T(1,128)S(1)} fusion(bf16[1,639,256]{2,1,0:T(8,128)(2,1)S(1)} %bitcast.125, bf16[128,1,256]{2,0,1:T(8,128)(2,1)S(1)} %bitcast.127), kind=kOutput, calls=%fused_computation.76 | convolution fusion | flops 33554432 | bytes 916992 | tf_op jit(solution)/shard_map/conv_general_dilated | solution.py:46
  200.2 2.4 collective-permute-start.2
  202.5 13.5 %fusion.47 = f32[1,512,256]{2,0,1:T(1,128)S(1)} fusion(bf16[1,639,256]{2,1,0:T(8,128)(2,1)S(1)} %bitcast.124, bf16[128,1,256]{2,0,1:T(8,128)(2,1)S(1)} %bitcast.128), kind=kOutput, calls=%fused_computation.74 | convolution fusion | flops 33554432 | bytes 916992 | tf_op jit(solution)/shard_map/conv_general_dilated | solution.py:46
  216.1 13.3 %fusion.45 = f32[1,512,256]{2,0,1:T(1,128)S(1)} fusion(bf16[1,639,256]{2,1,0:T(8,128)(2,1)S(1)} %bitcast.123, bf16[128,1,256]{2,0,1:T(8,128)(2,1)S(1)} %bitcast.129), kind=kOutput, calls=%fused_computation.72 | convolution fusion | flops 33554432 | bytes 916992 | tf_op jit(solution)/shard_map/conv_general_dilated | solution.py:46
  231.0 3.7 %fusion.12 = bf16[2,2048,256]{2,1,0:T(8,128)(2,1)S(1)} fusion(bf16[2,2048,256]{2,1,0:T(8,128)(2,1)S(1)} %pad_maximum_fusion, f32[2,256]{1,0:T(2,128)S(1)} %copy-done.18, f32[2,256]{1,0:T(2,128)S(1)} %copy-done.20, f32[2,256]{1,0:T(2,128)S(1)} %copy-done.10, f32[2,256]{1,0:T(2,128)S(1)} %copy-done.12, f32[2,256]{1,0:T(2,128)S(1)} %copy-done.14, ...), kind=kLoop, calls=%fused_computation.25 | loop fusion | flops 22020096 | bytes 4208640 | tf_op jit(solution)/shard_map/convert_element_type | solution.py:118
  234.7 14.2 %copy.69 = bf16[2,2048,256]{2,0,1:T(2,128)(2,1)} copy(bf16[2,2048,256]{2,1,0:T(8,128)(2,1)S(1)} %fusion.12) | data formatting | bytes 4194304 | tf_op jit(solution)/shard_map/convert_element_type | solution.py:118
  248.9 11.2 %all-to-all-start.2 = ((bf16[2,2048,256]{2,0,1:T(2,128)(2,1)}), bf16[2,2048,256]{2,0,1:T(2,128)(2,1)}, u32[]{:S(2)}, u32[]{:S(2)}) async-start(bf16[2,2048,256]{2,0,1:T(2,128)(2,1)} %copy.69), calls=%async_computation.2 | async-start | bytes 4194304 | tf_op jit(solution)/shard_map/all_to_all | solution.py:119
  260.1 4.6 %collective-permute-start.8 = (f32[129,256]{1,0:T(8,128)S(1)}, f32[129,256]{1,0:T(8,128)S(1)}, u32[]{:S(2)}, u32[]{:S(2)}) collective-permute-start(f32[129,256]{1,0:T(8,128)S(1)} %add.99), channel_id=1, source_target_pairs={{0,128},{16,144},{32,160},{48,176},{64,192},{80,208},{96,224},{112... | collective-permute-start | bytes 396296 | tf_op jit(solution)/shard_map/ppermute | solution.py:109
  266.6 3.6 %fusion.18 = (f32[2,256]{1,0:T(2,128)S(1)}, f32[2,256]{1,0:T(2,128)S(1)}, f32[2,256]{1,0:T(2,128)S(1)}, f32[2,256]{1,0:T(2,128)S(1)}, f32[2,256]{1,0:T(2,128)S(1)}, /*index=5*/f32[2,256]{1,0:T(2,128)S(1)}) fusion(bf16[2,2048,256]{2,1,0:T(8,128)(2,1)S(1)} %bitcast.112, bf16[1,2048,256]{2,1,0:T(8,128)(2,1)S(1)} %bitcast.120, bf16[1,2048,256]{2,1,0:T(8,128)(2,1)S(1)} %bitcast.117), kind=kLoop, calls=%fused_computation.31 | loop fusion | flops 23065600 | bytes 4206592 | tf_op jit(solution)/shard_map/reduce_sum | solution.py:37
  270.3 3.9 %collective-permute-start.3 = (f32[2,7,256]{2,0,1:T(2,128)S(1)}, f32[2,7,256]{2,0,1:T(2,128)S(1)}, u32[]{:S(2)}, u32[]{:S(2)}) collective-permute-start(f32[2,7,256]{2,0,1:T(2,128)S(1)} %constant_dynamic-update-slice_fusion), channel_id=1, source_target_pairs={{0,16},{16,0},{32,48},{48,32},{64,80},{80,64},{96,112},{112,96},{1... | collective-permute-start | bytes 43016 | tf_op jit(solution)/shard_map/ppermute | solution.py:62
  274.2 36.3 %collective-permute-done.3 = f32[2,7,256]{2,0,1:T(2,128)S(1)} collective-permute-done((f32[2,7,256]{2,0,1:T(2,128)S(1)}, f32[2,7,256]{2,0,1:T(2,128)S(1)}, u32[]{:S(2)}, u32[]{:S(2)}) %collective-permute-start.3) | collective-permute-done | bytes 14368 | tf_op jit(solution)/shard_map/ppermute | solution.py:62
  312.5 4.6 %collective-permute-done.4 = f32[2,7,256]{2,0,1:T(2,128)S(1)} collective-permute-done((f32[2,7,256]{2,0,1:T(2,128)S(1)}, f32[2,7,256]{2,0,1:T(2,128)S(1)}, u32[]{:S(2)}, u32[]{:S(2)}) %collective-permute-start.4) | collective-permute-done | bytes 14368 | tf_op jit(solution)/shard_map/ppermute | solution.py:62
  317.1 3.5 collective-permute-start.5
  320.6 2.1 collective-permute-done.5
  322.7 4.5 %collective-permute-start.6 = (f32[2,7,256]{2,0,1:T(2,128)S(1)}, f32[2,7,256]{2,0,1:T(2,128)S(1)}, u32[]{:S(2)}, u32[]{:S(2)}) collective-permute-start(f32[2,7,256]{2,0,1:T(2,128)S(1)} %add.109), channel_id=1, source_target_pairs={{0,128},{16,144},{32,160},{48,176},{64,192},{80,208},{96,224},{112... | collective-permute-start | bytes 43016 | tf_op jit(solution)/shard_map/ppermute | solution.py:62
  329.2 7.7 %collective-permute-start.7 = (f32[2,7,256]{2,0,1:T(2,128)S(1)}, f32[2,7,256]{2,0,1:T(2,128)S(1)}, u32[]{:S(2)}, u32[]{:S(2)}) collective-permute-start(f32[2,7,256]{2,0,1:T(2,128)S(1)} %add.110), channel_id=1, source_target_pairs={{0,256},{16,272},{32,288},{48,304},{64,320},{80,336},{96,352},{112... | collective-permute-start | bytes 43016 | tf_op jit(solution)/shard_map/ppermute | solution.py:62
  337.0 2.0 collective-permute-start.9
  339.7 9.7 %collective-permute-done.9 = f32[129,256]{1,0:T(8,128)S(1)} collective-permute-done((f32[129,256]{1,0:T(8,128)S(1)}, f32[129,256]{1,0:T(8,128)S(1)}, u32[]{:S(2)}, u32[]{:S(2)}) %collective-permute-start.9) | collective-permute-done | bytes 132128 | tf_op jit(solution)/shard_map/ppermute | solution.py:109
  350.6 2.8 copy.70
  353.4 2.3 broadcast_in_dim.60
  (98 shorter events, 14.4 us)
Async XLA Ops:
  1.9 21.8 %all-to-all-start.1 = ((bf16[1,128,16]{1,0,2:T(2,128)(2,1)}), bf16[1,128,16]{1,0,2:T(2,128)(2,1)S(1)}, u32[]{:S(2)}, u32[]{:S(2)}) async-start(bf16[1,128,16]{1,0,2:T(2,128)(2,1)} %broadcast_in_dim.52), calls=%async_computation.1 | async-start | bytes 16384 | tf_op jit(solution)/shard_map/all_to_all | solution.py:80
  21.4 9.8 %copy-start.6 = (bf16[128,256]{1,0:T(8,128)(2,1)S(1)}, bf16[128,256]{1,0:T(8,128)(2,1)}, u32[]{:S(2)}) copy-start(bf16[128,256]{1,0:T(8,128)(2,1)} %param.8) | copy-start | bytes 196612
  23.7 7.5 %copy-start.21 = (f32[2,7,256]{2,0,1:T(2,128)S(1)}, f32[2,7,256]{2,0,1:T(2,128)}, u32[]{:S(2)}) copy-start(f32[2,7,256]{2,0,1:T(2,128)} %param.7) | copy-start | bytes 43012
  23.7 32.4 %all-to-all-start = ((bf16[2,128,4096]{1,0,2:T(2,128)(2,1)}), bf16[2,128,4096]{1,0,2:T(2,128)(2,1)}, u32[]{:S(2)}, u32[]{:S(2)}) async-start(bf16[2,128,4096]{1,0,2:T(2,128)(2,1)} %bitcast.1), calls=%async_computation | async-start | bytes 4194304 | tf_op jit(solution)/shard_map/all_to_all | solution.py:79
  31.3 29.6 %copy-start.7 = (f32[2,256]{1,0:T(2,128)}, f32[2,256]{1,0:T(2,128)S(1)}, u32[]{:S(2)}) copy-start(f32[2,256]{1,0:T(2,128)S(1)} %get-tuple-element.34) | copy-start | bytes 6148
  31.3 29.6 %copy-start.9 = (f32[2,256]{1,0:T(2,128)}, f32[2,256]{1,0:T(2,128)S(1)}, u32[]{:S(2)}) copy-start(f32[2,256]{1,0:T(2,128)S(1)} %get-tuple-element.35) | copy-start | bytes 6148
  31.3 29.6 %copy-start.11 = (f32[2,256]{1,0:T(2,128)}, f32[2,256]{1,0:T(2,128)S(1)}, u32[]{:S(2)}) copy-start(f32[2,256]{1,0:T(2,128)S(1)} %get-tuple-element.36) | copy-start | bytes 6148
  31.3 29.6 %copy-start.13 = (f32[2,256]{1,0:T(2,128)}, f32[2,256]{1,0:T(2,128)S(1)}, u32[]{:S(2)}) copy-start(f32[2,256]{1,0:T(2,128)S(1)} %get-tuple-element.37) | copy-start | bytes 6148
  31.3 29.6 %copy-start.15 = (f32[2,256]{1,0:T(2,128)}, f32[2,256]{1,0:T(2,128)S(1)}, u32[]{:S(2)}) copy-start(f32[2,256]{1,0:T(2,128)S(1)} %get-tuple-element.38) | copy-start | bytes 6148
  31.3 29.6 %copy-start.17 = (f32[2,256]{1,0:T(2,128)}, f32[2,256]{1,0:T(2,128)S(1)}, u32[]{:S(2)}) copy-start(f32[2,256]{1,0:T(2,128)S(1)} %get-tuple-element.39) | copy-start | bytes 6148
  31.3 29.6 %copy-start.19 = (f32[2,256]{1,0:T(2,128)}, f32[2,256]{1,0:T(2,128)S(1)}, u32[]{:S(2)}) copy-start(f32[2,256]{1,0:T(2,128)S(1)} %get-tuple-element.40) | copy-start | bytes 6148
  60.8 3.8 %copy-start.2 = (bf16[2,128,16,256]{3,1,2,0:T(8,128)(2,1)}, bf16[2,128,16,256]{3,1,2,0:T(8,128)(2,1)S(1)}, u32[]{:S(2)}) copy-start(bf16[2,128,16,256]{3,1,2,0:T(8,128)(2,1)S(1)} %copy.53) | copy-start | bytes 6291460
  64.6 51.0 %copy-start = (f32[2,2048,256]{2,1,0:T(8,128)}, f32[2,2048,256]{2,1,0:T(8,128)S(1)}, u32[]{:S(2)}) copy-start(f32[2,2048,256]{2,1,0:T(8,128)S(1)} %fusion.5) | copy-start | bytes 12582916
  65.6 0.8 copy-start.23
  114.4 0.7 copy-start.22
  142.9 36.7 %collective-permute-start = (f32[129,256]{1,0:T(8,128)S(1)}, f32[129,256]{1,0:T(8,128)S(1)}, u32[]{:S(2)}, u32[]{:S(2)}) collective-permute-start(f32[129,256]{1,0:T(8,128)S(1)} %pad_maximum_fusion.1), channel_id=1, source_target_pairs={{0,16},{16,0},{32,48},{48,32},{64,80},{80,64},{96,112},{112,96},{1... | collective-permute-start | bytes 396296 | tf_op jit(solution)/shard_map/ppermute | solution.py:102
  179.7 20.4 %collective-permute-start.1 = (f32[129,256]{1,0:T(8,128)S(1)}, f32[129,256]{1,0:T(8,128)S(1)}, u32[]{:S(2)}, u32[]{:S(2)}) collective-permute-start(f32[129,256]{1,0:T(8,128)S(1)} %add.97), channel_id=1, source_target_pairs={{0,32},{16,48},{32,0},{48,16},{64,96},{80,112},{96,64},{112,80},{1... | collective-permute-start | bytes 396296 | tf_op jit(solution)/shard_map/ppermute | solution.py:102
  200.2 15.9 %collective-permute-start.2 = (f32[129,256]{1,0:T(8,128)S(1)}, f32[129,256]{1,0:T(8,128)S(1)}, u32[]{:S(2)}, u32[]{:S(2)}) collective-permute-start(f32[129,256]{1,0:T(8,128)S(1)} %add.98), channel_id=1, source_target_pairs={{0,64},{16,80},{32,96},{48,112},{64,0},{80,16},{96,32},{112,48},{1... | collective-permute-start | bytes 396296 | tf_op jit(solution)/shard_map/ppermute | solution.py:102
  216.1 13.4 %copy-start.1 = (f32[2,2048,256]{2,1,0:T(8,128)S(1)}, f32[2,2048,256]{2,1,0:T(8,128)}, u32[]{:S(2)}) copy-start(f32[2,2048,256]{2,1,0:T(8,128)} %copy-done) | copy-start | bytes 12582916
  230.2 4.5 %copy-start.4 = (bf16[2048,256]{1,0:T(8,128)(2,1)}, bf16[2048,256]{1,0:T(8,128)(2,1)S(1)}, u32[]{:S(2)}) copy-start(bf16[2048,256]{1,0:T(8,128)(2,1)S(1)} %get-tuple-element.29) | copy-start | bytes 3145732
  230.2 0.8 copy-start.18
  230.2 0.8 copy-start.20
  248.9 15.8 %copy-start.3 = (bf16[2,128,16,256]{3,1,2,0:T(8,128)(2,1)S(1)}, bf16[2,128,16,256]{3,1,2,0:T(8,128)(2,1)}, u32[]{:S(2)}) copy-start(bf16[2,128,16,256]{3,1,2,0:T(8,128)(2,1)} %copy-done.2) | copy-start | bytes 6291460
  248.9 101.7 %all-to-all-start.2 = ((bf16[2,2048,256]{2,0,1:T(2,128)(2,1)}), bf16[2,2048,256]{2,0,1:T(2,128)(2,1)}, u32[]{:S(2)}, u32[]{:S(2)}) async-start(bf16[2,2048,256]{2,0,1:T(2,128)(2,1)} %copy.69), calls=%async_computation.2 | async-start | bytes 4194304 | tf_op jit(solution)/shard_map/all_to_all | solution.py:119
  260.1 6.5 %copy-start.5 = (bf16[2048,256]{1,0:T(8,128)(2,1)S(1)}, bf16[2048,256]{1,0:T(8,128)(2,1)}, u32[]{:S(2)}) copy-start(bf16[2048,256]{1,0:T(8,128)(2,1)} %copy-done.4) | copy-start | bytes 3145732
  260.1 76.9 %collective-permute-start.8 = (f32[129,256]{1,0:T(8,128)S(1)}, f32[129,256]{1,0:T(8,128)S(1)}, u32[]{:S(2)}, u32[]{:S(2)}) collective-permute-start(f32[129,256]{1,0:T(8,128)S(1)} %add.99), channel_id=1, source_target_pairs={{0,128},{16,144},{32,160},{48,176},{64,192},{80,208},{96,224},{112... | collective-permute-start | bytes 396296 | tf_op jit(solution)/shard_map/ppermute | solution.py:109
  270.3 40.3 %collective-permute-start.3 = (f32[2,7,256]{2,0,1:T(2,128)S(1)}, f32[2,7,256]{2,0,1:T(2,128)S(1)}, u32[]{:S(2)}, u32[]{:S(2)}) collective-permute-start(f32[2,7,256]{2,0,1:T(2,128)S(1)} %constant_dynamic-update-slice_fusion), channel_id=1, source_target_pairs={{0,16},{16,0},{32,48},{48,32},{64,80},{80,64},{96,112},{112,96},{1... | collective-permute-start | bytes 43016 | tf_op jit(solution)/shard_map/ppermute | solution.py:62
  310.6 6.5 %collective-permute-start.4 = (f32[2,7,256]{2,0,1:T(2,128)S(1)}, f32[2,7,256]{2,0,1:T(2,128)S(1)}, u32[]{:S(2)}, u32[]{:S(2)}) collective-permute-start(f32[2,7,256]{2,0,1:T(2,128)S(1)} %add.107), channel_id=1, source_target_pairs={{0,32},{16,48},{32,0},{48,16},{64,96},{80,112},{96,64},{112,80},{1... | collective-permute-start | bytes 43016 | tf_op jit(solution)/shard_map/ppermute | solution.py:62
  317.1 5.6 %collective-permute-start.5 = (f32[2,7,256]{2,0,1:T(2,128)S(1)}, f32[2,7,256]{2,0,1:T(2,128)S(1)}, u32[]{:S(2)}, u32[]{:S(2)}) collective-permute-start(f32[2,7,256]{2,0,1:T(2,128)S(1)} %add.108), channel_id=1, source_target_pairs={{0,64},{16,80},{32,96},{48,112},{64,0},{80,16},{96,32},{112,48},{1... | collective-permute-start | bytes 43016 | tf_op jit(solution)/shard_map/ppermute | solution.py:62
  322.7 6.5 %collective-permute-start.6 = (f32[2,7,256]{2,0,1:T(2,128)S(1)}, f32[2,7,256]{2,0,1:T(2,128)S(1)}, u32[]{:S(2)}, u32[]{:S(2)}) collective-permute-start(f32[2,7,256]{2,0,1:T(2,128)S(1)} %add.109), channel_id=1, source_target_pairs={{0,128},{16,144},{32,160},{48,176},{64,192},{80,208},{96,224},{112... | collective-permute-start | bytes 43016 | tf_op jit(solution)/shard_map/ppermute | solution.py:62
  329.2 9.8 %collective-permute-start.7 = (f32[2,7,256]{2,0,1:T(2,128)S(1)}, f32[2,7,256]{2,0,1:T(2,128)S(1)}, u32[]{:S(2)}, u32[]{:S(2)}) collective-permute-start(f32[2,7,256]{2,0,1:T(2,128)S(1)} %add.110), channel_id=1, source_target_pairs={{0,256},{16,272},{32,288},{48,304},{64,320},{80,336},{96,352},{112... | collective-permute-start | bytes 43016 | tf_op jit(solution)/shard_map/ppermute | solution.py:62
  337.0 12.3 %collective-permute-start.9 = (f32[129,256]{1,0:T(8,128)S(1)}, f32[129,256]{1,0:T(8,128)S(1)}, u32[]{:S(2)}, u32[]{:S(2)}) collective-permute-start(f32[129,256]{1,0:T(8,128)S(1)} %add.112), channel_id=1, source_target_pairs={{0,256},{16,272},{32,288},{48,304},{64,320},{80,336},{96,352},{112... | collective-permute-start | bytes 396296 | tf_op jit(solution)/shard_map/ppermute | solution.py:109
  (5 other events, 3.5 us)

commit v5 on v1

--- a/solution.py
+++ b/solution.py
@@ -74,12 +74,15 @@
     loss_weight = jnp.where((token_ids[0] >= 97) & (token_ids[0] <= 122), 0.1, 1.0).astype(
         jnp.bfloat16
     )
-    weight_rows = jnp.broadcast_to(loss_weight[None, :, None], (1, length, shards))
-    all_inputs, all_weight = (
-        lax.all_to_all(inputs, "ctx", split_axis=2, concat_axis=1, tiled=True),
-        lax.all_to_all(weight_rows, "ctx", split_axis=2, concat_axis=1, tiled=True),
-    )
-    weight_seq = all_weight[0, :, 0].astype(jnp.float32)
+    extra = 8
+    width = inputs.shape[2] // shards
+    weight_row = jnp.tile(jnp.pad(loss_weight, (0, width - length)), shards)
+    extra_rows = jnp.zeros((2, extra, inputs.shape[2]), inputs.dtype).at[0, 0].set(weight_row)
+    joined = jnp.concatenate([inputs, extra_rows], axis=1)
+    received = lax.all_to_all(joined, "ctx", split_axis=2, concat_axis=1, tiled=True)
+    received = received.reshape(2, shards, length + extra, width)
+    all_inputs = received[:, :, :length].reshape(2, shards * length, width)
+    weight_seq = received[0, :, length, :length].reshape(-1).astype(jnp.float32)
     padded_inputs = jnp.pad(all_inputs, ((0, 0), (short_len - 1, 0), (0, 0)))
     filtered = short_forward(padded_inputs, short_filters)
     product = (filtered[0] * filtered[1]).astype(jnp.bfloat16)

time: 328 us -> 385 us (1.17)
  waiting for transfers between devices: 70.2 us -> 96.3 us
  other arithmetic: 18.6 us -> 29.6 us
  starting transfers between devices: 74.5 us -> 84.8 us
  local copies, waits for them, and re-layouts: 38 us -> 46.1 us
    ppermute x5, starting transfers between devices: 29.3 us -> 66 us  [butterfly_sum(): value = value + lax.ppermute(value, axis, perm)]
    all_to_all x2 -> x1, waiting for transfers between devices: 33.1 us -> 60.9 us  [local(): lax.all_to_all(joined, 'ctx', split_axis=2, concat_axis=1, tiled=True)]
    all_to_all x1, starting transfers between devices: 23.9 us -> 5.43 us  [local(): lax.all_to_all(grad_channels, 'ctx', split_axis=1, concat_axis=2, tiled=T...]
    concatenate x0 -> x1, other arithmetic: none -> 8.65 us  [local(): joined = jnp.concatenate([inputs, extra_rows], axis=1)]
    all_to_all x2 -> x1, starting transfers between devices: 21.2 us -> 13.4 us  [local(): lax.all_to_all(joined, 'ctx', split_axis=2, concat_axis=1, tiled=True)]
    all_to_all x1, local copies, waits for them, and re-layouts: 4.72 us -> 10.7 us  [local(): lax.all_to_all(joined, 'ctx', split_axis=2, concat_axis=1, tiled=True)]
    unnamed x19 -> x17, local copies, waits for them, and re-layouts: 9.91 us -> 8.81 us
  transfers between devices with their start and end apart: 8 -> 7, of which waited for: 7 -> 6; matrix products, arithmetic and copies ran while one was open for 13% -> 10% of each run, Pallas kernels for 0% -> 0%
where the time goes in v5:
time: 385 us; the launch traced here: 382 us
  matrix products  124 us (32%)
  waiting for transfers between devices  96.3 us (25%)
  starting transfers between devices  84.8 us (22%)
  local copies, waits for them, and re-layouts  46.1 us (12%)
  other arithmetic  29.6 us (8%)
    conv_general_dilated x3, matrix products, depthwise(): lax.conv_general_dilated(extended[None], kernel[:, None, :], (1,), 'VALID...  124 us
    ppermute x5, starting transfers between devices, butterfly_sum(): value = value + lax.ppermute(value, axis, perm)  66 us
    all_to_all x1, waiting for transfers between devices, local(): lax.all_to_all(joined, 'ctx', split_axis=2, concat_axis=1, tiled=True)  60.9 us
    ppermute x5, waiting for transfers between devices, butterfly_sum(): value = value + lax.ppermute(value, axis, perm)  35.4 us
    convert_element_type x1, local copies, waits for them, and re-layouts, local(): short_backward(padded_grads, short_filters).astype(jnp.bfloat16)  14.2 us
    all_to_all x1, starting transfers between devices, local(): lax.all_to_all(joined, 'ctx', split_axis=2, concat_axis=1, tiled=True)  13.4 us
    all_to_all x1, local copies, waits for them, and re-layouts, local(): lax.all_to_all(joined, 'ctx', split_axis=2, concat_axis=1, tiled=True)  10.7 us
    unnamed x17, local copies, waits for them, and re-layouts  8.81 us
  transfers between devices with their start and end apart: 7, of which 6 were waited for; matrix products, arithmetic and copies ran while one was open for 10% of the time, Pallas kernels for 0%

profile of v5, /device:TPU:6, one launch (start us, length us, event | category | flops | bytes accessed | tf_op | source)
XLA Modules:
  0.0 381.9 jit_solution(12125668680388147912)
XLA Ops:
  1.3 2.3 reshape.218
  3.6 6.2 %copy.43 = bf16[2,1,128,4096]{2,0,3,1:T(2,128)(2,1)} copy(bf16[2,1,128,4096]{3,2,1,0:T(8,128)(2,1)} %param.7) | data formatting | bytes 4194304 | tf_op args[0]
  9.8 8.6 %fusion.19 = bf16[2,136,4096]{1,0,2:T(2,128)(2,1)} fusion(bf16[1,1,4096]{1,0,2:T(2,128)(2,1)S(1)} %reshape.218, bf16[2,128,4096]{1,0,2:T(2,128)(2,1)} %bitcast.88), kind=kLoop, calls=%fused_computation.33 | loop fusion | flops 6684672 | bytes 4333568 | tf_op jit(solution)/shard_map/concatenate | solution.py:81
  18.4 13.4 %all-to-all-start = ((bf16[2,136,4096]{1,0,2:T(2,128)(2,1)}), bf16[2,136,4096]{1,0,2:T(2,128)(2,1)}, u32[]{:S(2)}, u32[]{:S(2)}) async-start(bf16[2,136,4096]{1,0,2:T(2,128)(2,1)} %fusion.19), calls=%async_computation | async-start | bytes 8388608 | tf_op jit(solution)/shard_map/all_to_all | solution.py:82
  31.9 60.9 %all-to-all-done = bf16[2,136,4096]{1,0,2:T(2,128)(2,1)} async-done(((bf16[2,136,4096]{1,0,2:T(2,128)(2,1)}), bf16[2,136,4096]{1,0,2:T(2,128)(2,1)}, u32[]{:S(2)}, u32[]{:S(2)}) %all-to-all-start) | async-done | bytes 2228256 | tf_op jit(solution)/shard_map/all_to_all | solution.py:82
  92.8 10.7 %copy.45 = bf16[2,136,16,256]{3,1,2,0:T(8,128)(2,1)} copy(bf16[2,136,16,256]{1,0,3,2:T(2,128)(2,1)} %bitcast.3) | data formatting | bytes 4456448 | tf_op jit(solution)/shard_map/all_to_all | solution.py:82
  103.5 0.8 slice_convert_fusion
  104.3 1.7 slice.146
  106.0 3.7 fusion.5
  112.0 47.9 %fusion.53 = f32[8,272,256]{2,0,1:T(8,128)S(1)} fusion(pred[8,272]{0,1:T(8,128)(4,1)S(1)} %copy-done.6, bf16[128,1,256]{2,0,1:T(8,128)(2,1)S(1)} %bitcast.96, bf16[8,399,256]{2,0,1:T(8,128)(2,1)S(1)} %fusion.77), kind=kOutput, calls=%fused_computation.78 | convolution fusion | flops 143163392 | bytes 3930240 | tf_op jit(solution)/shard_map/conv_general_dilated | solution.py:46
  160.7 1.4 fusion.34
  163.4 48.0 %fusion.50 = f32[8,272,256]{2,0,1:T(8,128)S(1)} fusion(pred[8,272]{0,1:T(8,128)(4,1)S(1)} %copy-done.6, bf16[128,1,256]{2,0,1:T(8,128)(2,1)S(1)} %bitcast.95, bf16[8,399,256]{2,0,1:T(8,128)(2,1)S(1)} %fusion.75), kind=kOutput, calls=%fused_computation.77 | convolution fusion | flops 143163392 | bytes 3930240 | tf_op jit(solution)/shard_map/conv_general_dilated | solution.py:46
  212.1 0.8 multiply_convert_fusion.1
  213.2 1.0 copy-done
  214.4 3.7 fusion.12
  218.1 14.2 %copy.54 = bf16[2,2048,256]{2,0,1:T(2,128)(2,1)} copy(bf16[2,2048,256]{2,1,0:T(8,128)(2,1)S(1)} %fusion.12) | data formatting | bytes 4194304 | tf_op jit(solution)/shard_map/convert_element_type | solution.py:98
  232.3 5.4 %all-to-all-start.1 = ((bf16[2,2048,256]{2,0,1:T(2,128)(2,1)}), bf16[2,2048,256]{2,0,1:T(2,128)(2,1)}, u32[]{:S(2)}, u32[]{:S(2)}) async-start(bf16[2,2048,256]{2,0,1:T(2,128)(2,1)} %copy.54), calls=%async_computation.1 | async-start | bytes 4194304 | tf_op jit(solution)/shard_map/all_to_all | solution.py:99
  237.8 28.2 %fusion.22 = f32[1,128,256]{2,0,1:T(1,128)S(1)} fusion(bf16[1,2175,256]{2,1,0:T(8,128)(2,1)} %copy-done.2, bf16[2048,1,256]{2,0,1:T(8,128)(2,1)} %fusion.34), kind=kOutput, calls=%fused_computation.42 | convolution fusion | flops 134217728 | bytes 2293248 | tf_op jit(solution)/shard_map/conv_general_dilated | solution.py:46
  266.1 4.9 %fusion.18 = (f32[2,256]{1,0:T(2,128)S(1)}, f32[2,256]{1,0:T(2,128)S(1)}, f32[2,256]{1,0:T(2,128)S(1)}, f32[2,256]{1,0:T(2,128)S(1)}, f32[2,256]{1,0:T(2,128)S(1)}, /*index=5*/f32[2,256]{1,0:T(2,128)S(1)}) fusion(bf16[2,2048,256]{2,1,0:T(8,128)(2,1)S(1)} %bitcast.83, bf16[1,2048,256]{2,1,0:T(8,128)(2,1)} %copy-done, ...), kind=kLoop, calls=%fused_computation.32 | loop fusion | flops 23065600 | bytes 4206592 | tf_op jit(solution)/shard_map/reduce_sum | solution.py:37
  271.1 2.2 multiply_reduce_fusion
  273.3 43.0 %collective-permute-start = (f32[143,256]{1,0:T(8,128)S(1)}, f32[143,256]{1,0:T(8,128)S(1)}, u32[]{:S(2)}, u32[]{:S(2)}) collective-permute-start(f32[143,256]{1,0:T(8,128)S(1)} %pad_maximum_fusion.1), channel_id=1, source_target_pairs={{0,16},{16,0},{32,48},{48,32},{64,80},{80,64},{96,112},{112,96},{1... | collective-permute-start | bytes 439304 | tf_op jit(solution)/shard_map/ppermute | solution.py:62
  316.4 11.8 %collective-permute-done = f32[143,256]{1,0:T(8,128)S(1)} collective-permute-done((f32[143,256]{1,0:T(8,128)S(1)}, f32[143,256]{1,0:T(8,128)S(1)}, u32[]{:S(2)}, u32[]{:S(2)}) %collective-permute-start) | collective-permute-done | bytes 146464 | tf_op jit(solution)/shard_map/ppermute | solution.py:62
  328.2 7.3 %collective-permute-start.1 = (f32[143,256]{1,0:T(8,128)S(1)}, f32[143,256]{1,0:T(8,128)S(1)}, u32[]{:S(2)}, u32[]{:S(2)}) collective-permute-start(f32[143,256]{1,0:T(8,128)S(1)} %fusion.70), channel_id=1, source_target_pairs={{0,32},{16,48},{32,0},{48,16},{64,96},{80,112},{96,64},{112,80},{1... | collective-permute-start | bytes 439304 | tf_op jit(solution)/shard_map/ppermute | solution.py:62
  335.5 6.2 %collective-permute-done.1 = f32[143,256]{1,0:T(8,128)S(1)} collective-permute-done((f32[143,256]{1,0:T(8,128)S(1)}, f32[143,256]{1,0:T(8,128)S(1)}, u32[]{:S(2)}, u32[]{:S(2)}) %collective-permute-start.1) | collective-permute-done | bytes 146464 | tf_op jit(solution)/shard_map/ppermute | solution.py:62
  341.7 3.5 collective-permute-start.2
  345.2 4.2 %collective-permute-done.2 = f32[143,256]{1,0:T(8,128)S(1)} collective-permute-done((f32[143,256]{1,0:T(8,128)S(1)}, f32[143,256]{1,0:T(8,128)S(1)}, u32[]{:S(2)}, u32[]{:S(2)}) %collective-permute-start.2) | collective-permute-done | bytes 146464 | tf_op jit(solution)/shard_map/ppermute | solution.py:62
  349.4 4.5 %collective-permute-start.3 = (f32[143,256]{1,0:T(8,128)S(1)}, f32[143,256]{1,0:T(8,128)S(1)}, u32[]{:S(2)}, u32[]{:S(2)}) collective-permute-start(f32[143,256]{1,0:T(8,128)S(1)} %add.104), channel_id=1, source_target_pairs={{0,128},{16,144},{32,160},{48,176},{64,192},{80,208},{96,224},{112... | collective-permute-start | bytes 439304 | tf_op jit(solution)/shard_map/ppermute | solution.py:62
  353.9 6.4 %collective-permute-done.3 = f32[143,256]{1,0:T(8,128)S(1)} collective-permute-done((f32[143,256]{1,0:T(8,128)S(1)}, f32[143,256]{1,0:T(8,128)S(1)}, u32[]{:S(2)}, u32[]{:S(2)}) %collective-permute-start.3) | collective-permute-done | bytes 146464 | tf_op jit(solution)/shard_map/ppermute | solution.py:62
  360.3 7.7 %collective-permute-start.4 = (f32[143,256]{1,0:T(8,128)S(1)}, f32[143,256]{1,0:T(8,128)S(1)}, u32[]{:S(2)}, u32[]{:S(2)}) collective-permute-start(f32[143,256]{1,0:T(8,128)S(1)} %add.105), channel_id=1, source_target_pairs={{0,256},{16,272},{32,288},{48,304},{64,320},{80,336},{96,352},{112... | collective-permute-start | bytes 439304 | tf_op jit(solution)/shard_map/ppermute | solution.py:62
  368.1 6.9 %collective-permute-done.4 = f32[143,256]{1,0:T(8,128)S(1)} collective-permute-done((f32[143,256]{1,0:T(8,128)S(1)}, f32[143,256]{1,0:T(8,128)S(1)}, u32[]{:S(2)}, u32[]{:S(2)}) %collective-permute-start.4) | collective-permute-done | bytes 146464 | tf_op jit(solution)/shard_map/ppermute | solution.py:62
  376.8 2.8 copy.55
  379.6 2.3 broadcast_in_dim.38
  (57 shorter events, 8.5 us)
Async XLA Ops:
  18.4 13.4 %copy-start.3 = (bf16[128,256]{1,0:T(8,128)(2,1)S(1)}, bf16[128,256]{1,0:T(8,128)(2,1)}, u32[]{:S(2)}) copy-start(bf16[128,256]{1,0:T(8,128)(2,1)} %param.10) | copy-start | bytes 196612
  18.4 13.5 %copy-start.5 = (f32[2,7,256]{2,0,1:T(2,128)S(1)}, f32[2,7,256]{2,0,1:T(2,128)}, u32[]{:S(2)}) copy-start(f32[2,7,256]{2,0,1:T(2,128)} %param.9) | copy-start | bytes 43012
  18.4 74.4 %all-to-all-start = ((bf16[2,136,4096]{1,0,2:T(2,128)(2,1)}), bf16[2,136,4096]{1,0,2:T(2,128)(2,1)}, u32[]{:S(2)}, u32[]{:S(2)}) async-start(bf16[2,136,4096]{1,0,2:T(2,128)(2,1)} %fusion.19), calls=%async_computation | async-start | bytes 8388608 | tf_op jit(solution)/shard_map/all_to_all | solution.py:82
  110.2 1.0 copy-start.2
  111.2 0.8 copy-start.6
  159.9 0.7 copy-start.4
  213.2 1.0 copy-start
  232.3 144.5 %all-to-all-start.1 = ((bf16[2,2048,256]{2,0,1:T(2,128)(2,1)}), bf16[2,2048,256]{2,0,1:T(2,128)(2,1)}, u32[]{:S(2)}, u32[]{:S(2)}) async-start(bf16[2,2048,256]{2,0,1:T(2,128)(2,1)} %copy.54), calls=%async_computation.1 | async-start | bytes 4194304 | tf_op jit(solution)/shard_map/all_to_all | solution.py:99
  266.1 4.9 %copy-start.1 = (bf16[1,2048,256]{2,1,0:T(8,128)(2,1)S(1)}, bf16[1,2048,256]{2,1,0:T(8,128)(2,1)}, u32[]{:S(2)}) copy-start(bf16[1,2048,256]{2,1,0:T(8,128)(2,1)} %copy-done) | copy-start | bytes 3145732
  273.3 54.8 %collective-permute-start = (f32[143,256]{1,0:T(8,128)S(1)}, f32[143,256]{1,0:T(8,128)S(1)}, u32[]{:S(2)}, u32[]{:S(2)}) collective-permute-start(f32[143,256]{1,0:T(8,128)S(1)} %pad_maximum_fusion.1), channel_id=1, source_target_pairs={{0,16},{16,0},{32,48},{48,32},{64,80},{80,64},{96,112},{112,96},{1... | collective-permute-start | bytes 439304 | tf_op jit(solution)/shard_map/ppermute | solution.py:62
  328.2 13.5 %collective-permute-start.1 = (f32[143,256]{1,0:T(8,128)S(1)}, f32[143,256]{1,0:T(8,128)S(1)}, u32[]{:S(2)}, u32[]{:S(2)}) collective-permute-start(f32[143,256]{1,0:T(8,128)S(1)} %fusion.70), channel_id=1, source_target_pairs={{0,32},{16,48},{32,0},{48,16},{64,96},{80,112},{96,64},{112,80},{1... | collective-permute-start | bytes 439304 | tf_op jit(solution)/shard_map/ppermute | solution.py:62
  341.7 7.7 %collective-permute-start.2 = (f32[143,256]{1,0:T(8,128)S(1)}, f32[143,256]{1,0:T(8,128)S(1)}, u32[]{:S(2)}, u32[]{:S(2)}) collective-permute-start(f32[143,256]{1,0:T(8,128)S(1)} %add.103), channel_id=1, source_target_pairs={{0,64},{16,80},{32,96},{48,112},{64,0},{80,16},{96,32},{112,48},{1... | collective-permute-start | bytes 439304 | tf_op jit(solution)/shard_map/ppermute | solution.py:62
  349.4 10.9 %collective-permute-start.3 = (f32[143,256]{1,0:T(8,128)S(1)}, f32[143,256]{1,0:T(8,128)S(1)}, u32[]{:S(2)}, u32[]{:S(2)}) collective-permute-start(f32[143,256]{1,0:T(8,128)S(1)} %add.104), channel_id=1, source_target_pairs={{0,128},{16,144},{32,160},{48,176},{64,192},{80,208},{96,224},{112... | collective-permute-start | bytes 439304 | tf_op jit(solution)/shard_map/ppermute | solution.py:62
  360.3 14.6 %collective-permute-start.4 = (f32[143,256]{1,0:T(8,128)S(1)}, f32[143,256]{1,0:T(8,128)S(1)}, u32[]{:S(2)}, u32[]{:S(2)}) collective-permute-start(f32[143,256]{1,0:T(8,128)S(1)} %add.105), channel_id=1, source_target_pairs={{0,256},{16,272},{32,288},{48,304},{64,320},{80,336},{96,352},{112... | collective-permute-start | bytes 439304 | tf_op jit(solution)/shard_map/ppermute | solution.py:62

commit v6 on v1

--- a/solution.py
+++ b/solution.py
@@ -43,6 +43,15 @@
 
 
 def depthwise(extended, kernel):
+    lanes = 128
+    if extended.shape[1] > lanes and extended.shape[1] % lanes == 0:
+        return jnp.concatenate(
+            [
+                depthwise(extended[:, k : k + lanes], kernel[:, k : k + lanes])
+                for k in range(0, extended.shape[1], lanes)
+            ],
+            axis=1,
+        )
     result = lax.conv_general_dilated(
         extended[None],
         kernel[:, None, :],

time: 328 us -> 296 us (0.902)
  the two profiles are of different devices: /device:TPU:6 before, /device:TPU:2 now
where the time goes in v6:
time: 296 us; the launch traced here: 292 us
  waiting for transfers between devices  84.9 us (29%)
  starting transfers between devices  75.5 us (26%)
  matrix products  74 us (25%)
  local copies, waits for them, and re-layouts  38.9 us (13%)
  other arithmetic  17.6 us (6%)
    conv_general_dilated x6, matrix products, depthwise(): lax.conv_general_dilated(extended[None], kernel[:, None, :], (1,), 'VALID...  74 us
    ppermute x5, waiting for transfers between devices, butterfly_sum(): value = value + lax.ppermute(value, axis, perm)  57.7 us
    all_to_all x1, starting transfers between devices, local(): lax.all_to_all(grad_channels, 'ctx', split_axis=1, concat_axis=2, tiled=T...  30.9 us
    all_to_all x1, waiting for transfers between devices, local(): lax.all_to_all(inputs, 'ctx', split_axis=2, concat_axis=1, tiled=True)  24.8 us
    ppermute x5, starting transfers between devices, butterfly_sum(): value = value + lax.ppermute(value, axis, perm)  24 us
    convert_element_type x1, local copies, waits for them, and re-layouts, local(): short_backward(padded_grads, short_filters).astype(jnp.bfloat16)  14 us
    all_to_all x1, starting transfers between devices, local(): lax.all_to_all(weight_rows, 'ctx', split_axis=2, concat_axis=1, tiled=True)  13.3 us
    unnamed x22, local copies, waits for them, and re-layouts  9.59 us
  transfers between devices with their start and end apart: 8, of which 7 were waited for; matrix products, arithmetic and copies ran while one was open for 9% of the time, Pallas kernels for 0%

profile of v6, /device:TPU:2, one launch (start us, length us, event | category | flops | bytes accessed | tf_op | source)
XLA Modules:
  0.0 292.4 jit_solution(11183730761404841240)
XLA Ops:
  1.9 13.3 %all-to-all-start = ((bf16[1,128,16]{1,0,2:T(2,128)(2,1)}), bf16[1,128,16]{1,0,2:T(2,128)(2,1)S(1)}, u32[]{:S(2)}, u32[]{:S(2)}) async-start(bf16[1,128,16]{1,0,2:T(2,128)(2,1)} %broadcast_in_dim.57), calls=%async_computation | async-start | bytes 16384 | tf_op jit(solution)/shard_map/all_to_all | solution.py:89
  15.2 6.2 %copy.107 = bf16[2,1,128,4096]{2,0,3,1:T(2,128)(2,1)} copy(bf16[2,1,128,4096]{3,2,1,0:T(8,128)(2,1)} %param.5) | data formatting | bytes 4194304 | tf_op args[0]
  21.4 2.4 all-to-all-done
  23.7 7.4 %all-to-all-start.1 = ((bf16[2,128,4096]{1,0,2:T(2,128)(2,1)}), bf16[2,128,4096]{1,0,2:T(2,128)(2,1)S(1)}, u32[]{:S(2)}, u32[]{:S(2)}) async-start(bf16[2,128,4096]{1,0,2:T(2,128)(2,1)} %bitcast.5), calls=%async_computation.1 | async-start | bytes 4194304 | tf_op jit(solution)/shard_map/all_to_all | solution.py:88
  31.3 24.8 %all-to-all-done.1 = bf16[2,128,4096]{1,0,2:T(2,128)(2,1)S(1)} async-done(((bf16[2,128,4096]{1,0,2:T(2,128)(2,1)}), bf16[2,128,4096]{1,0,2:T(2,128)(2,1)S(1)}, u32[]{:S(2)}, u32[]{:S(2)}) %all-to-all-start.1) | async-done | bytes 2097184 | tf_op jit(solution)/shard_map/all_to_all | solution.py:88
  56.1 1.3 copy-done.4
  57.4 4.7 %copy.108 = bf16[2,128,16,256]{3,1,2,0:T(8,128)(2,1)S(1)} copy(bf16[2,128,16,256]{1,0,3,2:T(2,128)(2,1)} %bitcast.94) | data formatting | bytes 4194304 | tf_op jit(solution)/shard_map/all_to_all | solution.py:88
  62.2 3.9 %fusion.5 = f32[2,2048,256]{2,1,0:T(8,128)S(1)} fusion(bf16[2,2048,256]{2,1,0:T(8,128)(2,1)S(1)} %bitcast.87, f32[2,256]{1,0:T(2,128)S(1)} %get-tuple-element.53, f32[2,256]{1,0:T(2,128)S(1)} %get-tuple-element.54, f32[2,256]{1,0:T(2,128)S(1)} %get-tuple-element.49, f32[2,256]{1,0:T(2,128)S(1)} %get-tuple-element.50, f32[2,256]{1,0:T(2,128)S(1)} %get-tuple-element.51, ...), kind=kLoop, calls=%fused_computation.18 | loop fusion | flops 20971520 | bytes 6305792 | tf_op jit(solution)/shard_map/add | solution.py:13
  67.0 12.2 %convolution_select_fusion.3 = f32[8,272,128]{2,0,1:T(8,128)S(1)} fusion(bf16[1,7,127,128]{3,1,2,0:T(8,128)(2,1)S(1)} %slice.168, bf16[1,8,272,128]{3,1,2,0:T(8,128)(2,1)S(1)} %copy.110, pred[8,272]{0,1:T(8,128)(4,1)S(1)} %copy-done.9, bf16[128,1,128]{2,0,1:T(8,128)(2,1)S(1)} %bitcast.104), kind=kOutput, calls=%fused_computation.61 | convolution fusion | flops 74033152 | bytes 1933696 | tf_op jit(solution)/shard_map/conv_general_dilated | solution.py:55
  79.8 12.0 %convolution_select_fusion.2 = f32[8,272,128]{2,0,1:T(8,128)S(1)} fusion(bf16[1,7,127,128]{3,1,2,0:T(8,128)(2,1)S(1)} %slice.170, bf16[1,8,272,128]{3,1,2,0:T(8,128)(2,1)S(1)} %copy.114, pred[8,272]{0,1:T(8,128)(4,1)S(1)} %copy-done.9, bf16[128,1,128]{2,0,1:T(8,128)(2,1)S(1)} %bitcast.103), kind=kOutput, calls=%fused_computation.60 | convolution fusion | flops 74033152 | bytes 1933696 | tf_op jit(solution)/shard_map/conv_general_dilated | solution.py:55
  94.4 13.8 %fusion.31 = f32[1,128,128]{2,0,1:T(1,128)S(1)} fusion(bf16[1,2175,128]{2,1,0:T(8,128)(2,1)S(1)} %get-tuple-element.42, bf16[2048,1,128]{2,0,1:T(8,128)(2,1)S(1)} %get-tuple-element.38), kind=kOutput, calls=%fused_computation.64 | convolution fusion | flops 67108864 | bytes 1146624 | tf_op jit(solution)/shard_map/conv_general_dilated | solution.py:55
  108.1 1.1 copy.124
  109.8 12.0 %convolution_select_fusion.1 = f32[8,272,128]{2,0,1:T(8,128)S(1)} fusion(bf16[1,7,127,128]{3,1,2,0:T(8,128)(2,1)S(1)} %slice.172, bf16[1,8,272,128]{3,1,2,0:T(8,128)(2,1)S(1)} %copy.118, pred[8,272]{0,1:T(8,128)(4,1)S(1)} %copy-done.9, bf16[128,1,128]{2,0,1:T(8,128)(2,1)S(1)} %get-tuple-element.44), kind=kOutput, calls=%fused_computation.59 | convolution fusion | flops 74033152 | bytes 1933696 | tf_op jit(solution)/shard_map/conv_general_dilated | solution.py:55
  121.8 12.0 %convolution_select_fusion = f32[8,272,128]{2,0,1:T(8,128)S(1)} fusion(bf16[1,7,127,128]{3,1,2,0:T(8,128)(2,1)S(1)} %slice.173, bf16[1,8,272,128]{3,1,2,0:T(8,128)(2,1)S(1)} %copy.121, pred[8,272]{0,1:T(8,128)(4,1)S(1)} %copy-done.9, bf16[128,1,128]{2,0,1:T(8,128)(2,1)S(1)} %get-tuple-element.45), kind=kOutput, calls=%fused_computation.58 | convolution fusion | flops 74033152 | bytes 1933696 | tf_op jit(solution)/shard_map/conv_general_dilated | solution.py:55
  134.7 0.9 multiply_convert_fusion.1
  137.0 3.7 %fusion.12 = bf16[2,2048,256]{2,1,0:T(8,128)(2,1)S(1)} fusion(bf16[2,2048,256]{2,1,0:T(8,128)(2,1)S(1)} %pad_maximum_fusion.2, f32[2,256]{1,0:T(2,128)S(1)} %get-tuple-element.53, f32[2,256]{1,0:T(2,128)S(1)} %get-tuple-element.54, f32[2,256]{1,0:T(2,128)S(1)} %get-tuple-element.49, f32[2,256]{1,0:T(2,128)S(1)} %get-tuple-element.50, ...), kind=kLoop, calls=%fused_computation.25 | loop fusion | flops 22020096 | bytes 4208640 | tf_op jit(solution)/shard_map/convert_element_type | solution.py:104
  140.6 14.0 %copy.125 = bf16[2,2048,256]{2,0,1:T(2,128)(2,1)} copy(bf16[2,2048,256]{2,1,0:T(8,128)(2,1)S(1)} %fusion.12) | data formatting | bytes 4194304 | tf_op jit(solution)/shard_map/convert_element_type | solution.py:104
  154.6 30.9 %all-to-all-start.2 = ((bf16[2,2048,256]{2,0,1:T(2,128)(2,1)}), bf16[2,2048,256]{2,0,1:T(2,128)(2,1)}, u32[]{:S(2)}, u32[]{:S(2)}) async-start(bf16[2,2048,256]{2,0,1:T(2,128)(2,1)} %copy.125), calls=%async_computation.2 | async-start | bytes 4194304 | tf_op jit(solution)/shard_map/all_to_all | solution.py:105
  185.5 12.1 %fusion.29 = f32[1,128,128]{2,0,1:T(1,128)S(1)} fusion(bf16[1,2175,128]{2,1,0:T(8,128)(2,1)} %copy-done.5, bf16[2048,1,128]{2,0,1:T(8,128)(2,1)} %get-tuple-element.39), kind=kOutput, calls=%fused_computation.62 | convolution fusion | flops 67108864 | bytes 1146624 | tf_op jit(solution)/shard_map/conv_general_dilated | solution.py:55
  197.8 4.7 %fusion.18 = (f32[2,256]{1,0:T(2,128)S(1)}, f32[2,256]{1,0:T(2,128)S(1)}, f32[2,256]{1,0:T(2,128)S(1)}, f32[2,256]{1,0:T(2,128)S(1)}, f32[2,256]{1,0:T(2,128)S(1)}, /*index=5*/f32[2,256]{1,0:T(2,128)S(1)}) fusion(bf16[2,2048,256]{2,1,0:T(8,128)(2,1)S(1)} %bitcast.88, bf16[1,2048,256]{2,1,0:T(8,128)(2,1)} %copy-done.2, ...), kind=kLoop, calls=%fused_computation.31 | loop fusion | flops 23065600 | bytes 4206592 | tf_op jit(solution)/shard_map/reduce_sum | solution.py:37
  203.3 6.3 %collective-permute-start = (f32[143,256]{1,0:T(8,128)S(1)}, f32[143,256]{1,0:T(8,128)S(1)}, u32[]{:S(2)}, u32[]{:S(2)}) collective-permute-start(f32[143,256]{1,0:T(8,128)S(1)} %pad_maximum_fusion.3), channel_id=1, source_target_pairs={{0,16},{16,0},{32,48},{48,32},{64,80},{80,64},{96,112},{112,96},{1... | collective-permute-start | bytes 439304 | tf_op jit(solution)/shard_map/ppermute | solution.py:71
  209.7 32.0 %collective-permute-done = f32[143,256]{1,0:T(8,128)S(1)} collective-permute-done((f32[143,256]{1,0:T(8,128)S(1)}, f32[143,256]{1,0:T(8,128)S(1)}, u32[]{:S(2)}, u32[]{:S(2)}) %collective-permute-start) | collective-permute-done | bytes 146464 | tf_op jit(solution)/shard_map/ppermute | solution.py:71
  241.7 1.9 collective-permute-start.1
  243.6 8.3 %collective-permute-done.1 = f32[143,256]{1,0:T(8,128)S(1)} collective-permute-done((f32[143,256]{1,0:T(8,128)S(1)}, f32[143,256]{1,0:T(8,128)S(1)}, u32[]{:S(2)}, u32[]{:S(2)}) %collective-permute-start.1) | collective-permute-done | bytes 146464 | tf_op jit(solution)/shard_map/ppermute | solution.py:71
  252.0 3.5 %collective-permute-start.2 = (f32[143,256]{1,0:T(8,128)S(1)}, f32[143,256]{1,0:T(8,128)S(1)}, u32[]{:S(2)}, u32[]{:S(2)}) collective-permute-start(f32[143,256]{1,0:T(8,128)S(1)} %add.87), channel_id=1, source_target_pairs={{0,64},{16,80},{32,96},{48,112},{64,0},{80,16},{96,32},{112,48},{1... | collective-permute-start | bytes 439304 | tf_op jit(solution)/shard_map/ppermute | solution.py:71
  255.5 4.2 %collective-permute-done.2 = f32[143,256]{1,0:T(8,128)S(1)} collective-permute-done((f32[143,256]{1,0:T(8,128)S(1)}, f32[143,256]{1,0:T(8,128)S(1)}, u32[]{:S(2)}, u32[]{:S(2)}) %collective-permute-start.2) | collective-permute-done | bytes 146464 | tf_op jit(solution)/shard_map/ppermute | solution.py:71
  259.6 4.5 %collective-permute-start.3 = (f32[143,256]{1,0:T(8,128)S(1)}, f32[143,256]{1,0:T(8,128)S(1)}, u32[]{:S(2)}, u32[]{:S(2)}) collective-permute-start(f32[143,256]{1,0:T(8,128)S(1)} %add.88), channel_id=1, source_target_pairs={{0,128},{16,144},{32,160},{48,176},{64,192},{80,208},{96,224},{112... | collective-permute-start | bytes 439304 | tf_op jit(solution)/shard_map/ppermute | solution.py:71
  264.2 6.4 %collective-permute-done.3 = f32[143,256]{1,0:T(8,128)S(1)} collective-permute-done((f32[143,256]{1,0:T(8,128)S(1)}, f32[143,256]{1,0:T(8,128)S(1)}, u32[]{:S(2)}, u32[]{:S(2)}) %collective-permute-start.3) | collective-permute-done | bytes 146464 | tf_op jit(solution)/shard_map/ppermute | solution.py:71
  270.5 7.7 %collective-permute-start.4 = (f32[143,256]{1,0:T(8,128)S(1)}, f32[143,256]{1,0:T(8,128)S(1)}, u32[]{:S(2)}, u32[]{:S(2)}) collective-permute-start(f32[143,256]{1,0:T(8,128)S(1)} %add.89), channel_id=1, source_target_pairs={{0,256},{16,272},{32,288},{48,304},{64,320},{80,336},{96,352},{112... | collective-permute-start | bytes 439304 | tf_op jit(solution)/shard_map/ppermute | solution.py:71
  278.3 6.8 %collective-permute-done.4 = f32[143,256]{1,0:T(8,128)S(1)} collective-permute-done((f32[143,256]{1,0:T(8,128)S(1)}, f32[143,256]{1,0:T(8,128)S(1)}, u32[]{:S(2)}, u32[]{:S(2)}) %collective-permute-start.4) | collective-permute-done | bytes 146464 | tf_op jit(solution)/shard_map/ppermute | solution.py:71
  287.0 2.8 copy.126
  289.8 2.3 broadcast_in_dim.66
  (75 shorter events, 10.9 us)
Async XLA Ops:
  1.9 21.8 %all-to-all-start = ((bf16[1,128,16]{1,0,2:T(2,128)(2,1)}), bf16[1,128,16]{1,0,2:T(2,128)(2,1)S(1)}, u32[]{:S(2)}, u32[]{:S(2)}) async-start(bf16[1,128,16]{1,0,2:T(2,128)(2,1)} %broadcast_in_dim.57), calls=%async_computation | async-start | bytes 16384 | tf_op jit(solution)/shard_map/all_to_all | solution.py:89
  23.7 7.4 %copy-start.6 = (bf16[128,256]{1,0:T(8,128)(2,1)S(1)}, bf16[128,256]{1,0:T(8,128)(2,1)}, u32[]{:S(2)}) copy-start(bf16[128,256]{1,0:T(8,128)(2,1)} %param.8) | copy-start | bytes 196612
  23.7 7.5 %copy-start.7 = (f32[2,7,256]{2,0,1:T(2,128)S(1)}, f32[2,7,256]{2,0,1:T(2,128)}, u32[]{:S(2)}) copy-start(f32[2,7,256]{2,0,1:T(2,128)} %param.7) | copy-start | bytes 43012
  23.7 32.4 %all-to-all-start.1 = ((bf16[2,128,4096]{1,0,2:T(2,128)(2,1)}), bf16[2,128,4096]{1,0,2:T(2,128)(2,1)S(1)}, u32[]{:S(2)}, u32[]{:S(2)}) async-start(bf16[2,128,4096]{1,0,2:T(2,128)(2,1)} %bitcast.5), calls=%async_computation.1 | async-start | bytes 4194304 | tf_op jit(solution)/shard_map/all_to_all | solution.py:88
  56.1 1.3 copy-start.4
  62.1 3.9 %copy-start = (bf16[2,128,16,256]{3,1,2,0:T(8,128)(2,1)}, bf16[2,128,16,256]{3,1,2,0:T(8,128)(2,1)S(1)}, u32[]{:S(2)}) copy-start(bf16[2,128,16,256]{3,1,2,0:T(8,128)(2,1)S(1)} %copy.108) | copy-start | bytes 6291460
  66.3 0.8 copy-start.9
  66.6 12.9 %copy-start.5 = (bf16[1,2175,128]{2,1,0:T(8,128)(2,1)}, bf16[1,2175,128]{2,1,0:T(8,128)(2,1)S(1)}, u32[]{:S(2)}) copy-start(bf16[1,2175,128]{2,1,0:T(8,128)(2,1)S(1)} %get-tuple-element.43) | copy-start | bytes 1670404
  92.1 0.7 copy-start.8
  136.0 1.0 copy-start.2
  154.6 132.4 %all-to-all-start.2 = ((bf16[2,2048,256]{2,0,1:T(2,128)(2,1)}), bf16[2,2048,256]{2,0,1:T(2,128)(2,1)}, u32[]{:S(2)}, u32[]{:S(2)}) async-start(bf16[2,2048,256]{2,0,1:T(2,128)(2,1)} %copy.125), calls=%async_computation.2 | async-start | bytes 4194304 | tf_op jit(solution)/shard_map/all_to_all | solution.py:105
  185.5 12.2 %copy-start.1 = (bf16[2,128,16,256]{3,1,2,0:T(8,128)(2,1)S(1)}, bf16[2,128,16,256]{3,1,2,0:T(8,128)(2,1)}, u32[]{:S(2)}) copy-start(bf16[2,128,16,256]{3,1,2,0:T(8,128)(2,1)} %copy-done) | copy-start | bytes 6291460
  197.8 4.8 %copy-start.3 = (bf16[1,2048,256]{2,1,0:T(8,128)(2,1)S(1)}, bf16[1,2048,256]{2,1,0:T(8,128)(2,1)}, u32[]{:S(2)}) copy-start(bf16[1,2048,256]{2,1,0:T(8,128)(2,1)} %copy-done.2) | copy-start | bytes 3145732
  203.3 38.4 %collective-permute-start = (f32[143,256]{1,0:T(8,128)S(1)}, f32[143,256]{1,0:T(8,128)S(1)}, u32[]{:S(2)}, u32[]{:S(2)}) collective-permute-start(f32[143,256]{1,0:T(8,128)S(1)} %pad_maximum_fusion.3), channel_id=1, source_target_pairs={{0,16},{16,0},{32,48},{48,32},{64,80},{80,64},{96,112},{112,96},{1... | collective-permute-start | bytes 439304 | tf_op jit(solution)/shard_map/ppermute | solution.py:71
  241.7 10.2 %collective-permute-start.1 = (f32[143,256]{1,0:T(8,128)S(1)}, f32[143,256]{1,0:T(8,128)S(1)}, u32[]{:S(2)}, u32[]{:S(2)}) collective-permute-start(f32[143,256]{1,0:T(8,128)S(1)} %fusion.87), channel_id=1, source_target_pairs={{0,32},{16,48},{32,0},{48,16},{64,96},{80,112},{96,64},{112,80},{1... | collective-permute-start | bytes 439304 | tf_op jit(solution)/shard_map/ppermute | solution.py:71
  252.0 7.7 %collective-permute-start.2 = (f32[143,256]{1,0:T(8,128)S(1)}, f32[143,256]{1,0:T(8,128)S(1)}, u32[]{:S(2)}, u32[]{:S(2)}) collective-permute-start(f32[143,256]{1,0:T(8,128)S(1)} %add.87), channel_id=1, source_target_pairs={{0,64},{16,80},{32,96},{48,112},{64,0},{80,16},{96,32},{112,48},{1... | collective-permute-start | bytes 439304 | tf_op jit(solution)/shard_map/ppermute | solution.py:71
  259.6 10.9 %collective-permute-start.3 = (f32[143,256]{1,0:T(8,128)S(1)}, f32[143,256]{1,0:T(8,128)S(1)}, u32[]{:S(2)}, u32[]{:S(2)}) collective-permute-start(f32[143,256]{1,0:T(8,128)S(1)} %add.88), channel_id=1, source_target_pairs={{0,128},{16,144},{32,160},{48,176},{64,192},{80,208},{96,224},{112... | collective-permute-start | bytes 439304 | tf_op jit(solution)/shard_map/ppermute | solution.py:71
  270.5 14.6 %collective-permute-start.4 = (f32[143,256]{1,0:T(8,128)S(1)}, f32[143,256]{1,0:T(8,128)S(1)}, u32[]{:S(2)}, u32[]{:S(2)}) collective-permute-start(f32[143,256]{1,0:T(8,128)S(1)} %add.89), channel_id=1, source_target_pairs={{0,256},{16,272},{32,288},{48,304},{64,320},{80,336},{96,352},{112... | collective-permute-start | bytes 439304 | tf_op jit(solution)/shard_map/ppermute | solution.py:71

commit v7 on v6

--- a/solution.py
+++ b/solution.py
@@ -102,7 +102,6 @@
     grad_filtered = jnp.stack([grad_key, grad_value])
     padded_grads = jnp.pad(grad_filtered, ((0, 0), (0, short_len - 1), (0, 0)))
     grad_channels = short_backward(padded_grads, short_filters).astype(jnp.bfloat16)
-    grad_inputs = lax.all_to_all(grad_channels, "ctx", split_axis=1, concat_axis=2, tiled=True)
     grad_taps = depthwise(padded_product, grad_mix)[::-1]
     grad_gain = jnp.sum(grad_mix.astype(jnp.float32) * product.astype(jnp.float32), axis=0)
     grad_short = short_weights(grad_filtered, padded_inputs)
@@ -111,6 +110,8 @@
         [grad_taps, grad_short.reshape(-1, grad_short.shape[-1]), grad_gain[None]], axis=0
     ).astype(jnp.float32)
     stacked = butterfly_sum(stacked, "dp", groups)
+    stacked, grad_channels = lax.optimization_barrier((stacked, grad_channels))
+    grad_inputs = lax.all_to_all(grad_channels, "ctx", split_axis=1, concat_axis=2, tiled=True)
     grad_taps = stacked[:taps]
     grad_short = stacked[taps : taps + grad_short.shape[0] * short_len].reshape(grad_short.shape)
     grad_gain = stacked[-1]

time: 296 us -> 320 us (1.081)
  the two profiles are of different devices: /device:TPU:2 before, /device:TPU:6 now
where the time goes in v7:
time: 320 us; the launch traced here: 316 us
  waiting for transfers between devices  106 us (33%)
  matrix products  76.1 us (24%)
  starting transfers between devices  72.2 us (23%)
  local copies, waits for them, and re-layouts  43.2 us (14%)
  other arithmetic  16.7 us (5%)
    conv_general_dilated x6, matrix products, depthwise(): lax.conv_general_dilated(extended[None], kernel[:, None, :], (1,), 'VALID...  76.1 us
    all_to_all x1, waiting for transfers between devices, local(): lax.all_to_all(grad_channels, 'ctx', split_axis=1, concat_axis=2, tiled=T...  49 us
    ppermute x5, starting transfers between devices, butterfly_sum(): value = value + lax.ppermute(value, axis, perm)  46.4 us
    all_to_all x1, waiting for transfers between devices, local(): lax.all_to_all(inputs, 'ctx', split_axis=2, concat_axis=1, tiled=True)  31.3 us
    ppermute x5, waiting for transfers between devices, butterfly_sum(): value = value + lax.ppermute(value, axis, perm)  24.3 us
    optimization_barrier x1, local copies, waits for them, and re-layouts, local(): stacked, grad_channels = lax.optimization_barrier((stacked, grad_channels))  14 us
    all_to_all x1, starting transfers between devices, local(): lax.all_to_all(weight_rows, 'ctx', split_axis=2, concat_axis=1, tiled=True)  13.2 us
    unnamed x48, local copies, waits for them, and re-layouts  11.6 us
  transfers between devices with their start and end apart: 8, of which 8 were waited for; matrix products, arithmetic and copies ran while one was open for 4% of the time, Pallas kernels for 0%

profile of v7, /device:TPU:6, one launch (start us, length us, event | category | flops | bytes accessed | tf_op | source)
XLA Modules:
  0.0 316.1 jit_solution(15226360437673286729)
XLA Ops:
  1.9 13.2 %all-to-all-start.1 = ((bf16[1,128,16]{1,0,2:T(2,128)(2,1)}), bf16[1,128,16]{1,0,2:T(2,128)(2,1)S(1)}, u32[]{:S(2)}, u32[]{:S(2)}) async-start(bf16[1,128,16]{1,0,2:T(2,128)(2,1)} %broadcast_in_dim.58), calls=%async_computation.1 | async-start | bytes 16384 | tf_op jit(solution)/shard_map/all_to_all | solution.py:89
  15.1 6.2 %copy.129 = bf16[2,1,128,4096]{2,0,3,1:T(2,128)(2,1)} copy(bf16[2,1,128,4096]{3,2,1,0:T(8,128)(2,1)} %param.5) | data formatting | bytes 4194304 | tf_op args[0]
  21.3 1.8 all-to-all-done.1
  23.1 8.0 %all-to-all-start = ((bf16[2,128,4096]{1,0,2:T(2,128)(2,1)}), bf16[2,128,4096]{1,0,2:T(2,128)(2,1)S(1)}, u32[]{:S(2)}, u32[]{:S(2)}) async-start(bf16[2,128,4096]{1,0,2:T(2,128)(2,1)} %bitcast.1), calls=%async_computation | async-start | bytes 4194304 | tf_op jit(solution)/shard_map/all_to_all | solution.py:88
  31.3 31.3 %all-to-all-done = bf16[2,128,4096]{1,0,2:T(2,128)(2,1)S(1)} async-done(((bf16[2,128,4096]{1,0,2:T(2,128)(2,1)}), bf16[2,128,4096]{1,0,2:T(2,128)(2,1)S(1)}, u32[]{:S(2)}, u32[]{:S(2)}) %all-to-all-start) | async-done | bytes 2097184 | tf_op jit(solution)/shard_map/all_to_all | solution.py:88
  62.6 1.3 copy-done.4
  63.9 4.7 %copy.130 = bf16[2,128,16,256]{3,1,2,0:T(8,128)(2,1)S(1)} copy(bf16[2,128,16,256]{1,0,3,2:T(2,128)(2,1)} %bitcast.94) | data formatting | bytes 4194304 | tf_op jit(solution)/shard_map/all_to_all | solution.py:88
  68.7 4.2 %fusion.5 = f32[2,2048,256]{2,1,0:T(8,128)S(1)} fusion(bf16[2,2048,256]{2,1,0:T(8,128)(2,1)S(1)} %bitcast.87, f32[2,256]{1,0:T(2,128)S(1)} %get-tuple-element.61, f32[2,256]{1,0:T(2,128)S(1)} %get-tuple-element.62, f32[2,256]{1,0:T(2,128)S(1)} %get-tuple-element.57, f32[2,256]{1,0:T(2,128)S(1)} %get-tuple-element.58, f32[2,256]{1,0:T(2,128)S(1)} %get-tuple-element.59, ...), kind=kLoop, calls=%fused_computation.18 | loop fusion | flops 20971520 | bytes 6305792 | tf_op jit(solution)/shard_map/add | solution.py:13
  74.3 12.0 %convolution_select_fusion.2 = f32[8,272,128]{2,0,1:T(8,128)S(1)} fusion(bf16[1,7,127,128]{3,1,2,0:T(8,128)(2,1)S(1)} %slice.170, bf16[1,8,272,128]{3,1,2,0:T(8,128)(2,1)S(1)} %copy.137, pred[8,272]{0,1:T(8,128)(4,1)S(1)} %copy-done.22, bf16[128,1,128]{2,0,1:T(8,128)(2,1)S(1)} %bitcast.105), kind=kOutput, calls=%fused_computation.60 | convolution fusion | flops 74033152 | bytes 1933696 | tf_op jit(solution)/shard_map/conv_general_dilated | solution.py:55
  86.4 12.2 %convolution_select_fusion.3 = f32[8,272,128]{2,0,1:T(8,128)S(1)} fusion(bf16[1,7,127,128]{3,1,2,0:T(8,128)(2,1)S(1)} %slice.168, bf16[1,8,272,128]{3,1,2,0:T(8,128)(2,1)S(1)} %copy.133, pred[8,272]{0,1:T(8,128)(4,1)S(1)} %copy-done.22, bf16[128,1,128]{2,0,1:T(8,128)(2,1)S(1)} %bitcast.104), kind=kOutput, calls=%fused_computation.61 | convolution fusion | flops 74033152 | bytes 1933696 | tf_op jit(solution)/shard_map/conv_general_dilated | solution.py:55
  102.0 14.0 %fusion.29 = f32[1,128,128]{2,0,1:T(1,128)S(1)} fusion(bf16[1,2175,128]{2,1,0:T(8,128)(2,1)S(1)} %get-tuple-element.51, bf16[2048,1,128]{2,0,1:T(8,128)(2,1)S(1)} %get-tuple-element.47), kind=kOutput, calls=%fused_computation.62 | convolution fusion | flops 67108864 | bytes 1146624 | tf_op jit(solution)/shard_map/conv_general_dilated | solution.py:55
  116.0 14.2 %fusion.31 = f32[1,128,128]{2,0,1:T(1,128)S(1)} fusion(bf16[1,2175,128]{2,1,0:T(8,128)(2,1)S(1)} %get-tuple-element.50, bf16[2048,1,128]{2,0,1:T(8,128)(2,1)S(1)} %get-tuple-element.46), kind=kOutput, calls=%fused_computation.64 | convolution fusion | flops 67108864 | bytes 1146624 | tf_op jit(solution)/shard_map/conv_general_dilated | solution.py:55
  131.9 11.9 %convolution_select_fusion = f32[8,272,128]{2,0,1:T(8,128)S(1)} fusion(bf16[1,7,127,128]{3,1,2,0:T(8,128)(2,1)S(1)} %slice.175, bf16[1,8,272,128]{3,1,2,0:T(8,128)(2,1)S(1)} %copy.148, pred[8,272]{0,1:T(8,128)(4,1)S(1)} %copy-done.22, bf16[128,1,128]{2,0,1:T(8,128)(2,1)S(1)} %get-tuple-element.53), kind=kOutput, calls=%fused_computation.58 | convolution fusion | flops 74033152 | bytes 1933696 | tf_op jit(solution)/shard_map/conv_general_dilated | solution.py:55
  143.8 11.9 %convolution_select_fusion.1 = f32[8,272,128]{2,0,1:T(8,128)S(1)} fusion(bf16[1,7,127,128]{3,1,2,0:T(8,128)(2,1)S(1)} %slice.174, bf16[1,8,272,128]{3,1,2,0:T(8,128)(2,1)S(1)} %copy.145, pred[8,272]{0,1:T(8,128)(4,1)S(1)} %copy-done.22, bf16[128,1,128]{2,0,1:T(8,128)(2,1)S(1)} %get-tuple-element.52), kind=kOutput, calls=%fused_computation.59 | convolution fusion | flops 74033152 | bytes 1933696 | tf_op jit(solution)/shard_map/conv_general_dilated | solution.py:55
  156.6 1.5 copy-done.1
  160.4 3.6 %fusion.11 = (f32[2,256]{1,0:T(2,128)S(1)}, f32[2,256]{1,0:T(2,128)S(1)}, f32[2,256]{1,0:T(2,128)S(1)}, f32[2,256]{1,0:T(2,128)S(1)}, f32[2,256]{1,0:T(2,128)S(1)}, /*index=5*/f32[2,256]{1,0:T(2,128)S(1)}) fusion(bf16[2,2048,256]{2,1,0:T(8,128)(2,1)S(1)} %bitcast.88, bf16[1,2048,256]{2,1,0:T(8,128)(2,1)S(1)} %multiply_convert_fusion, ...), kind=kLoop, calls=%fused_computation.24 | loop fusion | flops 23065600 | bytes 4206592 | tf_op jit(solution)/shard_map/reduce_sum | solution.py:37
  164.8 22.8 %collective-permute-start = (f32[143,256]{1,0:T(8,128)S(1)}, f32[143,256]{1,0:T(8,128)S(1)}, u32[]{:S(2)}, u32[]{:S(2)}) collective-permute-start(f32[143,256]{1,0:T(8,128)S(1)} %pad_maximum_fusion.3), channel_id=1, source_target_pairs={{0,16},{16,0},{32,48},{48,32},{64,80},{80,64},{96,112},{112,96},{1... | collective-permute-start | bytes 439304 | tf_op jit(solution)/shard_map/ppermute | solution.py:71
  187.6 4.7 %collective-permute-done = f32[143,256]{1,0:T(8,128)S(1)} collective-permute-done((f32[143,256]{1,0:T(8,128)S(1)}, f32[143,256]{1,0:T(8,128)S(1)}, u32[]{:S(2)}, u32[]{:S(2)}) %collective-permute-start) | collective-permute-done | bytes 146464 | tf_op jit(solution)/shard_map/ppermute | solution.py:71
  192.3 8.0 %collective-permute-start.1 = (f32[143,256]{1,0:T(8,128)S(1)}, f32[143,256]{1,0:T(8,128)S(1)}, u32[]{:S(2)}, u32[]{:S(2)}) collective-permute-start(f32[143,256]{1,0:T(8,128)S(1)} %fusion.87), channel_id=1, source_target_pairs={{0,32},{16,48},{32,0},{48,16},{64,96},{80,112},{96,64},{112,80},{1... | collective-permute-start | bytes 439304 | tf_op jit(solution)/shard_map/ppermute | solution.py:71
  200.2 6.2 %collective-permute-done.1 = f32[143,256]{1,0:T(8,128)S(1)} collective-permute-done((f32[143,256]{1,0:T(8,128)S(1)}, f32[143,256]{1,0:T(8,128)S(1)}, u32[]{:S(2)}, u32[]{:S(2)}) %collective-permute-start.1) | collective-permute-done | bytes 146464 | tf_op jit(solution)/shard_map/ppermute | solution.py:71
  206.5 3.5 %collective-permute-start.2 = (f32[143,256]{1,0:T(8,128)S(1)}, f32[143,256]{1,0:T(8,128)S(1)}, u32[]{:S(2)}, u32[]{:S(2)}) collective-permute-start(f32[143,256]{1,0:T(8,128)S(1)} %add.81), channel_id=1, source_target_pairs={{0,64},{16,80},{32,96},{48,112},{64,0},{80,16},{96,32},{112,48},{1... | collective-permute-start | bytes 439304 | tf_op jit(solution)/shard_map/ppermute | solution.py:71
  210.0 4.2 %collective-permute-done.2 = f32[143,256]{1,0:T(8,128)S(1)} collective-permute-done((f32[143,256]{1,0:T(8,128)S(1)}, f32[143,256]{1,0:T(8,128)S(1)}, u32[]{:S(2)}, u32[]{:S(2)}) %collective-permute-start.2) | collective-permute-done | bytes 146464 | tf_op jit(solution)/shard_map/ppermute | solution.py:71
  214.3 4.5 %collective-permute-start.3 = (f32[143,256]{1,0:T(8,128)S(1)}, f32[143,256]{1,0:T(8,128)S(1)}, u32[]{:S(2)}, u32[]{:S(2)}) collective-permute-start(f32[143,256]{1,0:T(8,128)S(1)} %add.82), channel_id=1, source_target_pairs={{0,128},{16,144},{32,160},{48,176},{64,192},{80,208},{96,224},{112... | collective-permute-start | bytes 439304 | tf_op jit(solution)/shard_map/ppermute | solution.py:71
  219.0 6.1 %collective-permute-done.3 = f32[143,256]{1,0:T(8,128)S(1)} collective-permute-done((f32[143,256]{1,0:T(8,128)S(1)}, f32[143,256]{1,0:T(8,128)S(1)}, u32[]{:S(2)}, u32[]{:S(2)}) %collective-permute-start.3) | collective-permute-done | bytes 146464 | tf_op jit(solution)/shard_map/ppermute | solution.py:71
  225.1 7.7 %collective-permute-start.4 = (f32[143,256]{1,0:T(8,128)S(1)}, f32[143,256]{1,0:T(8,128)S(1)}, u32[]{:S(2)}, u32[]{:S(2)}) collective-permute-start(f32[143,256]{1,0:T(8,128)S(1)} %add.83), channel_id=1, source_target_pairs={{0,256},{16,272},{32,288},{48,304},{64,320},{80,336},{96,352},{112... | collective-permute-start | bytes 439304 | tf_op jit(solution)/shard_map/ppermute | solution.py:71
  233.0 3.7 %fusion.18 = bf16[2,2048,256]{2,1,0:T(8,128)(2,1)S(1)} fusion(bf16[2,2048,256]{2,1,0:T(8,128)(2,1)S(1)} %pad_maximum_fusion.2, f32[2,256]{1,0:T(2,128)S(1)} %copy-done.17, f32[2,256]{1,0:T(2,128)S(1)} %copy-done.19, f32[2,256]{1,0:T(2,128)S(1)} %copy-done.9, f32[2,256]{1,0:T(2,128)S(1)} %copy-done.11, f32[2,256]{1,0:T(2,128)S(1)} %copy-done.13, ...), kind=kLoop, calls=%fused_computation.31 | loop fusion | flops 22020096 | bytes 4208640 | tf_op jit(solution)/shard_map/convert_element_type | solution.py:104
  236.7 3.1 collective-permute-done.4
  239.7 14.0 %copy.152 = bf16[2,2048,256]{2,0,1:T(2,128)(2,1)} copy(bf16[2,2048,256]{2,1,0:T(8,128)(2,1)S(1)} %fusion.18) | data formatting | bytes 4194304 | tf_op jit(solution)/shard_map/optimization_barrier | solution.py:113
  253.7 4.5 %all-to-all-start.2 = ((bf16[2,2048,256]{2,0,1:T(2,128)(2,1)}), bf16[2,2048,256]{2,0,1:T(2,128)(2,1)S(1)}, u32[]{:S(2)}, u32[]{:S(2)}) async-start(bf16[2,2048,256]{2,0,1:T(2,128)(2,1)} %copy.152), calls=%async_computation.2 | async-start | bytes 4194304 | tf_op jit(solution)/shard_map/all_to_all | solution.py:114
  260.1 49.0 %all-to-all-done.2 = bf16[2,2048,256]{2,0,1:T(2,128)(2,1)S(1)} async-done(((bf16[2,2048,256]{2,0,1:T(2,128)(2,1)}), bf16[2,2048,256]{2,0,1:T(2,128)(2,1)S(1)}, u32[]{:S(2)}, u32[]{:S(2)}) %all-to-all-start.2) | async-done | bytes 2097184 | tf_op jit(solution)/shard_map/all_to_all | solution.py:114
  309.2 2.5 copy.153
  311.7 4.2 %broadcast_in_dim.69 = bf16[2,1,128,4096]{3,2,1,0:T(8,128)(2,1)} reshape(bf16[2,128,16,256]{3,2,1,0:T(8,128)(2,1)} %copy.153) | data formatting | bytes 4194304 | tf_op jit(solution)/shard_map/broadcast_in_dim | solution.py:118
  (101 shorter events, 14.0 us)
Async XLA Ops:
  1.9 21.2 %all-to-all-start.1 = ((bf16[1,128,16]{1,0,2:T(2,128)(2,1)}), bf16[1,128,16]{1,0,2:T(2,128)(2,1)S(1)}, u32[]{:S(2)}, u32[]{:S(2)}) async-start(bf16[1,128,16]{1,0,2:T(2,128)(2,1)} %broadcast_in_dim.58), calls=%async_computation.1 | async-start | bytes 16384 | tf_op jit(solution)/shard_map/all_to_all | solution.py:89
  23.1 8.0 %copy-start.5 = (bf16[128,256]{1,0:T(8,128)(2,1)S(1)}, bf16[128,256]{1,0:T(8,128)(2,1)}, u32[]{:S(2)}) copy-start(bf16[128,256]{1,0:T(8,128)(2,1)} %param.8) | copy-start | bytes 196612
  23.1 8.1 %copy-start.20 = (f32[2,7,256]{2,0,1:T(2,128)S(1)}, f32[2,7,256]{2,0,1:T(2,128)}, u32[]{:S(2)}) copy-start(f32[2,7,256]{2,0,1:T(2,128)} %param.7) | copy-start | bytes 43012
  23.1 39.5 %all-to-all-start = ((bf16[2,128,4096]{1,0,2:T(2,128)(2,1)}), bf16[2,128,4096]{1,0,2:T(2,128)(2,1)S(1)}, u32[]{:S(2)}, u32[]{:S(2)}) async-start(bf16[2,128,4096]{1,0,2:T(2,128)(2,1)} %bitcast.1), calls=%async_computation | async-start | bytes 4194304 | tf_op jit(solution)/shard_map/all_to_all | solution.py:88
  31.2 37.4 %copy-start.6 = (f32[2,256]{1,0:T(2,128)}, f32[2,256]{1,0:T(2,128)S(1)}, u32[]{:S(2)}) copy-start(f32[2,256]{1,0:T(2,128)S(1)} %get-tuple-element.56) | copy-start | bytes 6148
  31.2 37.4 %copy-start.8 = (f32[2,256]{1,0:T(2,128)}, f32[2,256]{1,0:T(2,128)S(1)}, u32[]{:S(2)}) copy-start(f32[2,256]{1,0:T(2,128)S(1)} %get-tuple-element.57) | copy-start | bytes 6148
  31.2 37.4 %copy-start.10 = (f32[2,256]{1,0:T(2,128)}, f32[2,256]{1,0:T(2,128)S(1)}, u32[]{:S(2)}) copy-start(f32[2,256]{1,0:T(2,128)S(1)} %get-tuple-element.58) | copy-start | bytes 6148
  31.2 37.4 %copy-start.12 = (f32[2,256]{1,0:T(2,128)}, f32[2,256]{1,0:T(2,128)S(1)}, u32[]{:S(2)}) copy-start(f32[2,256]{1,0:T(2,128)S(1)} %get-tuple-element.59) | copy-start | bytes 6148
  31.2 37.4 %copy-start.14 = (f32[2,256]{1,0:T(2,128)}, f32[2,256]{1,0:T(2,128)S(1)}, u32[]{:S(2)}) copy-start(f32[2,256]{1,0:T(2,128)S(1)} %get-tuple-element.60) | copy-start | bytes 6148
  31.2 37.4 %copy-start.16 = (f32[2,256]{1,0:T(2,128)}, f32[2,256]{1,0:T(2,128)S(1)}, u32[]{:S(2)}) copy-start(f32[2,256]{1,0:T(2,128)S(1)} %get-tuple-element.61) | copy-start | bytes 6148
  31.3 37.4 %copy-start.18 = (f32[2,256]{1,0:T(2,128)}, f32[2,256]{1,0:T(2,128)S(1)}, u32[]{:S(2)}) copy-start(f32[2,256]{1,0:T(2,128)S(1)} %get-tuple-element.62) | copy-start | bytes 6148
  62.6 1.3 copy-start.4
  68.6 4.3 %copy-start.2 = (bf16[2,128,16,256]{3,1,2,0:T(8,128)(2,1)}, bf16[2,128,16,256]{3,1,2,0:T(8,128)(2,1)S(1)}, u32[]{:S(2)}) copy-start(bf16[2,128,16,256]{3,1,2,0:T(8,128)(2,1)S(1)} %copy.130) | copy-start | bytes 6291460
  72.9 26.3 %copy-start = (f32[2,2048,256]{2,1,0:T(8,128)}, f32[2,2048,256]{2,1,0:T(8,128)S(1)}, u32[]{:S(2)}) copy-start(f32[2,2048,256]{2,1,0:T(8,128)S(1)} %fusion.5) | copy-start | bytes 12582916
  73.5 0.8 copy-start.22
  99.0 0.7 copy-start.21
  155.8 2.2 copy-start.1
  158.8 1.6 copy-start.3
  164.8 27.4 %collective-permute-start = (f32[143,256]{1,0:T(8,128)S(1)}, f32[143,256]{1,0:T(8,128)S(1)}, u32[]{:S(2)}, u32[]{:S(2)}) collective-permute-start(f32[143,256]{1,0:T(8,128)S(1)} %pad_maximum_fusion.3), channel_id=1, source_target_pairs={{0,16},{16,0},{32,48},{48,32},{64,80},{80,64},{96,112},{112,96},{1... | collective-permute-start | bytes 439304 | tf_op jit(solution)/shard_map/ppermute | solution.py:71
  192.3 14.2 %collective-permute-start.1 = (f32[143,256]{1,0:T(8,128)S(1)}, f32[143,256]{1,0:T(8,128)S(1)}, u32[]{:S(2)}, u32[]{:S(2)}) collective-permute-start(f32[143,256]{1,0:T(8,128)S(1)} %fusion.87), channel_id=1, source_target_pairs={{0,32},{16,48},{32,0},{48,16},{64,96},{80,112},{96,64},{112,80},{1... | collective-permute-start | bytes 439304 | tf_op jit(solution)/shard_map/ppermute | solution.py:71
  206.5 7.7 %collective-permute-start.2 = (f32[143,256]{1,0:T(8,128)S(1)}, f32[143,256]{1,0:T(8,128)S(1)}, u32[]{:S(2)}, u32[]{:S(2)}) collective-permute-start(f32[143,256]{1,0:T(8,128)S(1)} %add.81), channel_id=1, source_target_pairs={{0,64},{16,80},{32,96},{48,112},{64,0},{80,16},{96,32},{112,48},{1... | collective-permute-start | bytes 439304 | tf_op jit(solution)/shard_map/ppermute | solution.py:71
  214.2 18.7 %copy-start.7 = (f32[2,256]{1,0:T(2,128)S(1)}, f32[2,256]{1,0:T(2,128)}, u32[]{:S(2)}) copy-start(f32[2,256]{1,0:T(2,128)} %copy-done.6) | copy-start | bytes 6148
  214.2 18.7 %copy-start.9 = (f32[2,256]{1,0:T(2,128)S(1)}, f32[2,256]{1,0:T(2,128)}, u32[]{:S(2)}) copy-start(f32[2,256]{1,0:T(2,128)} %copy-done.8) | copy-start | bytes 6148
  214.2 18.7 %copy-start.11 = (f32[2,256]{1,0:T(2,128)S(1)}, f32[2,256]{1,0:T(2,128)}, u32[]{:S(2)}) copy-start(f32[2,256]{1,0:T(2,128)} %copy-done.10) | copy-start | bytes 6148
  214.2 18.7 %copy-start.13 = (f32[2,256]{1,0:T(2,128)S(1)}, f32[2,256]{1,0:T(2,128)}, u32[]{:S(2)}) copy-start(f32[2,256]{1,0:T(2,128)} %copy-done.12) | copy-start | bytes 6148
  214.2 18.7 %copy-start.15 = (f32[2,256]{1,0:T(2,128)S(1)}, f32[2,256]{1,0:T(2,128)}, u32[]{:S(2)}) copy-start(f32[2,256]{1,0:T(2,128)} %copy-done.14) | copy-start | bytes 6148
  214.2 18.7 %copy-start.17 = (f32[2,256]{1,0:T(2,128)S(1)}, f32[2,256]{1,0:T(2,128)}, u32[]{:S(2)}) copy-start(f32[2,256]{1,0:T(2,128)} %copy-done.16) | copy-start | bytes 6148
  214.2 18.7 %copy-start.19 = (f32[2,256]{1,0:T(2,128)S(1)}, f32[2,256]{1,0:T(2,128)}, u32[]{:S(2)}) copy-start(f32[2,256]{1,0:T(2,128)} %copy-done.18) | copy-start | bytes 6148
  214.3 10.9 %collective-permute-start.3 = (f32[143,256]{1,0:T(8,128)S(1)}, f32[143,256]{1,0:T(8,128)S(1)}, u32[]{:S(2)}, u32[]{:S(2)}) collective-permute-start(f32[143,256]{1,0:T(8,128)S(1)} %add.82), channel_id=1, source_target_pairs={{0,128},{16,144},{32,160},{48,176},{64,192},{80,208},{96,224},{112... | collective-permute-start | bytes 439304 | tf_op jit(solution)/shard_map/ppermute | solution.py:71
  225.1 14.6 %collective-permute-start.4 = (f32[143,256]{1,0:T(8,128)S(1)}, f32[143,256]{1,0:T(8,128)S(1)}, u32[]{:S(2)}, u32[]{:S(2)}) collective-permute-start(f32[143,256]{1,0:T(8,128)S(1)} %add.83), channel_id=1, source_target_pairs={{0,256},{16,272},{32,288},{48,304},{64,320},{80,336},{96,352},{112... | collective-permute-start | bytes 439304 | tf_op jit(solution)/shard_map/ppermute | solution.py:71
  253.7 55.4 %all-to-all-start.2 = ((bf16[2,2048,256]{2,0,1:T(2,128)(2,1)}), bf16[2,2048,256]{2,0,1:T(2,128)(2,1)S(1)}, u32[]{:S(2)}, u32[]{:S(2)}) async-start(bf16[2,2048,256]{2,0,1:T(2,128)(2,1)} %copy.152), calls=%async_computation.2 | async-start | bytes 4194304 | tf_op jit(solution)/shard_map/all_to_all | solution.py:114

commit v8 on v6

--- a/solution.py
+++ b/solution.py
@@ -68,7 +68,8 @@
     bit = 1
     while bit < size:
         perm = [(i, i ^ bit) for i in range(size)]
-        value = value + lax.ppermute(value, axis, perm)
+        value = value.astype(jnp.bfloat16)
+        value = value.astype(jnp.float32) + lax.ppermute(value, axis, perm).astype(jnp.float32)
         bit *= 2
     return value
 

time: 296 us -> 299 us (1.010)
  the two profiles are of different devices: /device:TPU:2 before, /device:TPU:34 now
where the time goes in v8:
time: 299 us; the launch traced here: 295 us
  waiting for transfers between devices  96.2 us (32%)
  matrix products  75.7 us (25%)
  starting transfers between devices  66.6 us (22%)
  local copies, waits for them, and re-layouts  37.1 us (12%)
  other arithmetic  18 us (6%)
    conv_general_dilated x6, matrix products, depthwise(): lax.conv_general_dilated(extended[None], kernel[:, None, :], (1,), 'VALID...  75.7 us
    ppermute x5, waiting for transfers between devices, butterfly_sum(): lax.ppermute(value, axis, perm).astype(jnp.float32)  69.1 us
    all_to_all x1, starting transfers between devices, local(): lax.all_to_all(grad_channels, 'ctx', split_axis=1, concat_axis=2, tiled=T...  30.5 us
    all_to_all x1, waiting for transfers between devices, local(): lax.all_to_all(inputs, 'ctx', split_axis=2, concat_axis=1, tiled=True)  24.8 us
    ppermute x5, starting transfers between devices, butterfly_sum(): lax.ppermute(value, axis, perm).astype(jnp.float32)  15.5 us
    convert_element_type x1, local copies, waits for them, and re-layouts, local(): short_backward(padded_grads, short_filters).astype(jnp.bfloat16)  14 us
    all_to_all x1, starting transfers between devices, local(): lax.all_to_all(weight_rows, 'ctx', split_axis=2, concat_axis=1, tiled=True)  13.3 us
    unnamed x48, local copies, waits for them, and re-layouts  8.95 us
  transfers between devices with their start and end apart: 8, of which 7 were waited for; matrix products, arithmetic and copies ran while one was open for 3% of the time, Pallas kernels for 0%

profile of v8, /device:TPU:34, one launch (start us, length us, event | category | flops | bytes accessed | tf_op | source)
XLA Modules:
  0.0 295.1 jit_solution(5738623925197356855)
XLA Ops:
  1.9 13.3 %all-to-all-start = ((bf16[1,128,16]{1,0,2:T(2,128)(2,1)}), bf16[1,128,16]{1,0,2:T(2,128)(2,1)S(1)}, u32[]{:S(2)}, u32[]{:S(2)}) async-start(bf16[1,128,16]{1,0,2:T(2,128)(2,1)} %broadcast_in_dim.58), calls=%async_computation | async-start | bytes 16384 | tf_op jit(solution)/shard_map/all_to_all | solution.py:90
  15.2 6.2 %copy.111 = bf16[2,1,128,4096]{2,0,3,1:T(2,128)(2,1)} copy(bf16[2,1,128,4096]{3,2,1,0:T(8,128)(2,1)} %param.5) | data formatting | bytes 4194304 | tf_op args[0]
  21.4 2.4 all-to-all-done
  23.7 7.4 %all-to-all-start.1 = ((bf16[2,128,4096]{1,0,2:T(2,128)(2,1)}), bf16[2,128,4096]{1,0,2:T(2,128)(2,1)S(1)}, u32[]{:S(2)}, u32[]{:S(2)}) async-start(bf16[2,128,4096]{1,0,2:T(2,128)(2,1)} %bitcast.5), calls=%async_computation.1 | async-start | bytes 4194304 | tf_op jit(solution)/shard_map/all_to_all | solution.py:89
  31.3 24.8 %all-to-all-done.1 = bf16[2,128,4096]{1,0,2:T(2,128)(2,1)S(1)} async-done(((bf16[2,128,4096]{1,0,2:T(2,128)(2,1)}), bf16[2,128,4096]{1,0,2:T(2,128)(2,1)S(1)}, u32[]{:S(2)}, u32[]{:S(2)}) %all-to-all-start.1) | async-done | bytes 2097184 | tf_op jit(solution)/shard_map/all_to_all | solution.py:89
  56.1 1.3 copy-done.1
  57.4 4.7 %copy.112 = bf16[2,128,16,256]{3,1,2,0:T(8,128)(2,1)S(1)} copy(bf16[2,128,16,256]{1,0,3,2:T(2,128)(2,1)} %bitcast.107) | data formatting | bytes 4194304 | tf_op jit(solution)/shard_map/all_to_all | solution.py:89
  62.2 4.0 %fusion.5 = f32[2,2048,256]{2,1,0:T(8,128)S(1)} fusion(bf16[2,2048,256]{2,1,0:T(8,128)(2,1)S(1)} %bitcast.100, f32[2,256]{1,0:T(2,128)S(1)} %get-tuple-element.53, f32[2,256]{1,0:T(2,128)S(1)} %get-tuple-element.54, f32[2,256]{1,0:T(2,128)S(1)} %get-tuple-element.49, f32[2,256]{1,0:T(2,128)S(1)} %get-tuple-element.50, f32[2,256]{1,0:T(2,128)S(1)} %get-tuple-element.51, ...), kind=kLoop, calls=%fused_computation.18 | loop fusion | flops 20971520 | bytes 6305792 | tf_op jit(solution)/shard_map/add | solution.py:13
  67.2 12.3 %convolution_select_fusion.3 = f32[8,272,128]{2,0,1:T(8,128)S(1)} fusion(bf16[1,7,127,128]{3,1,2,0:T(8,128)(2,1)S(1)} %slice.168, bf16[1,8,272,128]{3,1,2,0:T(8,128)(2,1)S(1)} %copy.114, pred[8,272]{0,1:T(8,128)(4,1)S(1)} %copy-done.19, bf16[128,1,128]{2,0,1:T(8,128)(2,1)S(1)} %bitcast.117), kind=kOutput, calls=%fused_computation.61 | convolution fusion | flops 74033152 | bytes 1933696 | tf_op jit(solution)/shard_map/conv_general_dilated | solution.py:55
  80.0 11.9 %convolution_select_fusion.2 = f32[8,272,128]{2,0,1:T(8,128)S(1)} fusion(bf16[1,7,127,128]{3,1,2,0:T(8,128)(2,1)S(1)} %slice.170, bf16[1,8,272,128]{3,1,2,0:T(8,128)(2,1)S(1)} %copy.118, pred[8,272]{0,1:T(8,128)(4,1)S(1)} %copy-done.19, bf16[128,1,128]{2,0,1:T(8,128)(2,1)S(1)} %bitcast.116), kind=kOutput, calls=%fused_computation.60 | convolution fusion | flops 74033152 | bytes 1933696 | tf_op jit(solution)/shard_map/conv_general_dilated | solution.py:55
  95.1 12.2 %convolution_select_fusion.1 = f32[8,272,128]{2,0,1:T(8,128)S(1)} fusion(bf16[1,7,127,128]{3,1,2,0:T(8,128)(2,1)S(1)} %slice.172, bf16[1,8,272,128]{3,1,2,0:T(8,128)(2,1)S(1)} %copy.122, pred[8,272]{0,1:T(8,128)(4,1)S(1)} %copy-done.19, bf16[128,1,128]{2,0,1:T(8,128)(2,1)S(1)} %get-tuple-element.44), kind=kOutput, calls=%fused_computation.59 | convolution fusion | flops 74033152 | bytes 1933696 | tf_op jit(solution)/shard_map/conv_general_dilated | solution.py:55
  107.3 11.9 %convolution_select_fusion = f32[8,272,128]{2,0,1:T(8,128)S(1)} fusion(bf16[1,7,127,128]{3,1,2,0:T(8,128)(2,1)S(1)} %slice.173, bf16[1,8,272,128]{3,1,2,0:T(8,128)(2,1)S(1)} %copy.125, pred[8,272]{0,1:T(8,128)(4,1)S(1)} %copy-done.19, bf16[128,1,128]{2,0,1:T(8,128)(2,1)S(1)} %get-tuple-element.45), kind=kOutput, calls=%fused_computation.58 | convolution fusion | flops 74033152 | bytes 1933696 | tf_op jit(solution)/shard_map/conv_general_dilated | solution.py:55
  120.1 0.9 multiply_convert_fusion.1
  121.4 3.6 %fusion.18 = (bf16[2,256]{1,0:T(2,128)(2,1)S(1)}, bf16[2,256]{1,0:T(2,128)(2,1)S(1)}, bf16[2,256]{1,0:T(2,128)(2,1)S(1)}, bf16[2,256]{1,0:T(2,128)(2,1)S(1)}, bf...) fusion(bf16[2,2048,256]{2,1,0:T(8,128)(2,1)S(1)} %bitcast.101, bf16[1,2048,256]{2,1,0:T(8,128)(2,1)S(1)} %multiply_convert_fusion, ...), kind=kLoop, calls=%fused_computation.31 | loop fusion | flops 23065600 | bytes 4200448 | tf_op jit(solution)/shard_map/reduce_sum | solution.py:37
  125.2 13.5 %fusion.31 = f32[1,128,128]{2,0,1:T(1,128)S(1)} fusion(bf16[1,2175,128]{2,1,0:T(8,128)(2,1)S(1)} %get-tuple-element.42, bf16[2048,1,128]{2,0,1:T(8,128)(2,1)S(1)} %get-tuple-element.38), kind=kOutput, calls=%fused_computation.64 | convolution fusion | flops 67108864 | bytes 1146624 | tf_op jit(solution)/shard_map/conv_general_dilated | solution.py:55
  138.8 13.9 %fusion.29 = f32[1,128,128]{2,0,1:T(1,128)S(1)} fusion(bf16[1,2175,128]{2,1,0:T(8,128)(2,1)S(1)} %get-tuple-element.43, bf16[2048,1,128]{2,0,1:T(8,128)(2,1)S(1)} %get-tuple-element.39), kind=kOutput, calls=%fused_computation.62 | convolution fusion | flops 67108864 | bytes 1146624 | tf_op jit(solution)/shard_map/conv_general_dilated | solution.py:55
  152.8 3.9 %fusion.12 = bf16[2,2048,256]{2,1,0:T(8,128)(2,1)S(1)} fusion(bf16[2,2048,256]{2,1,0:T(8,128)(2,1)S(1)} %pad_maximum_fusion.2, f32[2,256]{1,0:T(2,128)S(1)} %copy-done.14, f32[2,256]{1,0:T(2,128)S(1)} %copy-done.16, f32[2,256]{1,0:T(2,128)S(1)} %copy-done.6, f32[2,256]{1,0:T(2,128)S(1)} %copy-done.8, f32[2,256]{1,0:T(2,128)S(1)} %copy-done.10, ...), kind=kLoop, calls=%fused_computation.25 | loop fusion | flops 22020096 | bytes 4208640 | tf_op jit(solution)/shard_map/convert_element_type | solution.py:105
  156.7 14.0 %copy.129 = bf16[2,2048,256]{2,0,1:T(2,128)(2,1)} copy(bf16[2,2048,256]{2,1,0:T(8,128)(2,1)S(1)} %fusion.12) | data formatting | bytes 4194304 | tf_op jit(solution)/shard_map/convert_element_type | solution.py:105
  170.7 30.5 %all-to-all-start.2 = ((bf16[2,2048,256]{2,0,1:T(2,128)(2,1)}), bf16[2,2048,256]{2,0,1:T(2,128)(2,1)}, u32[]{:S(2)}, u32[]{:S(2)}) async-start(bf16[2,2048,256]{2,0,1:T(2,128)(2,1)} %copy.129), calls=%async_computation.2 | async-start | bytes 4194304 | tf_op jit(solution)/shard_map/all_to_all | solution.py:106
  201.1 1.8 multiply_reduce_fusion
  203.2 6.3 %collective-permute-start = (bf16[143,256]{1,0:T(8,128)(2,1)S(1)}, bf16[143,256]{1,0:T(8,128)(2,1)S(1)}, u32[]{:S(2)}, u32[]{:S(2)}) collective-permute-start(bf16[143,256]{1,0:T(8,128)(2,1)S(1)} %pad_maximum_fusion.4), channel_id=1, source_target_pairs={{0,16},{16,0},{32,48},{48,32},{64,80},{80,64},{96,112},{112,96},{1... | collective-permute-start | bytes 219656 | tf_op jit(solution)/shard_map/ppermute | solution.py:72
  209.6 46.3 %collective-permute-done = bf16[143,256]{1,0:T(8,128)(2,1)S(1)} collective-permute-done((bf16[143,256]{1,0:T(8,128)(2,1)S(1)}, bf16[143,256]{1,0:T(8,128)(2,1)S(1)}, u32[]{:S(2)}, u32[]{:S(2)}) %collective-permute-start) | collective-permute-done | bytes 73248 | tf_op jit(solution)/shard_map/ppermute | solution.py:72
  255.9 1.9 collective-permute-start.1
  257.8 5.4 %collective-permute-done.1 = bf16[143,256]{1,0:T(8,128)(2,1)S(1)} collective-permute-done((bf16[143,256]{1,0:T(8,128)(2,1)S(1)}, bf16[143,256]{1,0:T(8,128)(2,1)S(1)}, u32[]{:S(2)}, u32[]{:S(2)}) %collective-permute-start.1) | collective-permute-done | bytes 73248 | tf_op jit(solution)/shard_map/ppermute | solution.py:72
  263.2 2.6 collective-permute-start.2
  265.8 3.7 %collective-permute-done.2 = bf16[143,256]{1,0:T(8,128)(2,1)S(1)} collective-permute-done((bf16[143,256]{1,0:T(8,128)(2,1)S(1)}, bf16[143,256]{1,0:T(8,128)(2,1)S(1)}, u32[]{:S(2)}, u32[]{:S(2)}) %collective-permute-start.2) | collective-permute-done | bytes 73248 | tf_op jit(solution)/shard_map/ppermute | solution.py:72
  269.5 2.7 collective-permute-start.3
  272.2 5.2 %collective-permute-done.3 = bf16[143,256]{1,0:T(8,128)(2,1)S(1)} collective-permute-done((bf16[143,256]{1,0:T(8,128)(2,1)S(1)}, bf16[143,256]{1,0:T(8,128)(2,1)S(1)}, u32[]{:S(2)}, u32[]{:S(2)}) %collective-permute-start.3) | collective-permute-done | bytes 73248 | tf_op jit(solution)/shard_map/ppermute | solution.py:72
  277.5 1.9 collective-permute-start.4
  279.4 8.5 %collective-permute-done.4 = bf16[143,256]{1,0:T(8,128)(2,1)S(1)} collective-permute-done((bf16[143,256]{1,0:T(8,128)(2,1)S(1)}, bf16[143,256]{1,0:T(8,128)(2,1)S(1)}, u32[]{:S(2)}, u32[]{:S(2)}) %collective-permute-start.4) | collective-permute-done | bytes 73248 | tf_op jit(solution)/shard_map/ppermute | solution.py:72
  289.8 2.8 copy.130
  292.6 2.3 broadcast_in_dim.67
  (96 shorter events, 9.5 us)
Async XLA Ops:
  1.9 21.8 %all-to-all-start = ((bf16[1,128,16]{1,0,2:T(2,128)(2,1)}), bf16[1,128,16]{1,0,2:T(2,128)(2,1)S(1)}, u32[]{:S(2)}, u32[]{:S(2)}) async-start(bf16[1,128,16]{1,0,2:T(2,128)(2,1)} %broadcast_in_dim.58), calls=%async_computation | async-start | bytes 16384 | tf_op jit(solution)/shard_map/all_to_all | solution.py:90
  23.7 7.4 %copy-start.2 = (bf16[128,256]{1,0:T(8,128)(2,1)S(1)}, bf16[128,256]{1,0:T(8,128)(2,1)}, u32[]{:S(2)}) copy-start(bf16[128,256]{1,0:T(8,128)(2,1)} %param.8) | copy-start | bytes 196612
  23.7 7.5 %copy-start.17 = (f32[2,7,256]{2,0,1:T(2,128)S(1)}, f32[2,7,256]{2,0,1:T(2,128)}, u32[]{:S(2)}) copy-start(f32[2,7,256]{2,0,1:T(2,128)} %param.7) | copy-start | bytes 43012
  23.7 32.4 %all-to-all-start.1 = ((bf16[2,128,4096]{1,0,2:T(2,128)(2,1)}), bf16[2,128,4096]{1,0,2:T(2,128)(2,1)S(1)}, u32[]{:S(2)}, u32[]{:S(2)}) async-start(bf16[2,128,4096]{1,0,2:T(2,128)(2,1)} %bitcast.5), calls=%async_computation.1 | async-start | bytes 4194304 | tf_op jit(solution)/shard_map/all_to_all | solution.py:89
  31.2 30.9 %copy-start.3 = (f32[2,256]{1,0:T(2,128)}, f32[2,256]{1,0:T(2,128)S(1)}, u32[]{:S(2)}) copy-start(f32[2,256]{1,0:T(2,128)S(1)} %get-tuple-element.48) | copy-start | bytes 6148
  31.3 30.9 %copy-start.5 = (f32[2,256]{1,0:T(2,128)}, f32[2,256]{1,0:T(2,128)S(1)}, u32[]{:S(2)}) copy-start(f32[2,256]{1,0:T(2,128)S(1)} %get-tuple-element.49) | copy-start | bytes 6148
  31.3 30.9 %copy-start.7 = (f32[2,256]{1,0:T(2,128)}, f32[2,256]{1,0:T(2,128)S(1)}, u32[]{:S(2)}) copy-start(f32[2,256]{1,0:T(2,128)S(1)} %get-tuple-element.50) | copy-start | bytes 6148
  31.3 30.9 %copy-start.9 = (f32[2,256]{1,0:T(2,128)}, f32[2,256]{1,0:T(2,128)S(1)}, u32[]{:S(2)}) copy-start(f32[2,256]{1,0:T(2,128)S(1)} %get-tuple-element.51) | copy-start | bytes 6148
  31.3 30.9 %copy-start.11 = (f32[2,256]{1,0:T(2,128)}, f32[2,256]{1,0:T(2,128)S(1)}, u32[]{:S(2)}) copy-start(f32[2,256]{1,0:T(2,128)S(1)} %get-tuple-element.52) | copy-start | bytes 6148
  31.3 30.9 %copy-start.13 = (f32[2,256]{1,0:T(2,128)}, f32[2,256]{1,0:T(2,128)S(1)}, u32[]{:S(2)}) copy-start(f32[2,256]{1,0:T(2,128)S(1)} %get-tuple-element.53) | copy-start | bytes 6148
  31.3 30.9 %copy-start.15 = (f32[2,256]{1,0:T(2,128)}, f32[2,256]{1,0:T(2,128)S(1)}, u32[]{:S(2)}) copy-start(f32[2,256]{1,0:T(2,128)S(1)} %get-tuple-element.54) | copy-start | bytes 6148
  56.1 1.3 copy-start.1
  66.4 0.8 copy-start.19
  92.3 0.7 copy-start.18
  121.4 3.7 %copy-start = (bf16[1,2048,256]{2,1,0:T(8,128)(2,1)}, bf16[1,2048,256]{2,1,0:T(8,128)(2,1)S(1)}, u32[]{:S(2)}) copy-start(bf16[1,2048,256]{2,1,0:T(8,128)(2,1)S(1)} %multiply_convert_fusion) | copy-start | bytes 3145732
  138.7 14.0 %copy-start.4 = (f32[2,256]{1,0:T(2,128)S(1)}, f32[2,256]{1,0:T(2,128)}, u32[]{:S(2)}) copy-start(f32[2,256]{1,0:T(2,128)} %copy-done.3) | copy-start | bytes 6148
  138.7 14.0 %copy-start.6 = (f32[2,256]{1,0:T(2,128)S(1)}, f32[2,256]{1,0:T(2,128)}, u32[]{:S(2)}) copy-start(f32[2,256]{1,0:T(2,128)} %copy-done.5) | copy-start | bytes 6148
  138.8 14.0 %copy-start.8 = (f32[2,256]{1,0:T(2,128)S(1)}, f32[2,256]{1,0:T(2,128)}, u32[]{:S(2)}) copy-start(f32[2,256]{1,0:T(2,128)} %copy-done.7) | copy-start | bytes 6148
  138.8 14.0 %copy-start.10 = (f32[2,256]{1,0:T(2,128)S(1)}, f32[2,256]{1,0:T(2,128)}, u32[]{:S(2)}) copy-start(f32[2,256]{1,0:T(2,128)} %copy-done.9) | copy-start | bytes 6148
  138.8 14.0 %copy-start.12 = (f32[2,256]{1,0:T(2,128)S(1)}, f32[2,256]{1,0:T(2,128)}, u32[]{:S(2)}) copy-start(f32[2,256]{1,0:T(2,128)} %copy-done.11) | copy-start | bytes 6148
  138.8 14.0 %copy-start.14 = (f32[2,256]{1,0:T(2,128)S(1)}, f32[2,256]{1,0:T(2,128)}, u32[]{:S(2)}) copy-start(f32[2,256]{1,0:T(2,128)} %copy-done.13) | copy-start | bytes 6148
  138.8 14.0 %copy-start.16 = (f32[2,256]{1,0:T(2,128)S(1)}, f32[2,256]{1,0:T(2,128)}, u32[]{:S(2)}) copy-start(f32[2,256]{1,0:T(2,128)} %copy-done.15) | copy-start | bytes 6148
  170.7 119.1 %all-to-all-start.2 = ((bf16[2,2048,256]{2,0,1:T(2,128)(2,1)}), bf16[2,2048,256]{2,0,1:T(2,128)(2,1)}, u32[]{:S(2)}, u32[]{:S(2)}) async-start(bf16[2,2048,256]{2,0,1:T(2,128)(2,1)} %copy.129), calls=%async_computation.2 | async-start | bytes 4194304 | tf_op jit(solution)/shard_map/all_to_all | solution.py:106
  203.2 52.7 %collective-permute-start = (bf16[143,256]{1,0:T(8,128)(2,1)S(1)}, bf16[143,256]{1,0:T(8,128)(2,1)S(1)}, u32[]{:S(2)}, u32[]{:S(2)}) collective-permute-start(bf16[143,256]{1,0:T(8,128)(2,1)S(1)} %pad_maximum_fusion.4), channel_id=1, source_target_pairs={{0,16},{16,0},{32,48},{48,32},{64,80},{80,64},{96,112},{112,96},{1... | collective-permute-start | bytes 219656 | tf_op jit(solution)/shard_map/ppermute | solution.py:72
  255.9 7.3 %collective-permute-start.1 = (bf16[143,256]{1,0:T(8,128)(2,1)S(1)}, bf16[143,256]{1,0:T(8,128)(2,1)S(1)}, u32[]{:S(2)}, u32[]{:S(2)}) collective-permute-start(bf16[143,256]{1,0:T(8,128)(2,1)S(1)} %add_convert_fusion.3), channel_id=1, source_target_pairs={{0,32},{16,48},{32,0},{48,16},{64,96},{80,112},{96,64},{112,80},{1... | collective-permute-start | bytes 219656 | tf_op jit(solution)/shard_map/ppermute | solution.py:72
  263.2 6.2 %collective-permute-start.2 = (bf16[143,256]{1,0:T(8,128)(2,1)S(1)}, bf16[143,256]{1,0:T(8,128)(2,1)S(1)}, u32[]{:S(2)}, u32[]{:S(2)}) collective-permute-start(bf16[143,256]{1,0:T(8,128)(2,1)S(1)} %add_convert_fusion.2), channel_id=1, source_target_pairs={{0,64},{16,80},{32,96},{48,112},{64,0},{80,16},{96,32},{112,48},{1... | collective-permute-start | bytes 219656 | tf_op jit(solution)/shard_map/ppermute | solution.py:72
  269.5 7.9 %collective-permute-start.3 = (bf16[143,256]{1,0:T(8,128)(2,1)S(1)}, bf16[143,256]{1,0:T(8,128)(2,1)S(1)}, u32[]{:S(2)}, u32[]{:S(2)}) collective-permute-start(bf16[143,256]{1,0:T(8,128)(2,1)S(1)} %add_convert_fusion.1), channel_id=1, source_target_pairs={{0,128},{16,144},{32,160},{48,176},{64,192},{80,208},{96,224},{112... | collective-permute-start | bytes 219656 | tf_op jit(solution)/shard_map/ppermute | solution.py:72
  277.5 10.4 %collective-permute-start.4 = (bf16[143,256]{1,0:T(8,128)(2,1)S(1)}, bf16[143,256]{1,0:T(8,128)(2,1)S(1)}, u32[]{:S(2)}, u32[]{:S(2)}) collective-permute-start(bf16[143,256]{1,0:T(8,128)(2,1)S(1)} %add_convert_fusion), channel_id=1, source_target_pairs={{0,256},{16,272},{32,288},{48,304},{64,320},{80,336},{96,352},{112... | collective-permute-start | bytes 219656 | tf_op jit(solution)/shard_map/ppermute | solution.py:72
